TPU v7x, 1024 devices: a whole 8x8x8 slice. The times are simulated.
1024 devices in a mesh: phase: 2 (over core), px: 8 (over y), py: 64 (over z, x).
Axes of the slice: x: 8, y: 8, z: 8, core: 2. Of those that a mesh axis runs over, the one named last changes fastest.
Arguments:
- node_latents: bfloat16 [2, 8, 64, 128, 256], P(None, 'px', 'py'), may hold values from -6 to 6
- edge_latents: bfloat16 [2, 8, 64, 5, 64, 256], P(None, 'px', 'py'), may hold values from -6 to 6
- tile_offsets: int32 [8, 64, 5], P('px', 'py'), may hold values from 0 to 8, as said below
- edge_dst: int32 [8, 64, 5, 64], P('px', 'py'), may hold values from 0 to 127
- edge_src: int32 [8, 64, 5, 64], P('px', 'py'), may hold values from 0 to 127
- edge_in_w: bfloat16 [2, 768, 256], P('phase'), may hold values from -0.21875 to 0.21875
- edge_out_w: bfloat16 [2, 256, 256], P('phase'), may hold values from -0.375 to 0.375
- node_in_w: bfloat16 [2, 512, 256], P('phase'), may hold values from -0.25 to 0.25
- node_out_w: bfloat16 [2, 256, 256], P('phase'), may hold values from -0.375 to 0.375
- node_cot: bfloat16 [2, 8, 64, 128, 256], P(None, 'px', 'py'), may hold values from -6 to 6
- edge_cot: bfloat16 [2, 8, 64, 5, 64, 256], P(None, 'px', 'py'), may hold values from -6 to 6
Outputs:
- node_out: bfloat16 [2, 2, 8, 64, 128, 256], P('phase', None, 'px', 'py')
- edge_out: bfloat16 [2, 2, 8, 64, 5, 64, 256], P('phase', None, 'px', 'py')
- node_grad: float32 [2, 2, 8, 64, 128, 256], P('phase', None, 'px', 'py')
- edge_grad: float32 [2, 2, 8, 64, 5, 64, 256], P('phase', None, 'px', 'py')
Inputs may be any that keep to these rules, and one draw needn't show every extreme that they name: `tile_offsets`: code c names the source block (a + c // 3 - 1, b + c % 3 - 1). Tile 0 of every destination block may take any code; tiles 1, 2, 3, 4 take codes from the finite set (0, 1, 2), the finite set (6, 7, 8), the finite set (0, 3, 6) and the finite set (2, 5, 8) respectively.
All inputs are finite; a program needn't handle non-finite values.
Results may differ from a plain program's by a relative error of at most 0.014.
Values may be sent and summed in bfloat16 or wider, within the bound.
No kernel may reach another device: no remote copies, remote signals or barrier semaphores. Data moves between devices by JAX's collectives and lax.ppermute only.
A program may use at most 32 MiB of HBM per device.

v0:
```python
import jax
import jax.numpy as jnp
from jax import lax
from jax.sharding import PartitionSpec as P


def padded(cells, sides, width):
    for axis, dim in sides:
        count = lax.axis_size(axis)
        ends = count - 1
        head = lax.slice_in_dim(cells, 0, width, axis=dim)
        tail = lax.slice_in_dim(cells, cells.shape[dim] - width, cells.shape[dim], axis=dim)
        cells = jnp.concatenate(
            [
                lax.ppermute(tail, axis, [(i, (i + 1) % count) for i in range(ends)]),
                cells,
                lax.ppermute(head, axis, [((i + 1) % count, i) for i in range(ends)]),
            ],
            axis=dim,
        )
    return cells


def from_behind(array, axis, by):
    count = lax.axis_size(axis)
    pairs = [(i, i + by) for i in range(count) if 0 <= i + by < count]
    return lax.ppermute(array, axis, pairs)


def normalize(values):
    centred = values - jnp.mean(values, axis=-1, keepdims=True)
    inverse = lax.rsqrt(jnp.mean(centred * centred, axis=-1, keepdims=True) + 1e-05)
    return (centred * inverse, inverse)


def norm_back(values, upstream):
    normed, inverse = normalize(values)
    return inverse * (
        upstream
        - jnp.mean(upstream, axis=-1, keepdims=True)
        - normed * jnp.mean(upstream * normed, axis=-1, keepdims=True)
    )


def silu_slope(values):
    squash = jax.nn.sigmoid(values)
    return squash * (1.0 + values * (1.0 - squash))


def times_plain(left, right):
    return jnp.dot(left, right, preferred_element_type=jnp.float32)


def times_turned(left, right):
    return lax.dot_general(
        left, right, (((1,), (1,)), ((), ())), preferred_element_type=jnp.float32
    )


def exact_sum(form, left, right):
    return jnp.einsum(
        form, left, right, precision=lax.Precision.HIGHEST, preferred_element_type=jnp.float32
    )


def forward(weights, tables, node_flat, edge_flat, source_table):
    edge_in, edge_outer, node_in, node_outer = weights
    dst_onehot, src_onehot, source_block, block_pick = tables
    blocks_y, tiles, edges_tile, block_nodes = dst_onehot.shape
    feature_width = node_flat.shape[1]
    node_blocks = node_flat.reshape(blocks_y, block_nodes, feature_width)
    at_dst = jnp.einsum(
        "ytkn,ynd->ytkd", dst_onehot, node_blocks, preferred_element_type=jnp.float32
    ).astype(jnp.bfloat16)
    src_blocks = jnp.take(source_table, source_block, axis=0)
    at_src = jnp.einsum(
        "ytkn,ytnd->ytkd", src_onehot, src_blocks, preferred_element_type=jnp.float32
    ).astype(jnp.bfloat16)
    at_dst = at_dst.reshape(-1, feature_width)
    at_src = at_src.reshape(-1, feature_width)
    act_edge = (
        times_plain(edge_flat, edge_in[:feature_width])
        + times_plain(at_dst, edge_in[feature_width : 2 * feature_width])
        + times_plain(at_src, edge_in[2 * feature_width :])
    )
    hidden_edge = jax.nn.silu(act_edge).astype(jnp.bfloat16)
    edge_pre = times_plain(hidden_edge, edge_outer)
    message = normalize(edge_pre)[0]
    edge_new = (edge_flat.astype(jnp.float32) + message).astype(jnp.bfloat16)
    summed = exact_sum(
        "ytkn,ytkd->ynd",
        dst_onehot.astype(jnp.float32),
        message.reshape(blocks_y, tiles, edges_tile, feature_width),
    )
    summed = summed.reshape(-1, feature_width).astype(jnp.bfloat16)
    act_node = times_plain(node_flat, node_in[:feature_width]) + times_plain(
        summed, node_in[feature_width:]
    )
    hidden_node = jax.nn.silu(act_node).astype(jnp.bfloat16)
    node_pre = times_plain(hidden_node, node_outer)
    node_new = (node_flat.astype(jnp.float32) + normalize(node_pre)[0]).astype(jnp.bfloat16)
    return (node_new, edge_new, (act_edge, edge_pre, act_node, node_pre))


def backward(weights, tables, kept_values, grad_node, grad_edge):
    edge_in, edge_outer, node_in, node_outer = weights
    dst_onehot, src_onehot, source_block, block_pick = tables
    blocks_y, tiles, edges_tile, block_nodes = dst_onehot.shape
    act_edge, edge_pre, act_node, node_pre = kept_values
    feature_width = grad_node.shape[1]
    dst_float = dst_onehot.astype(jnp.float32)
    src_float = src_onehot.astype(jnp.float32)
    pre_node_grad = norm_back(node_pre, grad_node).astype(jnp.bfloat16)
    act_node_grad = (times_turned(pre_node_grad, node_outer) * silu_slope(act_node)).astype(
        jnp.bfloat16
    )
    node_self_grad = times_turned(act_node_grad, node_in[:feature_width])
    summed_grad = times_turned(act_node_grad, node_in[feature_width:])
    summed_blocks = summed_grad.reshape(blocks_y, block_nodes, feature_width)
    message_grad = grad_edge + exact_sum("ytkn,ynd->ytkd", dst_float, summed_blocks).reshape(
        -1, feature_width
    )
    pre_edge_grad = norm_back(edge_pre, message_grad).astype(jnp.bfloat16)
    act_edge_grad = (times_turned(pre_edge_grad, edge_outer) * silu_slope(act_edge)).astype(
        jnp.bfloat16
    )
    edge_self_grad = times_turned(act_edge_grad, edge_in[:feature_width])
    dst_side_grad = times_turned(act_edge_grad, edge_in[feature_width : 2 * feature_width])
    src_side_grad = times_turned(act_edge_grad, edge_in[2 * feature_width :])
    edge_back = grad_edge + edge_self_grad
    dst_sums = exact_sum(
        "ytkn,ytkd->ynd",
        dst_float,
        dst_side_grad.reshape(blocks_y, tiles, edges_tile, feature_width),
    )
    node_back = grad_node + node_self_grad + dst_sums.reshape(-1, feature_width)
    per_tile = exact_sum(
        "ytkn,ytkd->ytnd",
        src_float,
        src_side_grad.reshape(blocks_y, tiles, edges_tile, feature_width),
    )
    table_back = exact_sum("ytb,ytnd->bnd", block_pick, per_tile)
    return (node_back, edge_back, table_back)


def body(
    node_latents,
    edge_latents,
    tile_offsets,
    edge_dst,
    edge_src,
    edge_in_w,
    edge_out_w,
    node_in_w,
    node_out_w,
    node_cot,
    edge_cot,
):
    window_count = node_latents.shape[0]
    blocks_y = node_latents.shape[2]
    block_nodes = node_latents.shape[3]
    feature_width = node_latents.shape[4]
    tile_codes = tile_offsets[0]
    step_x = tile_codes // 3 - 1
    step_y = tile_codes % 3 - 1
    block_y = lax.broadcasted_iota(jnp.int32, tile_codes.shape, 0)
    source_block = (1 + step_x) * (blocks_y + 2) + block_y + 1 + step_y
    table_blocks = 3 * (blocks_y + 2)
    node_iota = lax.broadcasted_iota(jnp.int32, edge_dst[0].shape + (block_nodes,), 3)
    dst_onehot = (edge_dst[0][..., None] == node_iota).astype(jnp.bfloat16)
    src_onehot = (edge_src[0][..., None] == node_iota).astype(jnp.bfloat16)
    block_iota = lax.broadcasted_iota(jnp.int32, source_block.shape + (table_blocks,), 2)
    block_pick = (source_block[..., None] == block_iota).astype(jnp.float32)
    tables = (dst_onehot, src_onehot, source_block, block_pick)
    weights = (edge_in_w[0], edge_out_w[0], node_in_w[0], node_out_w[0])
    is_first = lax.axis_index("phase") == 0
    node_rows = node_latents.reshape(window_count, -1, feature_width)
    edge_rows = edge_latents.reshape(window_count, -1, feature_width)
    cot_nodes = node_cot.reshape(window_count, -1, feature_width)
    cot_edges = edge_cot.reshape(window_count, -1, feature_width)
    layer_results = []
    kept_list = []
    passed = None
    for step in range(window_count + 1):
        pick = min(step, window_count - 1)
        if passed is None:
            node_input, edge_input = (node_rows[pick], edge_rows[pick])
        else:
            node_input = jnp.where(is_first, node_rows[pick], passed[0])
            edge_input = jnp.where(is_first, edge_rows[pick], passed[1])
        node_grid = node_input.reshape(1, blocks_y, block_nodes, feature_width)
        extended = padded(node_grid, (("px", 0), ("py", 1)), 1)
        node_new, edge_new, kept_values = forward(
            weights,
            tables,
            node_input,
            edge_input,
            extended.reshape(table_blocks, block_nodes, feature_width),
        )
        layer_results.append((node_new, edge_new))
        kept_list.append(kept_values)
        if step < window_count:
            passed = from_behind((node_new, edge_new), "phase", 1)
    grad_results = []
    handed = None
    for step in range(window_count + 1):
        pick = min(step, window_count - 1)
        node_seed = cot_nodes[pick].astype(jnp.float32)
        edge_seed = cot_edges[pick].astype(jnp.float32)
        kept_values = jax.tree.map(
            lambda left, right: jnp.where(is_first, left, right),
            kept_list[max(step - 1, 0)],
            kept_list[min(step + 1, window_count)],
        )
        if handed is None:
            node_upstream, edge_upstream = (node_seed, edge_seed)
        else:
            node_upstream = jnp.where(is_first, handed[0], node_seed)
            edge_upstream = jnp.where(is_first, handed[1], edge_seed)
        node_back, edge_back, table_back = backward(
            weights, tables, kept_values, node_upstream, edge_upstream
        )
        rim_grid = table_back.reshape(3, blocks_y + 2, block_nodes, feature_width)
        beside_all = padded(rim_grid.astype(jnp.bfloat16), (("px", 0), ("py", 1)), 1).astype(
            rim_grid.dtype
        )
        owned_grad = (
            rim_grid[1, 1 : blocks_y + 1]
            + beside_all[0, 2 : blocks_y + 2]
            + beside_all[4, 2 : blocks_y + 2]
        )
        owned_grad = owned_grad.at[0].add(beside_all[2, 0] + beside_all[0, 0] + beside_all[4, 0])
        owned_grad = owned_grad.at[blocks_y - 1].add(
            beside_all[2, blocks_y + 3] + beside_all[0, blocks_y + 3] + beside_all[4, blocks_y + 3]
        )
        node_back, edge_back = (node_back + owned_grad.reshape(-1, feature_width), edge_back)
        grad_results.append((node_back, edge_back))
        if step < window_count:
            handed = (
                from_behind(node_back.astype(jnp.bfloat16), "phase", -1).astype(node_back.dtype),
                from_behind(edge_back.astype(jnp.bfloat16), "phase", -1).astype(edge_back.dtype),
            )
    node_shape = (1,) + node_latents.shape
    edge_shape = (1,) + edge_latents.shape
    node_result = jnp.stack(
        [
            jnp.where(is_first, layer_results[w][0], layer_results[w + 1][0])
            for w in range(window_count)
        ]
    ).reshape(node_shape)
    edge_result = jnp.stack(
        [
            jnp.where(is_first, layer_results[w][1], layer_results[w + 1][1])
            for w in range(window_count)
        ]
    ).reshape(edge_shape)
    node_gradient = jnp.stack(
        [
            jnp.where(is_first, grad_results[w + 1][0], grad_results[w][0])
            for w in range(window_count)
        ]
    ).reshape(node_shape)
    edge_gradient = jnp.stack(
        [
            jnp.where(is_first, grad_results[w + 1][1], grad_results[w][1])
            for w in range(window_count)
        ]
    ).reshape(edge_shape)
    return (node_result, edge_result, node_gradient, edge_gradient)


def solution(mesh):
    return jax.shard_map(
        body,
        mesh=mesh,
        in_specs=(
            P(None, "px", "py", None, None),
            P(None, "px", "py", None, None, None),
            P("px", "py", None),
            P("px", "py", None, None),
            P("px", "py", None, None),
            P("phase", None, None),
            P("phase", None, None),
            P("phase", None, None),
            P("phase", None, None),
            P(None, "px", "py", None, None),
            P(None, "px", "py", None, None, None),
        ),
        out_specs=(
            P("phase", None, "px", "py", None, None),
            P("phase", None, "px", "py", None, None, None),
            P("phase", None, "px", "py", None, None),
            P("phase", None, "px", "py", None, None, None),
        ),
        check_vma=False,
    )
```

profile of v0, /device:TPU:576, one launch (start us, length us, event | category | flops | bytes accessed | tf_op | source)
XLA Modules:
  0.0 201.3 jit_solution(7462458751481601396)
XLA Ops:
  3.8 3.6 %collective-permute-start = (bf16[1,1,128,256]{3,2,1,0:T(8,128)(2,1)S(1)}, bf16[1,1,128,256]{3,2,1,0:T(8,128)(2,1)S(1)}, u32[]{:S(2)}, u32[]{:S(2)}) collective-permute-start(bf16[1,1,128,256]{3,2,1,0:T(8,128)(2,1)S(1)} %slice_bitcast_fusion), channel_id=1, source_target_pairs={{0,64},{64,128},{128,192},{192,256},{256,320},{320,384},{384,448},... | collective-permute-start | bytes 196616 | tf_op jit(solution)/shard_map/ppermute | solution.py:15
  22.7 6.0 %collective-permute-done.2 = bf16[3,1,128,256]{3,2,1,0:T(8,128)(2,1)S(1)} collective-permute-done((bf16[3,1,128,256]{3,2,1,0:T(8,128)(2,1)S(1)}, bf16[3,1,128,256]{3,2,1,0:T(8,128)(2,1)S(1)}, u32[]{:S(2)}, u32[]{:S(2)}) %collective-permute-start.2) | collective-permute-done | bytes 196640 | tf_op jit(solution)/shard_map/ppermute | solution.py:15
  34.7 3.5 %collective-permute-start.7 = (bf16[1,1,128,256]{3,2,1,0:T(8,128)(2,1)S(1)}, bf16[1,1,128,256]{3,2,1,0:T(8,128)(2,1)S(1)}, u32[]{:S(2)}, u32[]{:S(2)}) collective-permute-start(bf16[1,1,128,256]{3,2,1,0:T(8,128)(2,1)S(1)} %bitcast.381), channel_id=1, source_target_pairs={{64,0},{128,64},{192,128},{256,192},{320,256},{384,320},{448,384},... | collective-permute-start | bytes 196616 | tf_op jit(solution)/shard_map/ppermute | solution.py:17
  41.0 4.5 %collective-permute-done.6 = bf16[1,1,128,256]{3,2,1,0:T(8,128)(2,1)S(1)} collective-permute-done((bf16[1,1,128,256]{3,2,1,0:T(8,128)(2,1)S(1)}, bf16[1,1,128,256]{3,2,1,0:T(8,128)(2,1)S(1)}, u32[]{:S(2)}, u32[]{:S(2)}) %collective-permute-start.6) | collective-permute-done | bytes 65568 | tf_op jit(solution)/shard_map/ppermute | solution.py:15
  47.5 3.9 %collective-permute-start.8 = (bf16[3,1,128,256]{3,2,1,0:T(8,128)(2,1)S(1)}, bf16[3,1,128,256]{3,2,1,0:T(8,128)(2,1)S(1)}, u32[]{:S(2)}, u32[]{:S(2)}) collective-permute-start(bf16[3,1,128,256]{3,2,1,0:T(8,128)(2,1)S(1)} %pad_maximum_fusion.15), channel_id=1, source_target_pairs={{0,1},{1,2},{2,3},{3,4},{4,5},{5,6},{6,7},{7,8},{8,9},{9,10},{10,1... | collective-permute-start | bytes 589832 | tf_op jit(solution)/shard_map/ppermute | solution.py:15
  53.1 5.2 %collective-permute-done.8 = bf16[3,1,128,256]{3,2,1,0:T(8,128)(2,1)S(1)} collective-permute-done((bf16[3,1,128,256]{3,2,1,0:T(8,128)(2,1)S(1)}, bf16[3,1,128,256]{3,2,1,0:T(8,128)(2,1)S(1)}, u32[]{:S(2)}, u32[]{:S(2)}) %collective-permute-start.8) | collective-permute-done | bytes 196640 | tf_op jit(solution)/shard_map/ppermute | solution.py:15
  69.1 3.9 %collective-permute-start.12 = (bf16[1,1,128,256]{3,2,1,0:T(8,128)(2,1)S(1)}, bf16[1,1,128,256]{3,2,1,0:T(8,128)(2,1)S(1)}, u32[]{:S(2)}, u32[]{:S(2)}) collective-permute-start(bf16[1,1,128,256]{3,2,1,0:T(8,128)(2,1)S(1)} %bitcast.378), channel_id=1, source_target_pairs={{0,64},{64,128},{128,192},{192,256},{256,320},{320,384},{384,448},... | collective-permute-start | bytes 196616 | tf_op jit(solution)/shard_map/ppermute | solution.py:15
  78.4 3.9 %collective-permute-start.14 = (bf16[3,1,128,256]{3,2,1,0:T(8,128)(2,1)S(1)}, bf16[3,1,128,256]{3,2,1,0:T(8,128)(2,1)S(1)}, u32[]{:S(2)}, u32[]{:S(2)}) collective-permute-start(bf16[3,1,128,256]{3,2,1,0:T(8,128)(2,1)S(1)} %pad_maximum_fusion.16), channel_id=1, source_target_pairs={{0,1},{1,2},{2,3},{3,4},{4,5},{5,6},{6,7},{7,8},{8,9},{9,10},{10,1... | collective-permute-start | bytes 589832 | tf_op jit(solution)/shard_map/ppermute | solution.py:15
  84.0 5.2 %collective-permute-done.14 = bf16[3,1,128,256]{3,2,1,0:T(8,128)(2,1)S(1)} collective-permute-done((bf16[3,1,128,256]{3,2,1,0:T(8,128)(2,1)S(1)}, bf16[3,1,128,256]{3,2,1,0:T(8,128)(2,1)S(1)}, u32[]{:S(2)}, u32[]{:S(2)}) %collective-permute-start.14) | collective-permute-done | bytes 196640 | tf_op jit(solution)/shard_map/ppermute | solution.py:15
  102.2 4.1 %collective-permute-start.16 = (bf16[1,3,128,256]{3,2,1,0:T(8,128)(2,1)S(1)}, bf16[1,3,128,256]{3,2,1,0:T(8,128)(2,1)S(1)}, u32[]{:S(2)}, u32[]{:S(2)}) collective-permute-start(bf16[1,3,128,256]{3,2,1,0:T(8,128)(2,1)S(1)} %get-tuple-element.132), channel_id=1, source_target_pairs={{0,64},{64,128},{128,192},{192,256},{256,320},{320,384},{384,448},... | collective-permute-start | bytes 589832 | tf_op jit(solution)/shard_map/ppermute | solution.py:15
  113.0 3.9 %collective-permute-start.18 = (bf16[5,1,128,256]{3,2,1,0:T(8,128)(2,1)S(1)}, bf16[5,1,128,256]{3,2,1,0:T(8,128)(2,1)S(1)}, u32[]{:S(2)}, u32[]{:S(2)}) collective-permute-start(bf16[5,1,128,256]{3,2,1,0:T(8,128)(2,1)S(1)} %get-tuple-element.126), channel_id=1, source_target_pairs={{0,1},{1,2},{2,3},{3,4},{4,5},{5,6},{6,7},{7,8},{8,9},{9,10},{10,1... | collective-permute-start | bytes 983048 | tf_op jit(solution)/shard_map/ppermute | solution.py:15
  117.2 4.8 %collective-permute-done.19 = bf16[5,1,128,256]{3,2,1,0:T(8,128)(2,1)S(1)} collective-permute-done((bf16[5,1,128,256]{3,2,1,0:T(8,128)(2,1)S(1)}, bf16[5,1,128,256]{3,2,1,0:T(8,128)(2,1)S(1)}, u32[]{:S(2)}, u32[]{:S(2)}) %collective-permute-start.19) | collective-permute-done | bytes 327712 | tf_op jit(solution)/shard_map/ppermute | solution.py:17
  122.0 5.2 %collective-permute-done.18 = bf16[5,1,128,256]{3,2,1,0:T(8,128)(2,1)S(1)} collective-permute-done((bf16[5,1,128,256]{3,2,1,0:T(8,128)(2,1)S(1)}, bf16[5,1,128,256]{3,2,1,0:T(8,128)(2,1)S(1)}, u32[]{:S(2)}, u32[]{:S(2)}) %collective-permute-start.18) | collective-permute-done | bytes 327712 | tf_op jit(solution)/shard_map/ppermute | solution.py:15
  137.8 3.0 %collective-permute-start.22 = (bf16[1,3,128,256]{3,2,1,0:T(8,128)(2,1)S(1)}, bf16[1,3,128,256]{3,2,1,0:T(8,128)(2,1)S(1)}, u32[]{:S(2)}, u32[]{:S(2)}) collective-permute-start(bf16[1,3,128,256]{3,2,1,0:T(8,128)(2,1)S(1)} %get-tuple-element.130), channel_id=1, source_target_pairs={{0,64},{64,128},{128,192},{192,256},{256,320},{320,384},{384,448},... | collective-permute-start | bytes 589832 | tf_op jit(solution)/shard_map/ppermute | solution.py:15
  140.8 3.0 %collective-permute-done.23 = bf16[1,3,128,256]{3,2,1,0:T(8,128)(2,1)S(1)} collective-permute-done((bf16[1,3,128,256]{3,2,1,0:T(8,128)(2,1)S(1)}, bf16[1,3,128,256]{3,2,1,0:T(8,128)(2,1)S(1)}, u32[]{:S(2)}, u32[]{:S(2)}) %collective-permute-start.23) | collective-permute-done | bytes 196640 | tf_op jit(solution)/shard_map/ppermute | solution.py:17
  143.8 3.7 %collective-permute-done.22 = bf16[1,3,128,256]{3,2,1,0:T(8,128)(2,1)S(1)} collective-permute-done((bf16[1,3,128,256]{3,2,1,0:T(8,128)(2,1)S(1)}, bf16[1,3,128,256]{3,2,1,0:T(8,128)(2,1)S(1)}, u32[]{:S(2)}, u32[]{:S(2)}) %collective-permute-start.22) | collective-permute-done | bytes 196640 | tf_op jit(solution)/shard_map/ppermute | solution.py:15
  149.6 3.9 %collective-permute-start.24 = (bf16[5,1,128,256]{3,2,1,0:T(8,128)(2,1)S(1)}, bf16[5,1,128,256]{3,2,1,0:T(8,128)(2,1)S(1)}, u32[]{:S(2)}, u32[]{:S(2)}) collective-permute-start(bf16[5,1,128,256]{3,2,1,0:T(8,128)(2,1)S(1)} %get-tuple-element.124), channel_id=1, source_target_pairs={{0,1},{1,2},{2,3},{3,4},{4,5},{5,6},{6,7},{7,8},{8,9},{9,10},{10,1... | collective-permute-start | bytes 983048 | tf_op jit(solution)/shard_map/ppermute | solution.py:15
  154.2 4.0 %collective-permute-done.25 = bf16[5,1,128,256]{3,2,1,0:T(8,128)(2,1)S(1)} collective-permute-done((bf16[5,1,128,256]{3,2,1,0:T(8,128)(2,1)S(1)}, bf16[5,1,128,256]{3,2,1,0:T(8,128)(2,1)S(1)}, u32[]{:S(2)}, u32[]{:S(2)}) %collective-permute-start.25) | collective-permute-done | bytes 327712 | tf_op jit(solution)/shard_map/ppermute | solution.py:17
  158.2 5.2 %collective-permute-done.24 = bf16[5,1,128,256]{3,2,1,0:T(8,128)(2,1)S(1)} collective-permute-done((bf16[5,1,128,256]{3,2,1,0:T(8,128)(2,1)S(1)}, bf16[5,1,128,256]{3,2,1,0:T(8,128)(2,1)S(1)}, u32[]{:S(2)}, u32[]{:S(2)}) %collective-permute-start.24) | collective-permute-done | bytes 327712 | tf_op jit(solution)/shard_map/ppermute | solution.py:15
  174.1 3.9 %collective-permute-start.28 = (bf16[1,3,128,256]{3,2,1,0:T(8,128)(2,1)S(1)}, bf16[1,3,128,256]{3,2,1,0:T(8,128)(2,1)S(1)}, u32[]{:S(2)}, u32[]{:S(2)}) collective-permute-start(bf16[1,3,128,256]{3,2,1,0:T(8,128)(2,1)S(1)} %get-tuple-element.128), channel_id=1, source_target_pairs={{0,64},{64,128},{128,192},{192,256},{256,320},{320,384},{384,448},... | collective-permute-start | bytes 589832 | tf_op jit(solution)/shard_map/ppermute | solution.py:15
  181.0 3.1 %collective-permute-done.28 = bf16[1,3,128,256]{3,2,1,0:T(8,128)(2,1)S(1)} collective-permute-done((bf16[1,3,128,256]{3,2,1,0:T(8,128)(2,1)S(1)}, bf16[1,3,128,256]{3,2,1,0:T(8,128)(2,1)S(1)}, u32[]{:S(2)}, u32[]{:S(2)}) %collective-permute-start.28) | collective-permute-done | bytes 196640 | tf_op jit(solution)/shard_map/ppermute | solution.py:15
  186.2 3.9 %collective-permute-start.30 = (bf16[5,1,128,256]{3,2,1,0:T(8,128)(2,1)S(1)}, bf16[5,1,128,256]{3,2,1,0:T(8,128)(2,1)S(1)}, u32[]{:S(2)}, u32[]{:S(2)}) collective-permute-start(bf16[5,1,128,256]{3,2,1,0:T(8,128)(2,1)S(1)} %get-tuple-element.122), channel_id=1, source_target_pairs={{0,1},{1,2},{2,3},{3,4},{4,5},{5,6},{6,7},{7,8},{8,9},{9,10},{10,1... | collective-permute-start | bytes 983048 | tf_op jit(solution)/shard_map/ppermute | solution.py:15
  191.2 3.8 %collective-permute-done.31 = bf16[5,1,128,256]{3,2,1,0:T(8,128)(2,1)S(1)} collective-permute-done((bf16[5,1,128,256]{3,2,1,0:T(8,128)(2,1)S(1)}, bf16[5,1,128,256]{3,2,1,0:T(8,128)(2,1)S(1)}, u32[]{:S(2)}, u32[]{:S(2)}) %collective-permute-start.31) | collective-permute-done | bytes 327712 | tf_op jit(solution)/shard_map/ppermute | solution.py:17
  195.1 5.2 %collective-permute-done.30 = bf16[5,1,128,256]{3,2,1,0:T(8,128)(2,1)S(1)} collective-permute-done((bf16[5,1,128,256]{3,2,1,0:T(8,128)(2,1)S(1)}, bf16[5,1,128,256]{3,2,1,0:T(8,128)(2,1)S(1)}, u32[]{:S(2)}, u32[]{:S(2)}) %collective-permute-start.30) | collective-permute-done | bytes 327712 | tf_op jit(solution)/shard_map/ppermute | solution.py:15
  (246 shorter events, 98.4 us)
Async XLA Ops:
  1.6 13.2 %collective-permute-start.1 = (bf16[1,1,128,256]{3,2,1,0:T(8,128)(2,1)S(1)}, bf16[1,1,128,256]{3,2,1,0:T(8,128)(2,1)S(1)}, u32[]{:S(2)}, u32[]{:S(2)}) collective-permute-start(bf16[1,1,128,256]{3,2,1,0:T(8,128)(2,1)S(1)} %slice_bitcast_fusion), channel_id=1, source_target_pairs={{64,0},{128,64},{192,128},{256,192},{320,256},{384,320},{448,384},... | collective-permute-start | bytes 196616 | tf_op jit(solution)/shard_map/ppermute | solution.py:17
  3.8 10.9 %collective-permute-start = (bf16[1,1,128,256]{3,2,1,0:T(8,128)(2,1)S(1)}, bf16[1,1,128,256]{3,2,1,0:T(8,128)(2,1)S(1)}, u32[]{:S(2)}, u32[]{:S(2)}) collective-permute-start(bf16[1,1,128,256]{3,2,1,0:T(8,128)(2,1)S(1)} %slice_bitcast_fusion), channel_id=1, source_target_pairs={{0,64},{64,128},{128,192},{192,256},{256,320},{320,384},{384,448},... | collective-permute-start | bytes 196616 | tf_op jit(solution)/shard_map/ppermute | solution.py:15
  14.8 8.0 %collective-permute-start.3 = (bf16[3,1,128,256]{3,2,1,0:T(8,128)(2,1)S(1)}, bf16[3,1,128,256]{3,2,1,0:T(8,128)(2,1)S(1)}, u32[]{:S(2)}, u32[]{:S(2)}) collective-permute-start(bf16[3,1,128,256]{3,2,1,0:T(8,128)(2,1)S(1)} %pad_maximum_fusion.14), channel_id=1, source_target_pairs={{1,0},{2,1},{3,2},{4,3},{5,4},{6,5},{7,6},{8,7},{9,8},{10,9},{11,1... | collective-permute-start | bytes 589832 | tf_op jit(solution)/shard_map/ppermute | solution.py:17
  17.7 11.0 %collective-permute-start.2 = (bf16[3,1,128,256]{3,2,1,0:T(8,128)(2,1)S(1)}, bf16[3,1,128,256]{3,2,1,0:T(8,128)(2,1)S(1)}, u32[]{:S(2)}, u32[]{:S(2)}) collective-permute-start(bf16[3,1,128,256]{3,2,1,0:T(8,128)(2,1)S(1)} %pad_maximum_fusion.14), channel_id=1, source_target_pairs={{0,1},{1,2},{2,3},{3,4},{4,5},{5,6},{6,7},{7,8},{8,9},{9,10},{10,1... | collective-permute-start | bytes 589832 | tf_op jit(solution)/shard_map/ppermute | solution.py:15
  33.4 18.1 %collective-permute-start.5 = (bf16[320,256]{1,0:T(8,128)(2,1)S(1)}, bf16[320,256]{1,0:T(8,128)(2,1)S(1)}, u32[]{:S(2)}, u32[]{:S(2)}) collective-permute-start(bf16[320,256]{1,0:T(8,128)(2,1)S(1)} %get-tuple-element.118), channel_id=1, source_target_pairs={{0,512},{1,513},{2,514},{3,515},{4,516},{5,517},{6,518},{7,519},{8... | collective-permute-start | bytes 491528 | tf_op jit(solution)/shard_map/ppermute | solution.py:27
  38.2 7.4 %collective-permute-start.6 = (bf16[1,1,128,256]{3,2,1,0:T(8,128)(2,1)S(1)}, bf16[1,1,128,256]{3,2,1,0:T(8,128)(2,1)S(1)}, u32[]{:S(2)}, u32[]{:S(2)}) collective-permute-start(bf16[1,1,128,256]{3,2,1,0:T(8,128)(2,1)S(1)} %bitcast.382), channel_id=1, source_target_pairs={{0,64},{64,128},{128,192},{192,256},{256,320},{320,384},{384,448},... | collective-permute-start | bytes 196616 | tf_op jit(solution)/shard_map/ppermute | solution.py:15
  45.6 7.6 %collective-permute-start.9 = (bf16[3,1,128,256]{3,2,1,0:T(8,128)(2,1)S(1)}, bf16[3,1,128,256]{3,2,1,0:T(8,128)(2,1)S(1)}, u32[]{:S(2)}, u32[]{:S(2)}) collective-permute-start(bf16[3,1,128,256]{3,2,1,0:T(8,128)(2,1)S(1)} %pad_maximum_fusion.15), channel_id=1, source_target_pairs={{1,0},{2,1},{3,2},{4,3},{5,4},{6,5},{7,6},{8,7},{9,8},{10,9},{11,1... | collective-permute-start | bytes 589832 | tf_op jit(solution)/shard_map/ppermute | solution.py:17
  47.5 10.9 %collective-permute-start.8 = (bf16[3,1,128,256]{3,2,1,0:T(8,128)(2,1)S(1)}, bf16[3,1,128,256]{3,2,1,0:T(8,128)(2,1)S(1)}, u32[]{:S(2)}, u32[]{:S(2)}) collective-permute-start(bf16[3,1,128,256]{3,2,1,0:T(8,128)(2,1)S(1)} %pad_maximum_fusion.15), channel_id=1, source_target_pairs={{0,1},{1,2},{2,3},{3,4},{4,5},{5,6},{6,7},{7,8},{8,9},{9,10},{10,1... | collective-permute-start | bytes 589832 | tf_op jit(solution)/shard_map/ppermute | solution.py:15
  65.8 16.5 %collective-permute-start.11 = (bf16[320,256]{1,0:T(8,128)(2,1)S(1)}, bf16[320,256]{1,0:T(8,128)(2,1)S(1)}, u32[]{:S(2)}, u32[]{:S(2)}) collective-permute-start(bf16[320,256]{1,0:T(8,128)(2,1)S(1)} %get-tuple-element.112), channel_id=1, source_target_pairs={{0,512},{1,513},{2,514},{3,515},{4,516},{5,517},{6,518},{7,519},{8... | collective-permute-start | bytes 491528 | tf_op jit(solution)/shard_map/ppermute | solution.py:27
  76.5 7.6 %collective-permute-start.15 = (bf16[3,1,128,256]{3,2,1,0:T(8,128)(2,1)S(1)}, bf16[3,1,128,256]{3,2,1,0:T(8,128)(2,1)S(1)}, u32[]{:S(2)}, u32[]{:S(2)}) collective-permute-start(bf16[3,1,128,256]{3,2,1,0:T(8,128)(2,1)S(1)} %pad_maximum_fusion.16), channel_id=1, source_target_pairs={{1,0},{2,1},{3,2},{4,3},{5,4},{6,5},{7,6},{8,7},{9,8},{10,9},{11,1... | collective-permute-start | bytes 589832 | tf_op jit(solution)/shard_map/ppermute | solution.py:17
  78.4 10.9 %collective-permute-start.14 = (bf16[3,1,128,256]{3,2,1,0:T(8,128)(2,1)S(1)}, bf16[3,1,128,256]{3,2,1,0:T(8,128)(2,1)S(1)}, u32[]{:S(2)}, u32[]{:S(2)}) collective-permute-start(bf16[3,1,128,256]{3,2,1,0:T(8,128)(2,1)S(1)} %pad_maximum_fusion.16), channel_id=1, source_target_pairs={{0,1},{1,2},{2,3},{3,4},{4,5},{5,6},{6,7},{7,8},{8,9},{9,10},{10,1... | collective-permute-start | bytes 589832 | tf_op jit(solution)/shard_map/ppermute | solution.py:15
  100.3 9.0 %collective-permute-start.17 = (bf16[1,3,128,256]{3,2,1,0:T(8,128)(2,1)S(1)}, bf16[1,3,128,256]{3,2,1,0:T(8,128)(2,1)S(1)}, u32[]{:S(2)}, u32[]{:S(2)}) collective-permute-start(bf16[1,3,128,256]{3,2,1,0:T(8,128)(2,1)S(1)} %get-tuple-element.133), channel_id=1, source_target_pairs={{64,0},{128,64},{192,128},{256,192},{320,256},{384,320},{448,384},... | collective-permute-start | bytes 589832 | tf_op jit(solution)/shard_map/ppermute | solution.py:17
  102.2 8.8 %collective-permute-start.16 = (bf16[1,3,128,256]{3,2,1,0:T(8,128)(2,1)S(1)}, bf16[1,3,128,256]{3,2,1,0:T(8,128)(2,1)S(1)}, u32[]{:S(2)}, u32[]{:S(2)}) collective-permute-start(bf16[1,3,128,256]{3,2,1,0:T(8,128)(2,1)S(1)} %get-tuple-element.132), channel_id=1, source_target_pairs={{0,64},{64,128},{128,192},{192,256},{256,320},{320,384},{384,448},... | collective-permute-start | bytes 589832 | tf_op jit(solution)/shard_map/ppermute | solution.py:15
  107.0 24.3 %collective-permute-start.21 = (bf16[320,256]{1,0:T(8,128)(2,1)S(1)}, bf16[320,256]{1,0:T(8,128)(2,1)S(1)}, u32[]{:S(2)}, u32[]{:S(2)}) collective-permute-start(bf16[320,256]{1,0:T(8,128)(2,1)S(1)} %get-tuple-element.167), channel_id=1, source_target_pairs={{512,0},{513,1},{514,2},{515,3},{516,4},{517,5},{518,6},{519,7},{5... | collective-permute-start | bytes 491528 | tf_op jit(solution)/shard_map/ppermute | solution.py:27
  111.0 11.0 %collective-permute-start.19 = (bf16[5,1,128,256]{3,2,1,0:T(8,128)(2,1)S(1)}, bf16[5,1,128,256]{3,2,1,0:T(8,128)(2,1)S(1)}, u32[]{:S(2)}, u32[]{:S(2)}) collective-permute-start(bf16[5,1,128,256]{3,2,1,0:T(8,128)(2,1)S(1)} %get-tuple-element.127), channel_id=1, source_target_pairs={{1,0},{2,1},{3,2},{4,3},{5,4},{6,5},{7,6},{8,7},{9,8},{10,9},{11,1... | collective-permute-start | bytes 983048 | tf_op jit(solution)/shard_map/ppermute | solution.py:17
  113.0 14.3 %collective-permute-start.18 = (bf16[5,1,128,256]{3,2,1,0:T(8,128)(2,1)S(1)}, bf16[5,1,128,256]{3,2,1,0:T(8,128)(2,1)S(1)}, u32[]{:S(2)}, u32[]{:S(2)}) collective-permute-start(bf16[5,1,128,256]{3,2,1,0:T(8,128)(2,1)S(1)} %get-tuple-element.126), channel_id=1, source_target_pairs={{0,1},{1,2},{2,3},{3,4},{4,5},{5,6},{6,7},{7,8},{8,9},{9,10},{10,1... | collective-permute-start | bytes 983048 | tf_op jit(solution)/shard_map/ppermute | solution.py:15
  135.0 8.9 %collective-permute-start.23 = (bf16[1,3,128,256]{3,2,1,0:T(8,128)(2,1)S(1)}, bf16[1,3,128,256]{3,2,1,0:T(8,128)(2,1)S(1)}, u32[]{:S(2)}, u32[]{:S(2)}) collective-permute-start(bf16[1,3,128,256]{3,2,1,0:T(8,128)(2,1)S(1)} %get-tuple-element.131), channel_id=1, source_target_pairs={{64,0},{128,64},{192,128},{256,192},{320,256},{384,320},{448,384},... | collective-permute-start | bytes 589832 | tf_op jit(solution)/shard_map/ppermute | solution.py:17
  137.8 9.8 %collective-permute-start.22 = (bf16[1,3,128,256]{3,2,1,0:T(8,128)(2,1)S(1)}, bf16[1,3,128,256]{3,2,1,0:T(8,128)(2,1)S(1)}, u32[]{:S(2)}, u32[]{:S(2)}) collective-permute-start(bf16[1,3,128,256]{3,2,1,0:T(8,128)(2,1)S(1)} %get-tuple-element.130), channel_id=1, source_target_pairs={{0,64},{64,128},{128,192},{192,256},{256,320},{320,384},{384,448},... | collective-permute-start | bytes 589832 | tf_op jit(solution)/shard_map/ppermute | solution.py:15
  147.6 10.5 %collective-permute-start.25 = (bf16[5,1,128,256]{3,2,1,0:T(8,128)(2,1)S(1)}, bf16[5,1,128,256]{3,2,1,0:T(8,128)(2,1)S(1)}, u32[]{:S(2)}, u32[]{:S(2)}) collective-permute-start(bf16[5,1,128,256]{3,2,1,0:T(8,128)(2,1)S(1)} %get-tuple-element.125), channel_id=1, source_target_pairs={{1,0},{2,1},{3,2},{4,3},{5,4},{6,5},{7,6},{8,7},{9,8},{10,9},{11,1... | collective-permute-start | bytes 983048 | tf_op jit(solution)/shard_map/ppermute | solution.py:17
  149.6 13.8 %collective-permute-start.24 = (bf16[5,1,128,256]{3,2,1,0:T(8,128)(2,1)S(1)}, bf16[5,1,128,256]{3,2,1,0:T(8,128)(2,1)S(1)}, u32[]{:S(2)}, u32[]{:S(2)}) collective-permute-start(bf16[5,1,128,256]{3,2,1,0:T(8,128)(2,1)S(1)} %get-tuple-element.124), channel_id=1, source_target_pairs={{0,1},{1,2},{2,3},{3,4},{4,5},{5,6},{6,7},{7,8},{8,9},{9,10},{10,1... | collective-permute-start | bytes 983048 | tf_op jit(solution)/shard_map/ppermute | solution.py:15
  172.2 8.8 %collective-permute-start.29 = (bf16[1,3,128,256]{3,2,1,0:T(8,128)(2,1)S(1)}, bf16[1,3,128,256]{3,2,1,0:T(8,128)(2,1)S(1)}, u32[]{:S(2)}, u32[]{:S(2)}) collective-permute-start(bf16[1,3,128,256]{3,2,1,0:T(8,128)(2,1)S(1)} %get-tuple-element.129), channel_id=1, source_target_pairs={{64,0},{128,64},{192,128},{256,192},{320,256},{384,320},{448,384},... | collective-permute-start | bytes 589832 | tf_op jit(solution)/shard_map/ppermute | solution.py:17
  174.1 10.1 %collective-permute-start.28 = (bf16[1,3,128,256]{3,2,1,0:T(8,128)(2,1)S(1)}, bf16[1,3,128,256]{3,2,1,0:T(8,128)(2,1)S(1)}, u32[]{:S(2)}, u32[]{:S(2)}) collective-permute-start(bf16[1,3,128,256]{3,2,1,0:T(8,128)(2,1)S(1)} %get-tuple-element.128), channel_id=1, source_target_pairs={{0,64},{64,128},{128,192},{192,256},{256,320},{320,384},{384,448},... | collective-permute-start | bytes 589832 | tf_op jit(solution)/shard_map/ppermute | solution.py:15
  184.2 10.8 %collective-permute-start.31 = (bf16[5,1,128,256]{3,2,1,0:T(8,128)(2,1)S(1)}, bf16[5,1,128,256]{3,2,1,0:T(8,128)(2,1)S(1)}, u32[]{:S(2)}, u32[]{:S(2)}) collective-permute-start(bf16[5,1,128,256]{3,2,1,0:T(8,128)(2,1)S(1)} %get-tuple-element.123), channel_id=1, source_target_pairs={{1,0},{2,1},{3,2},{4,3},{5,4},{6,5},{7,6},{8,7},{9,8},{10,9},{11,1... | collective-permute-start | bytes 983048 | tf_op jit(solution)/shard_map/ppermute | solution.py:17
  186.2 14.1 %collective-permute-start.30 = (bf16[5,1,128,256]{3,2,1,0:T(8,128)(2,1)S(1)}, bf16[5,1,128,256]{3,2,1,0:T(8,128)(2,1)S(1)}, u32[]{:S(2)}, u32[]{:S(2)}) collective-permute-start(bf16[5,1,128,256]{3,2,1,0:T(8,128)(2,1)S(1)} %get-tuple-element.122), channel_id=1, source_target_pairs={{0,1},{1,2},{2,3},{3,4},{4,5},{5,6},{6,7},{7,8},{8,9},{9,10},{10,1... | collective-permute-start | bytes 983048 | tf_op jit(solution)/shard_map/ppermute | solution.py:15
  (32 other events, 171.9 us)
where the time goes:
time: 202 us; the launch traced here: 201 us
  starting transfers between devices  80.6 us (40%)
  waiting for transfers between devices  73.9 us (37%)
  matrix products  24.9 us (12%)
  other arithmetic  11.5 us (6%)
  local copies, waits for them, and re-layouts  8.29 us (4%)
    ppermute x12, waiting for transfers between devices, padded(): lax.ppermute(tail, axis, [(i, (i + 1) % count) for i in range(ends)])  48.3 us
    ppermute x12, starting transfers between devices, padded(): lax.ppermute(tail, axis, [(i, (i + 1) % count) for i in range(ends)])  43.5 us
    ppermute x12, starting transfers between devices, padded(): lax.ppermute(head, axis, [((i + 1) % count, i) for i in range(ends)])  26.8 us
    ppermute x12, waiting for transfers between devices, padded(): lax.ppermute(head, axis, [((i + 1) % count, i) for i in range(ends)])  23.1 us
    dot_general x15, matrix products, exact_sum(): jnp.einsum(form, left, right, precision=lax.Precision.HIGHEST, preferred_...  10.9 us
    ppermute x8, starting transfers between devices, from_behind(): return lax.ppermute(array, axis, pairs)  10.3 us
    dot_general x21, matrix products, times_turned(): lax.dot_general(left, right, (((1,), (1,)), ((), ())), preferred_element_...  5.17 us
    dot_general x21, matrix products, times_plain(): return jnp.dot(left, right, preferred_element_type=jnp.float32)  4.55 us
  transfers between devices with their start and end apart: 32, of which 22 were waited for; matrix products, arithmetic and copies ran while one was open for 8% of the time, Pallas kernels for 0%

commit v1 on v0

v1 whole, which is shorter than its diff:
```python
import jax
import jax.numpy as jnp
from jax import lax
from jax.sharding import PartitionSpec as P


def shifted(array, axis, by):
    count = lax.axis_size(axis)
    pairs = [(i, i + by) for i in range(count) if 0 <= i + by < count]
    return lax.ppermute(array, axis, pairs)


def normalize(values):
    centred = values - jnp.mean(values, axis=-1, keepdims=True)
    inverse = lax.rsqrt(jnp.mean(centred * centred, axis=-1, keepdims=True) + 1e-05)
    return (centred * inverse, inverse)


def norm_back(values, upstream):
    normed, inverse = normalize(values)
    return inverse * (
        upstream
        - jnp.mean(upstream, axis=-1, keepdims=True)
        - normed * jnp.mean(upstream * normed, axis=-1, keepdims=True)
    )


def silu_slope(values):
    squash = jax.nn.sigmoid(values)
    return squash * (1.0 + values * (1.0 - squash))


def times_plain(left, right):
    return jnp.einsum("mrk,kd->mrd", left, right, preferred_element_type=jnp.float32)


def times_turned(left, right):
    return jnp.einsum("mrd,kd->mrk", left, right, preferred_element_type=jnp.float32)


def exact_sum(form, left, right):
    return jnp.einsum(
        form, left, right, precision=lax.Precision.HIGHEST, preferred_element_type=jnp.float32
    )


def neighbourhood(node_blocks):
    column = jnp.stack(
        [shifted(node_blocks, "px", 1), node_blocks, shifted(node_blocks, "px", -1)], axis=1
    )
    grid = jnp.stack([shifted(column, "py", 1), column, shifted(column, "py", -1)], axis=2)
    return grid.reshape((grid.shape[0], 9) + grid.shape[3:])


def return_to_owners(table_back):
    grid = table_back.reshape((table_back.shape[0], 3, 3) + table_back.shape[2:])
    low = grid[:, :, 0].astype(jnp.bfloat16)
    high = grid[:, :, 2].astype(jnp.bfloat16)
    column = (
        grid[:, :, 1]
        + shifted(low, "py", -1).astype(jnp.float32)
        + shifted(high, "py", 1).astype(jnp.float32)
    )
    low = column[:, 0].astype(jnp.bfloat16)
    high = column[:, 2].astype(jnp.bfloat16)
    return (
        column[:, 1]
        + shifted(low, "px", -1).astype(jnp.float32)
        + shifted(high, "px", 1).astype(jnp.float32)
    )


def forward(weights, tables, node_blocks, edge_rows):
    edge_in, edge_outer, node_in, node_outer = weights
    dst_onehot, src_onehot, block_pick = tables
    windows, block_nodes, width = node_blocks.shape
    tiles, edges_tile = dst_onehot.shape[:2]
    source_table = neighbourhood(node_blocks)
    at_dst = jnp.einsum(
        "tkn,mnd->mtkd", dst_onehot, node_blocks, preferred_element_type=jnp.float32
    ).astype(jnp.bfloat16)
    src_blocks = jnp.einsum(
        "tb,mbnd->mtnd", block_pick.astype(jnp.bfloat16), source_table,
        preferred_element_type=jnp.float32,
    ).astype(jnp.bfloat16)
    at_src = jnp.einsum(
        "tkn,mtnd->mtkd", src_onehot, src_blocks, preferred_element_type=jnp.float32
    ).astype(jnp.bfloat16)
    at_dst = at_dst.reshape(windows, -1, width)
    at_src = at_src.reshape(windows, -1, width)
    act_edge = (
        times_plain(edge_rows, edge_in[:width])
        + times_plain(at_dst, edge_in[width : 2 * width])
        + times_plain(at_src, edge_in[2 * width :])
    )
    hidden_edge = jax.nn.silu(act_edge).astype(jnp.bfloat16)
    edge_pre = times_plain(hidden_edge, edge_outer)
    message = normalize(edge_pre)[0]
    edge_new = (edge_rows.astype(jnp.float32) + message).astype(jnp.bfloat16)
    summed = exact_sum(
        "tkn,mtkd->mnd",
        dst_onehot.astype(jnp.float32),
        message.reshape(windows, tiles, edges_tile, width),
    ).astype(jnp.bfloat16)
    act_node = times_plain(node_blocks, node_in[:width]) + times_plain(summed, node_in[width:])
    hidden_node = jax.nn.silu(act_node).astype(jnp.bfloat16)
    node_pre = times_plain(hidden_node, node_outer)
    node_new = (node_blocks.astype(jnp.float32) + normalize(node_pre)[0]).astype(jnp.bfloat16)
    return (node_new, edge_new, (act_edge, edge_pre, act_node, node_pre))


def backward(weights, tables, kept_values, grad_node, grad_edge):
    edge_in, edge_outer, node_in, node_outer = weights
    dst_onehot, src_onehot, block_pick = tables
    act_edge, edge_pre, act_node, node_pre = kept_values
    windows, block_nodes, width = grad_node.shape
    tiles, edges_tile = dst_onehot.shape[:2]
    dst_float = dst_onehot.astype(jnp.float32)
    src_float = src_onehot.astype(jnp.float32)
    pre_node_grad = norm_back(node_pre, grad_node).astype(jnp.bfloat16)
    act_node_grad = (times_turned(pre_node_grad, node_outer) * silu_slope(act_node)).astype(
        jnp.bfloat16
    )
    node_self_grad = times_turned(act_node_grad, node_in[:width])
    summed_grad = times_turned(act_node_grad, node_in[width:])
    message_grad = grad_edge + exact_sum("tkn,mnd->mtkd", dst_float, summed_grad).reshape(
        windows, -1, width
    )
    pre_edge_grad = norm_back(edge_pre, message_grad).astype(jnp.bfloat16)
    act_edge_grad = (times_turned(pre_edge_grad, edge_outer) * silu_slope(act_edge)).astype(
        jnp.bfloat16
    )
    edge_self_grad = times_turned(act_edge_grad, edge_in[:width])
    dst_side_grad = times_turned(act_edge_grad, edge_in[width : 2 * width])
    src_side_grad = times_turned(act_edge_grad, edge_in[2 * width :])
    edge_back = grad_edge + edge_self_grad
    dst_sums = exact_sum(
        "tkn,mtkd->mnd", dst_float, dst_side_grad.reshape(windows, tiles, edges_tile, width)
    )
    per_tile = exact_sum(
        "tkn,mtkd->mtnd", src_float, src_side_grad.reshape(windows, tiles, edges_tile, width)
    )
    table_back = exact_sum("tb,mtnd->mbnd", block_pick, per_tile)
    node_back = grad_node + node_self_grad + dst_sums + return_to_owners(table_back)
    return (node_back, edge_back)


def body(
    node_latents,
    edge_latents,
    tile_offsets,
    edge_dst,
    edge_src,
    edge_in_w,
    edge_out_w,
    node_in_w,
    node_out_w,
    node_cot,
    edge_cot,
):
    windows = node_latents.shape[0]
    block_nodes = node_latents.shape[3]
    width = node_latents.shape[4]
    tile_codes = tile_offsets[0, 0]
    node_iota = lax.broadcasted_iota(jnp.int32, edge_dst[0, 0].shape + (block_nodes,), 2)
    dst_onehot = (edge_dst[0, 0][..., None] == node_iota).astype(jnp.bfloat16)
    src_onehot = (edge_src[0, 0][..., None] == node_iota).astype(jnp.bfloat16)
    block_iota = lax.broadcasted_iota(jnp.int32, tile_codes.shape + (9,), 1)
    block_pick = (tile_codes[..., None] == block_iota).astype(jnp.float32)
    tables = (dst_onehot, src_onehot, block_pick)
    is_first = lax.axis_index("phase") == 0
    own = jnp.concatenate([edge_in_w[0], edge_out_w[0], node_in_w[0], node_out_w[0]], axis=0)
    other = lax.ppermute(own, "phase", [(0, 1), (1, 0)])
    sections = (jnp.where(is_first, own, other), jnp.where(is_first, other, own))
    cuts = [0, 3 * width, 4 * width, 6 * width, 7 * width]
    weights = [
        tuple(packed[cuts[i] : cuts[i + 1]] for i in range(4)) for packed in sections
    ]
    node_zero = node_latents.reshape(windows, block_nodes, width)
    edge_zero = edge_latents.reshape(windows, -1, width)
    node_one, edge_one, kept_one = forward(weights[0], tables, node_zero, edge_zero)
    node_two, edge_two, kept_two = forward(weights[1], tables, node_one, edge_one)
    grad_node_one, grad_edge_one = backward(
        weights[1],
        tables,
        kept_two,
        node_cot.reshape(windows, block_nodes, width).astype(jnp.float32),
        edge_cot.reshape(windows, -1, width).astype(jnp.float32),
    )
    grad_node_zero, grad_edge_zero = backward(
        weights[0], tables, kept_one, grad_node_one, grad_edge_one
    )
    node_shape = (1,) + node_latents.shape
    edge_shape = (1,) + edge_latents.shape
    node_result = jnp.where(is_first, node_one, node_two).reshape(node_shape)
    edge_result = jnp.where(is_first, edge_one, edge_two).reshape(edge_shape)
    node_gradient = jnp.where(is_first, grad_node_zero, grad_node_one).reshape(node_shape)
    edge_gradient = jnp.where(is_first, grad_edge_zero, grad_edge_one).reshape(edge_shape)
    return (node_result, edge_result, node_gradient, edge_gradient)


def solution(mesh):
    return jax.shard_map(
        body,
        mesh=mesh,
        in_specs=(
            P(None, "px", "py", None, None),
            P(None, "px", "py", None, None, None),
            P("px", "py", None),
            P("px", "py", None, None),
            P("px", "py", None, None),
            P("phase", None, None),
            P("phase", None, None),
            P("phase", None, None),
            P("phase", None, None),
            P(None, "px", "py", None, None),
            P(None, "px", "py", None, None, None),
        ),
        out_specs=(
            P("phase", None, "px", "py", None, None),
            P("phase", None, "px", "py", None, None, None),
            P("phase", None, "px", "py", None, None),
            P("phase", None, "px", "py", None, None, None),
        ),
        check_vma=False,
    )
```

time: 202 us -> 164 us (0.81)
  the two profiles are of different devices: /device:TPU:576 before, /device:TPU:430 now
where the time goes in v1:
time: 164 us; the launch traced here: 163 us
  starting transfers between devices  63.1 us (38%)
  waiting for transfers between devices  42.5 us (26%)
  matrix products  31.6 us (19%)
  local copies, waits for them, and re-layouts  13.6 us (8%)
  other arithmetic  10.8 us (7%)
  between operations  1.82 us (1%)
    ppermute x16, starting transfers between devices, shifted(): return lax.ppermute(array, axis, pairs)  61.2 us
    ppermute x16, waiting for transfers between devices, shifted(): return lax.ppermute(array, axis, pairs)  42.5 us
    dot_general x14, matrix products, times_turned(): jnp.einsum('mrd,kd->mrk', left, right, preferred_element_type=jnp.float32)  13.3 us
    dot_general x10, matrix products, exact_sum(): jnp.einsum(form, left, right, precision=lax.Precision.HIGHEST, preferred_...  11.3 us
    unnamed x88, local copies, waits for them, and re-layouts  7.07 us
    dot_general x14, matrix products, times_plain(): jnp.einsum('mrk,kd->mrd', left, right, preferred_element_type=jnp.float32)  4.18 us
  transfers between devices with their start and end apart: 17, of which 13 were waited for; matrix products, arithmetic and copies ran while one was open for 10% of the time, Pallas kernels for 0%

profile of v1, /device:TPU:430, one launch (start us, length us, event | category | flops | bytes accessed | tf_op | source)
XLA Modules:
  0.0 163.4 jit_solution(3127146818401775356)
XLA Ops:
  0.7 2.4 %collective-permute-start.2 = (bf16[2,128,256]{2,1,0:T(8,128)(2,1)}, bf16[2,128,256]{2,1,0:T(8,128)(2,1)S(1)}, u32[]{:S(2)}, u32[]{:S(2)}) collective-permute-start(bf16[2,128,256]{2,1,0:T(8,128)(2,1)} %bitcast.386), channel_id=1, source_target_pairs={{64,0},{128,64},{192,128},{256,192},{320,256},{384,320},{448,384},... | collective-permute-start | bytes 393224 | tf_op jit(solution)/shard_map/ppermute | solution.py:10
  3.0 3.6 %collective-permute-start.1 = (bf16[2,128,256]{2,1,0:T(8,128)(2,1)}, bf16[2,128,256]{2,1,0:T(8,128)(2,1)S(1)}, u32[]{:S(2)}, u32[]{:S(2)}) collective-permute-start(bf16[2,128,256]{2,1,0:T(8,128)(2,1)} %bitcast.387), channel_id=1, source_target_pairs={{0,64},{64,128},{128,192},{192,256},{256,320},{320,384},{384,448},... | collective-permute-start | bytes 393224 | tf_op jit(solution)/shard_map/ppermute | solution.py:10
  14.7 3.3 %collective-permute-start.4 = (bf16[2,3,128,256]{3,2,0,1:T(8,128)(2,1)}, bf16[2,3,128,256]{3,2,0,1:T(8,128)(2,1)}, u32[]{:S(2)}, u32[]{:S(2)}) collective-permute-start(bf16[2,3,128,256]{3,2,0,1:T(8,128)(2,1)} %get-tuple-element.38), channel_id=1, source_target_pairs={{1,0},{2,1},{3,2},{4,3},{5,4},{6,5},{7,6},{8,7},{9,8},{10,9},{11,1... | collective-permute-start | bytes 1179656 | tf_op jit(solution)/shard_map/ppermute | solution.py:10
  18.1 5.8 %collective-permute-start.3 = (bf16[2,3,128,256]{3,2,0,1:T(8,128)(2,1)}, bf16[2,3,128,256]{3,2,0,1:T(8,128)(2,1)}, u32[]{:S(2)}, u32[]{:S(2)}) collective-permute-start(bf16[2,3,128,256]{3,2,0,1:T(8,128)(2,1)} %get-tuple-element.38), channel_id=1, source_target_pairs={{0,1},{1,2},{2,3},{3,4},{4,5},{5,6},{6,7},{7,8},{8,9},{9,10},{10,1... | collective-permute-start | bytes 1179656 | tf_op jit(solution)/shard_map/ppermute | solution.py:10
  24.5 7.3 %collective-permute-done.4 = bf16[2,3,128,256]{3,2,0,1:T(8,128)(2,1)} collective-permute-done((bf16[2,3,128,256]{3,2,0,1:T(8,128)(2,1)}, bf16[2,3,128,256]{3,2,0,1:T(8,128)(2,1)}, u32[]{:S(2)}, u32[]{:S(2)}) %collective-permute-start.4) | collective-permute-done | bytes 393248 | tf_op jit(solution)/shard_map/ppermute | solution.py:10
  41.7 2.2 %collective-permute-start.6 = (bf16[2,128,256]{2,1,0:T(8,128)(2,1)S(1)}, bf16[2,128,256]{2,1,0:T(8,128)(2,1)S(1)}, u32[]{:S(2)}, u32[]{:S(2)}) collective-permute-start(bf16[2,128,256]{2,1,0:T(8,128)(2,1)S(1)} %add_convert_fusion.3), channel_id=1, source_target_pairs={{64,0},{128,64},{192,128},{256,192},{320,256},{384,320},{448,384},... | collective-permute-start | bytes 393224 | tf_op jit(solution)/shard_map/ppermute | solution.py:10
  43.9 4.5 %collective-permute-start.5 = (bf16[2,128,256]{2,1,0:T(8,128)(2,1)S(1)}, bf16[2,128,256]{2,1,0:T(8,128)(2,1)S(1)}, u32[]{:S(2)}, u32[]{:S(2)}) collective-permute-start(bf16[2,128,256]{2,1,0:T(8,128)(2,1)S(1)} %add_convert_fusion.3), channel_id=1, source_target_pairs={{0,64},{64,128},{128,192},{192,256},{256,320},{320,384},{384,448},... | collective-permute-start | bytes 393224 | tf_op jit(solution)/shard_map/ppermute | solution.py:10
  52.9 7.9 %collective-permute-start.7 = (bf16[2,3,128,256]{3,2,0,1:T(8,128)(2,1)S(1)}, bf16[2,3,128,256]{3,2,0,1:T(8,128)(2,1)S(1)}, u32[]{:S(2)}, u32[]{:S(2)}) collective-permute-start(bf16[2,3,128,256]{3,2,0,1:T(8,128)(2,1)S(1)} %get-tuple-element.36), channel_id=1, source_target_pairs={{0,1},{1,2},{2,3},{3,4},{4,5},{5,6},{6,7},{7,8},{8,9},{9,10},{10,1... | collective-permute-start | bytes 1179656 | tf_op jit(solution)/shard_map/ppermute | solution.py:10
  61.4 5.1 %collective-permute-done.8 = bf16[2,3,128,256]{3,2,0,1:T(8,128)(2,1)S(1)} collective-permute-done((bf16[2,3,128,256]{3,2,0,1:T(8,128)(2,1)S(1)}, bf16[2,3,128,256]{3,2,0,1:T(8,128)(2,1)S(1)}, u32[]{:S(2)}, u32[]{:S(2)}) %collective-permute-start.8) | collective-permute-done | bytes 393248 | tf_op jit(solution)/shard_map/ppermute | solution.py:10
  79.6 2.4 %fusion.39 = f32[5,2,256,128]{3,2,1,0:T(8,128)} fusion(f32[2,5,64,256]{3,2,1,0:T(8,128)S(1)} %bitcast.383, s32[5,64]{1,0:T(8,128)S(1)} %bitcast.416), kind=kOutput, calls=%fused_computation.72 | convolution fusion | flops 251699200 | bytes 1967360 | tf_op jit(solution)/shard_map/tkn,mtkd->mtnd/dot_general | solution.py:42
  82.0 2.1 %copy.156 = f32[5,2,256,128]{2,0,3,1:T(8,128)S(1)} copy(f32[5,2,256,128]{3,2,1,0:T(8,128)} %fusion.39) | data formatting | bytes 2621440 | tf_op jit(solution)/shard_map/tkn,mtkd->mtnd/dot_general | solution.py:42
  84.1 2.7 %convolution_bitcast_fusion.1 = f32[2,9,128,256]{3,1,2,0:T(8,128)S(1)} fusion(f32[5,2,256,128]{2,0,3,1:T(8,128)S(1)} %copy.156, s32[5]{0:T(128)} %bitcast.418), kind=kOutput, calls=%fused_computation.1 | convolution fusion | flops 35389484 | bytes 3670036 | tf_op jit(solution)/shard_map/tb,mtnd->mbnd/dot_general | solution.py:42
  88.2 7.7 %collective-permute-start.10 = (bf16[2,3,128,256]{3,2,0,1:T(8,128)(2,1)S(1)}, bf16[2,3,128,256]{3,2,0,1:T(8,128)(2,1)S(1)}, u32[]{:S(2)}, u32[]{:S(2)}) collective-permute-start(bf16[2,3,128,256]{3,2,0,1:T(8,128)(2,1)S(1)} %get-tuple-element.30), channel_id=1, source_target_pairs={{0,1},{1,2},{2,3},{3,4},{4,5},{5,6},{6,7},{7,8},{8,9},{9,10},{10,1... | collective-permute-start | bytes 1179656 | tf_op jit(solution)/shard_map/ppermute | solution.py:10
  99.9 2.2 %collective-permute-done.10 = bf16[2,3,128,256]{3,2,0,1:T(8,128)(2,1)S(1)} collective-permute-done((bf16[2,3,128,256]{3,2,0,1:T(8,128)(2,1)S(1)}, bf16[2,3,128,256]{3,2,0,1:T(8,128)(2,1)S(1)}, u32[]{:S(2)}, u32[]{:S(2)}) %collective-permute-start.10) | collective-permute-done | bytes 393248 | tf_op jit(solution)/shard_map/ppermute | solution.py:10
  102.1 7.4 %collective-permute-done.9 = bf16[2,3,128,256]{3,2,0,1:T(8,128)(2,1)S(1)} collective-permute-done((bf16[2,3,128,256]{3,2,0,1:T(8,128)(2,1)S(1)}, bf16[2,3,128,256]{3,2,0,1:T(8,128)(2,1)S(1)}, u32[]{:S(2)}, u32[]{:S(2)}) %collective-permute-start.9) | collective-permute-done | bytes 393248 | tf_op jit(solution)/shard_map/ppermute | solution.py:10
  109.7 4.7 %collective-permute-start.12 = (bf16[2,128,256]{2,1,0:T(8,128)(2,1)S(1)}, bf16[2,128,256]{2,1,0:T(8,128)(2,1)S(1)}, u32[]{:S(2)}, u32[]{:S(2)}) collective-permute-start(bf16[2,128,256]{2,1,0:T(8,128)(2,1)S(1)} %get-tuple-element.34), channel_id=1, source_target_pairs={{0,64},{64,128},{128,192},{192,256},{256,320},{320,384},{384,448},... | collective-permute-start | bytes 393224 | tf_op jit(solution)/shard_map/ppermute | solution.py:10
  114.4 2.1 %collective-permute-start.11 = (bf16[2,128,256]{2,1,0:T(8,128)(2,1)S(1)}, bf16[2,128,256]{2,1,0:T(8,128)(2,1)S(1)}, u32[]{:S(2)}, u32[]{:S(2)}) collective-permute-start(bf16[2,128,256]{2,1,0:T(8,128)(2,1)S(1)} %get-tuple-element.33), channel_id=1, source_target_pairs={{64,0},{128,64},{192,128},{256,192},{320,256},{384,320},{448,384},... | collective-permute-start | bytes 393224 | tf_op jit(solution)/shard_map/ppermute | solution.py:10
  117.1 5.3 %collective-permute-done.11 = bf16[2,128,256]{2,1,0:T(8,128)(2,1)S(1)} collective-permute-done((bf16[2,128,256]{2,1,0:T(8,128)(2,1)S(1)}, bf16[2,128,256]{2,1,0:T(8,128)(2,1)S(1)}, u32[]{:S(2)}, u32[]{:S(2)}) %collective-permute-start.11) | collective-permute-done | bytes 131104 | tf_op jit(solution)/shard_map/ppermute | solution.py:10
  125.1 2.1 %fusion.132 = (f32[2,320]{1,0:T(2,128)S(1)}, f32[2,320]{1,0:T(2,128)S(1)}, f32[2,320,256]{2,1,0:T(8,128)S(1)}, f32[2,320,256]{2,1,0:T(8,128)}) fusion(f32[2,320,256]{2,1,0:T(8,128)S(1)} %get-tuple-element.24, f32[2,320,256]{2,1,0:T(8,128)S(1)} %bitcast.381, f32[2,320,256]{2,1,0:T(8,128)S(1)} %bitcast.375, bf16[2,320,256]{2,1,0:T(8,128)(2,1)S(1)} %copy-done.6, ...), kind=kOutput, calls=%fused_computation.227 | convolution fusion | flops 84704000 | bytes 3740672 | tf_op jit(solution)/shard_map/mrd,kd->mrk/dot_general | solution.py:38
  134.3 2.1 %collective-permute-start.14 = (bf16[2,3,128,256]{3,2,0,1:T(8,128)(2,1)S(1)}, bf16[2,3,128,256]{3,2,0,1:T(8,128)(2,1)S(1)}, u32[]{:S(2)}, u32[]{:S(2)}) collective-permute-start(bf16[2,3,128,256]{3,2,0,1:T(8,128)(2,1)S(1)} %get-tuple-element.28), channel_id=1, source_target_pairs={{0,1},{1,2},{2,3},{3,4},{4,5},{5,6},{6,7},{7,8},{8,9},{9,10},{10,1... | collective-permute-start | bytes 1179656 | tf_op jit(solution)/shard_map/ppermute | solution.py:10
  136.3 3.9 %collective-permute-start.13 = (bf16[2,3,128,256]{3,2,0,1:T(8,128)(2,1)S(1)}, bf16[2,3,128,256]{3,2,0,1:T(8,128)(2,1)S(1)}, u32[]{:S(2)}, u32[]{:S(2)}) collective-permute-start(bf16[2,3,128,256]{3,2,0,1:T(8,128)(2,1)S(1)} %get-tuple-element.27), channel_id=1, source_target_pairs={{1,0},{2,1},{3,2},{4,3},{5,4},{6,5},{7,6},{8,7},{9,8},{10,9},{11,1... | collective-permute-start | bytes 1179656 | tf_op jit(solution)/shard_map/ppermute | solution.py:10
  144.1 5.2 %collective-permute-done.13 = bf16[2,3,128,256]{3,2,0,1:T(8,128)(2,1)S(1)} collective-permute-done((bf16[2,3,128,256]{3,2,0,1:T(8,128)(2,1)S(1)}, bf16[2,3,128,256]{3,2,0,1:T(8,128)(2,1)S(1)}, u32[]{:S(2)}, u32[]{:S(2)}) %collective-permute-start.13) | collective-permute-done | bytes 393248 | tf_op jit(solution)/shard_map/ppermute | solution.py:10
  149.5 5.1 %collective-permute-start.16 = (bf16[2,128,256]{2,1,0:T(8,128)(2,1)S(1)}, bf16[2,128,256]{2,1,0:T(8,128)(2,1)S(1)}, u32[]{:S(2)}, u32[]{:S(2)}) collective-permute-start(bf16[2,128,256]{2,1,0:T(8,128)(2,1)S(1)} %get-tuple-element.32), channel_id=1, source_target_pairs={{0,64},{64,128},{128,192},{192,256},{256,320},{320,384},{384,448},... | collective-permute-start | bytes 393224 | tf_op jit(solution)/shard_map/ppermute | solution.py:10
  157.1 4.4 %collective-permute-done.15 = bf16[2,128,256]{2,1,0:T(8,128)(2,1)S(1)} collective-permute-done((bf16[2,128,256]{2,1,0:T(8,128)(2,1)S(1)}, bf16[2,128,256]{2,1,0:T(8,128)(2,1)S(1)}, u32[]{:S(2)}, u32[]{:S(2)}) %collective-permute-start.15) | collective-permute-done | bytes 131104 | tf_op jit(solution)/shard_map/ppermute | solution.py:10
  (192 shorter events, 60.0 us)
Async XLA Ops:
  0.7 13.3 %collective-permute-start.2 = (bf16[2,128,256]{2,1,0:T(8,128)(2,1)}, bf16[2,128,256]{2,1,0:T(8,128)(2,1)S(1)}, u32[]{:S(2)}, u32[]{:S(2)}) collective-permute-start(bf16[2,128,256]{2,1,0:T(8,128)(2,1)} %bitcast.386), channel_id=1, source_target_pairs={{64,0},{128,64},{192,128},{256,192},{320,256},{384,320},{448,384},... | collective-permute-start | bytes 393224 | tf_op jit(solution)/shard_map/ppermute | solution.py:10
  3.0 10.9 %collective-permute-start.1 = (bf16[2,128,256]{2,1,0:T(8,128)(2,1)}, bf16[2,128,256]{2,1,0:T(8,128)(2,1)S(1)}, u32[]{:S(2)}, u32[]{:S(2)}) collective-permute-start(bf16[2,128,256]{2,1,0:T(8,128)(2,1)} %bitcast.387), channel_id=1, source_target_pairs={{0,64},{64,128},{128,192},{192,256},{256,320},{320,384},{384,448},... | collective-permute-start | bytes 393224 | tf_op jit(solution)/shard_map/ppermute | solution.py:10
  12.0 23.5 %collective-permute-start = (bf16[1792,256]{0,1:T(8,128)(2,1)}, bf16[1792,256]{0,1:T(8,128)(2,1)}, u32[]{:S(2)}, u32[]{:S(2)}) collective-permute-start(bf16[1792,256]{0,1:T(8,128)(2,1)} %pad_maximum_fusion.2), channel_id=1, source_target_pairs={{0,512},{512,0},{1,513},{513,1},{2,514},{514,2},{3,515},{515,3},{4... | collective-permute-start | bytes 2752520 | tf_op jit(solution)/shard_map/ppermute | solution.py:173
  14.7 17.0 %collective-permute-start.4 = (bf16[2,3,128,256]{3,2,0,1:T(8,128)(2,1)}, bf16[2,3,128,256]{3,2,0,1:T(8,128)(2,1)}, u32[]{:S(2)}, u32[]{:S(2)}) collective-permute-start(bf16[2,3,128,256]{3,2,0,1:T(8,128)(2,1)} %get-tuple-element.38), channel_id=1, source_target_pairs={{1,0},{2,1},{3,2},{4,3},{5,4},{6,5},{7,6},{8,7},{9,8},{10,9},{11,1... | collective-permute-start | bytes 1179656 | tf_op jit(solution)/shard_map/ppermute | solution.py:10
  18.1 14.9 %collective-permute-start.3 = (bf16[2,3,128,256]{3,2,0,1:T(8,128)(2,1)}, bf16[2,3,128,256]{3,2,0,1:T(8,128)(2,1)}, u32[]{:S(2)}, u32[]{:S(2)}) collective-permute-start(bf16[2,3,128,256]{3,2,0,1:T(8,128)(2,1)} %get-tuple-element.38), channel_id=1, source_target_pairs={{0,1},{1,2},{2,3},{3,4},{4,5},{5,6},{6,7},{7,8},{8,9},{9,10},{10,1... | collective-permute-start | bytes 1179656 | tf_op jit(solution)/shard_map/ppermute | solution.py:10
  37.0 41.9 %copy-start.2 = (bf16[1792,256]{0,1:T(8,128)(2,1)}, bf16[1792,256]{0,1:T(8,128)(2,1)S(1)}, u32[]{:S(2)}) copy-start(bf16[1792,256]{0,1:T(8,128)(2,1)S(1)} %get-tuple-element.25) | copy-start | bytes 2752516
  41.5 26.3 %copy-start.35 = (f32[2,128]{1,0:T(2,128)}, f32[2,128]{1,0:T(2,128)S(1)}, u32[]{:S(2)}) copy-start(f32[2,128]{1,0:T(2,128)S(1)} %add_rsqrt_fusion.3) | copy-start | bytes 3076
  41.7 7.9 %collective-permute-start.6 = (bf16[2,128,256]{2,1,0:T(8,128)(2,1)S(1)}, bf16[2,128,256]{2,1,0:T(8,128)(2,1)S(1)}, u32[]{:S(2)}, u32[]{:S(2)}) collective-permute-start(bf16[2,128,256]{2,1,0:T(8,128)(2,1)S(1)} %add_convert_fusion.3), channel_id=1, source_target_pairs={{64,0},{128,64},{192,128},{256,192},{320,256},{384,320},{448,384},... | collective-permute-start | bytes 393224 | tf_op jit(solution)/shard_map/ppermute | solution.py:10
  43.9 7.0 %collective-permute-start.5 = (bf16[2,128,256]{2,1,0:T(8,128)(2,1)S(1)}, bf16[2,128,256]{2,1,0:T(8,128)(2,1)S(1)}, u32[]{:S(2)}, u32[]{:S(2)}) collective-permute-start(bf16[2,128,256]{2,1,0:T(8,128)(2,1)S(1)} %add_convert_fusion.3), channel_id=1, source_target_pairs={{0,64},{64,128},{128,192},{192,256},{256,320},{320,384},{384,448},... | collective-permute-start | bytes 393224 | tf_op jit(solution)/shard_map/ppermute | solution.py:10
  51.0 15.5 %collective-permute-start.8 = (bf16[2,3,128,256]{3,2,0,1:T(8,128)(2,1)S(1)}, bf16[2,3,128,256]{3,2,0,1:T(8,128)(2,1)S(1)}, u32[]{:S(2)}, u32[]{:S(2)}) collective-permute-start(bf16[2,3,128,256]{3,2,0,1:T(8,128)(2,1)S(1)} %get-tuple-element.36), channel_id=1, source_target_pairs={{1,0},{2,1},{3,2},{4,3},{5,4},{6,5},{7,6},{8,7},{9,8},{10,9},{11,1... | collective-permute-start | bytes 1179656 | tf_op jit(solution)/shard_map/ppermute | solution.py:10
  52.9 14.8 %collective-permute-start.7 = (bf16[2,3,128,256]{3,2,0,1:T(8,128)(2,1)S(1)}, bf16[2,3,128,256]{3,2,0,1:T(8,128)(2,1)S(1)}, u32[]{:S(2)}, u32[]{:S(2)}) collective-permute-start(bf16[2,3,128,256]{3,2,0,1:T(8,128)(2,1)S(1)} %get-tuple-element.36), channel_id=1, source_target_pairs={{0,1},{1,2},{2,3},{3,4},{4,5},{5,6},{6,7},{7,8},{8,9},{9,10},{10,1... | collective-permute-start | bytes 1179656 | tf_op jit(solution)/shard_map/ppermute | solution.py:10
  88.2 13.8 %collective-permute-start.10 = (bf16[2,3,128,256]{3,2,0,1:T(8,128)(2,1)S(1)}, bf16[2,3,128,256]{3,2,0,1:T(8,128)(2,1)S(1)}, u32[]{:S(2)}, u32[]{:S(2)}) collective-permute-start(bf16[2,3,128,256]{3,2,0,1:T(8,128)(2,1)S(1)} %get-tuple-element.30), channel_id=1, source_target_pairs={{0,1},{1,2},{2,3},{3,4},{4,5},{5,6},{6,7},{7,8},{8,9},{9,10},{10,1... | collective-permute-start | bytes 1179656 | tf_op jit(solution)/shard_map/ppermute | solution.py:10
  96.0 13.6 %collective-permute-start.9 = (bf16[2,3,128,256]{3,2,0,1:T(8,128)(2,1)S(1)}, bf16[2,3,128,256]{3,2,0,1:T(8,128)(2,1)S(1)}, u32[]{:S(2)}, u32[]{:S(2)}) collective-permute-start(bf16[2,3,128,256]{3,2,0,1:T(8,128)(2,1)S(1)} %get-tuple-element.29), channel_id=1, source_target_pairs={{1,0},{2,1},{3,2},{4,3},{5,4},{6,5},{7,6},{8,7},{9,8},{10,9},{11,1... | collective-permute-start | bytes 1179656 | tf_op jit(solution)/shard_map/ppermute | solution.py:10
  99.9 22.5 %copy-start.11 = (f32[2,128,256]{2,1,0:T(8,128)S(1)}, f32[2,128,256]{2,1,0:T(8,128)}, u32[]{:S(2)}) copy-start(f32[2,128,256]{2,1,0:T(8,128)} %copy-done.10) | copy-start | bytes 786436
  99.9 22.5 %copy-start.19 = (bf16[2,1,1,128,256]{4,3,2,1,0:T(8,128)(2,1)S(1)}, bf16[2,1,1,128,256]{4,3,2,1,0:T(8,128)(2,1)}, u32[]{:S(2)}) copy-start(bf16[2,1,1,128,256]{4,3,2,1,0:T(8,128)(2,1)} %param.20) | copy-start | bytes 393220
  99.9 22.5 %copy-start.26 = (bf16[2,128,256]{1,2,0:T(8,128)(2,1)S(1)}, bf16[2,128,256]{1,2,0:T(8,128)(2,1)}, u32[]{:S(2)}) copy-start(bf16[2,128,256]{1,2,0:T(8,128)(2,1)} %copy-done.25) | copy-start | bytes 393220
  99.9 22.5 %copy-start.36 = (f32[2,128]{1,0:T(2,128)S(1)}, f32[2,128]{1,0:T(2,128)}, u32[]{:S(2)}) copy-start(f32[2,128]{1,0:T(2,128)} %copy-done.35) | copy-start | bytes 3076
  109.7 7.4 %collective-permute-start.12 = (bf16[2,128,256]{2,1,0:T(8,128)(2,1)S(1)}, bf16[2,128,256]{2,1,0:T(8,128)(2,1)S(1)}, u32[]{:S(2)}, u32[]{:S(2)}) collective-permute-start(bf16[2,128,256]{2,1,0:T(8,128)(2,1)S(1)} %get-tuple-element.34), channel_id=1, source_target_pairs={{0,64},{64,128},{128,192},{192,256},{256,320},{320,384},{384,448},... | collective-permute-start | bytes 393224 | tf_op jit(solution)/shard_map/ppermute | solution.py:10
  114.4 7.9 %collective-permute-start.11 = (bf16[2,128,256]{2,1,0:T(8,128)(2,1)S(1)}, bf16[2,128,256]{2,1,0:T(8,128)(2,1)S(1)}, u32[]{:S(2)}, u32[]{:S(2)}) collective-permute-start(bf16[2,128,256]{2,1,0:T(8,128)(2,1)S(1)} %get-tuple-element.33), channel_id=1, source_target_pairs={{64,0},{128,64},{192,128},{256,192},{320,256},{384,320},{448,384},... | collective-permute-start | bytes 393224 | tf_op jit(solution)/shard_map/ppermute | solution.py:10
  134.3 9.8 %collective-permute-start.14 = (bf16[2,3,128,256]{3,2,0,1:T(8,128)(2,1)S(1)}, bf16[2,3,128,256]{3,2,0,1:T(8,128)(2,1)S(1)}, u32[]{:S(2)}, u32[]{:S(2)}) collective-permute-start(bf16[2,3,128,256]{3,2,0,1:T(8,128)(2,1)S(1)} %get-tuple-element.28), channel_id=1, source_target_pairs={{0,1},{1,2},{2,3},{3,4},{4,5},{5,6},{6,7},{7,8},{8,9},{9,10},{10,1... | collective-permute-start | bytes 1179656 | tf_op jit(solution)/shard_map/ppermute | solution.py:10
  136.3 13.0 %collective-permute-start.13 = (bf16[2,3,128,256]{3,2,0,1:T(8,128)(2,1)S(1)}, bf16[2,3,128,256]{3,2,0,1:T(8,128)(2,1)S(1)}, u32[]{:S(2)}, u32[]{:S(2)}) collective-permute-start(bf16[2,3,128,256]{3,2,0,1:T(8,128)(2,1)S(1)} %get-tuple-element.27), channel_id=1, source_target_pairs={{1,0},{2,1},{3,2},{4,3},{5,4},{6,5},{7,6},{8,7},{9,8},{10,9},{11,1... | collective-permute-start | bytes 1179656 | tf_op jit(solution)/shard_map/ppermute | solution.py:10
  143.4 18.1 %copy-start.21 = (f32[2,128,256]{2,1,0:T(8,128)S(1)}, f32[2,128,256]{2,1,0:T(8,128)}, u32[]{:S(2)}) copy-start(f32[2,128,256]{2,1,0:T(8,128)} %copy-done.20) | copy-start | bytes 786436
  149.5 7.6 %collective-permute-start.16 = (bf16[2,128,256]{2,1,0:T(8,128)(2,1)S(1)}, bf16[2,128,256]{2,1,0:T(8,128)(2,1)S(1)}, u32[]{:S(2)}, u32[]{:S(2)}) collective-permute-start(bf16[2,128,256]{2,1,0:T(8,128)(2,1)S(1)} %get-tuple-element.32), channel_id=1, source_target_pairs={{0,64},{64,128},{128,192},{192,256},{256,320},{320,384},{384,448},... | collective-permute-start | bytes 393224 | tf_op jit(solution)/shard_map/ppermute | solution.py:10
  154.6 6.9 %collective-permute-start.15 = (bf16[2,128,256]{2,1,0:T(8,128)(2,1)S(1)}, bf16[2,128,256]{2,1,0:T(8,128)(2,1)S(1)}, u32[]{:S(2)}, u32[]{:S(2)}) collective-permute-start(bf16[2,128,256]{2,1,0:T(8,128)(2,1)S(1)} %get-tuple-element.31), channel_id=1, source_target_pairs={{64,0},{128,64},{192,128},{256,192},{320,256},{384,320},{448,384},... | collective-permute-start | bytes 393224 | tf_op jit(solution)/shard_map/ppermute | solution.py:10
  (34 other events, 190.3 us)

commit v2 on v1

--- a/solution.py
+++ b/solution.py
@@ -45,28 +45,28 @@
 
 
 def neighbourhood(node_blocks):
-    column = jnp.stack(
-        [shifted(node_blocks, "px", 1), node_blocks, shifted(node_blocks, "px", -1)], axis=1
-    )
-    grid = jnp.stack([shifted(column, "py", 1), column, shifted(column, "py", -1)], axis=2)
+    row = jnp.stack(
+        [shifted(node_blocks, "py", 1), node_blocks, shifted(node_blocks, "py", -1)], axis=1
+    )
+    grid = jnp.stack([shifted(row, "px", 1), row, shifted(row, "px", -1)], axis=1)
     return grid.reshape((grid.shape[0], 9) + grid.shape[3:])
 
 
 def return_to_owners(table_back):
     grid = table_back.reshape((table_back.shape[0], 3, 3) + table_back.shape[2:])
-    low = grid[:, :, 0].astype(jnp.bfloat16)
-    high = grid[:, :, 2].astype(jnp.bfloat16)
-    column = (
-        grid[:, :, 1]
+    low = grid[:, 0].astype(jnp.bfloat16)
+    high = grid[:, 2].astype(jnp.bfloat16)
+    row = (
+        grid[:, 1]
+        + shifted(low, "px", -1).astype(jnp.float32)
+        + shifted(high, "px", 1).astype(jnp.float32)
+    )
+    low = row[:, 0].astype(jnp.bfloat16)
+    high = row[:, 2].astype(jnp.bfloat16)
+    return (
+        row[:, 1]
         + shifted(low, "py", -1).astype(jnp.float32)
         + shifted(high, "py", 1).astype(jnp.float32)
-    )
-    low = column[:, 0].astype(jnp.bfloat16)
-    high = column[:, 2].astype(jnp.bfloat16)
-    return (
-        column[:, 1]
-        + shifted(low, "px", -1).astype(jnp.float32)
-        + shifted(high, "px", 1).astype(jnp.float32)
     )
 
 
@@ -176,26 +176,53 @@
     weights = [
         tuple(packed[cuts[i] : cuts[i + 1]] for i in range(4)) for packed in sections
     ]
-    node_zero = node_latents.reshape(windows, block_nodes, width)
-    edge_zero = edge_latents.reshape(windows, -1, width)
+    def mine(array):
+        return jnp.where(is_first, array[0], array[1])[None]
+
+    node_zero = mine(node_latents).reshape(1, block_nodes, width)
+    edge_zero = mine(edge_latents).reshape(1, -1, width)
     node_one, edge_one, kept_one = forward(weights[0], tables, node_zero, edge_zero)
     node_two, edge_two, kept_two = forward(weights[1], tables, node_one, edge_one)
+    latent_send = jnp.where(
+        is_first,
+        jnp.concatenate([node_two[0], edge_two[0]], axis=0),
+        jnp.concatenate([node_one[0], edge_one[0]], axis=0),
+    )
+    latent_recv = lax.ppermute(latent_send, "phase", [(0, 1), (1, 0)])
     grad_node_one, grad_edge_one = backward(
         weights[1],
         tables,
         kept_two,
-        node_cot.reshape(windows, block_nodes, width).astype(jnp.float32),
-        edge_cot.reshape(windows, -1, width).astype(jnp.float32),
+        mine(node_cot).reshape(1, block_nodes, width).astype(jnp.float32),
+        mine(edge_cot).reshape(1, -1, width).astype(jnp.float32),
     )
     grad_node_zero, grad_edge_zero = backward(
         weights[0], tables, kept_one, grad_node_one, grad_edge_one
     )
+    grad_send = jnp.where(
+        is_first,
+        jnp.concatenate([grad_node_one[0], grad_edge_one[0]], axis=0),
+        jnp.concatenate([grad_node_zero[0], grad_edge_zero[0]], axis=0),
+    )
+    grad_recv = lax.ppermute(grad_send, "phase", [(0, 1), (1, 0)])
+
+    def placed(own_first, own_second, received, shape):
+        kept = jnp.where(is_first, own_first, own_second)
+        pair = jnp.where(
+            is_first, jnp.stack([kept, received]), jnp.stack([received, kept])
+        )
+        return pair.reshape(shape)
+
     node_shape = (1,) + node_latents.shape
     edge_shape = (1,) + edge_latents.shape
-    node_result = jnp.where(is_first, node_one, node_two).reshape(node_shape)
-    edge_result = jnp.where(is_first, edge_one, edge_two).reshape(edge_shape)
-    node_gradient = jnp.where(is_first, grad_node_zero, grad_node_one).reshape(node_shape)
-    edge_gradient = jnp.where(is_first, grad_edge_zero, grad_edge_one).reshape(edge_shape)
+    node_result = placed(node_one[0], node_two[0], latent_recv[:block_nodes], node_shape)
+    edge_result = placed(edge_one[0], edge_two[0], latent_recv[block_nodes:], edge_shape)
+    node_gradient = placed(
+        grad_node_zero[0], grad_node_one[0], grad_recv[:block_nodes], node_shape
+    )
+    edge_gradient = placed(
+        grad_edge_zero[0], grad_edge_one[0], grad_recv[block_nodes:], edge_shape
+    )
     return (node_result, edge_result, node_gradient, edge_gradient)
 
 

time: 164 us -> 141 us (0.86)
  the two profiles are of different devices: /device:TPU:430 before, /device:TPU:431 now
where the time goes in v2:
time: 141 us; the launch traced here: 140 us
  starting transfers between devices  71.4 us (51%)
  waiting for transfers between devices  29.9 us (21%)
  matrix products  18.5 us (13%)
  other arithmetic  11.2 us (8%)
  local copies, waits for them, and re-layouts  7.12 us (5%)
  between operations  1.7 us (1%)
    ppermute x16, starting transfers between devices, shifted(): return lax.ppermute(array, axis, pairs)  56.4 us
    ppermute x16, waiting for transfers between devices, shifted(): return lax.ppermute(array, axis, pairs)  29.9 us
    dot_general x10, matrix products, exact_sum(): jnp.einsum(form, left, right, precision=lax.Precision.HIGHEST, preferred_...  7.39 us
    ppermute x1, starting transfers between devices, body(): grad_recv = lax.ppermute(grad_send, 'phase', [(0, 1), (1, 0)])  6.57 us
    dot_general x14, matrix products, times_turned(): jnp.einsum('mrd,kd->mrk', left, right, preferred_element_type=jnp.float32)  6.13 us
    ppermute x1, starting transfers between devices, body(): latent_recv = lax.ppermute(latent_send, 'phase', [(0, 1), (1, 0)])  5.28 us
    ppermute x1, starting transfers between devices, body(): other = lax.ppermute(own, 'phase', [(0, 1), (1, 0)])  3.14 us
    dot_general x14, matrix products, times_plain(): jnp.einsum('mrk,kd->mrd', left, right, preferred_element_type=jnp.float32)  3.1 us
  transfers between devices with their start and end apart: 19, of which 11 were waited for; matrix products, arithmetic and copies ran while one was open for 10% of the time, Pallas kernels for 0%

profile of v2, /device:TPU:431, one launch (start us, length us, event | category | flops | bytes accessed | tf_op | source)
XLA Modules:
  0.0 139.8 jit_solution(14391406172547624909)
XLA Ops:
  1.6 3.1 %collective-permute-start.2 = (bf16[1,128,256]{2,1,0:T(8,128)(2,1)S(1)}, bf16[1,128,256]{2,1,0:T(8,128)(2,1)S(1)}, u32[]{:S(2)}, u32[]{:S(2)}) collective-permute-start(bf16[1,128,256]{2,1,0:T(8,128)(2,1)S(1)} %fusion.179), channel_id=1, source_target_pairs={{1,0},{2,1},{3,2},{4,3},{5,4},{6,5},{7,6},{8,7},{9,8},{10,9},{11,1... | collective-permute-start | bytes 196616 | tf_op jit(solution)/shard_map/ppermute | solution.py:10
  4.7 5.5 %collective-permute-start.1 = (bf16[1,128,256]{2,1,0:T(8,128)(2,1)S(1)}, bf16[1,128,256]{2,1,0:T(8,128)(2,1)S(1)}, u32[]{:S(2)}, u32[]{:S(2)}) collective-permute-start(bf16[1,128,256]{2,1,0:T(8,128)(2,1)S(1)} %fusion.179), channel_id=1, source_target_pairs={{0,1},{1,2},{2,3},{3,4},{4,5},{5,6},{6,7},{7,8},{8,9},{9,10},{10,1... | collective-permute-start | bytes 196616 | tf_op jit(solution)/shard_map/ppermute | solution.py:10
  11.5 3.1 %collective-permute-start = (bf16[1792,256]{1,0:T(8,128)(2,1)S(1)}, bf16[1792,256]{1,0:T(8,128)(2,1)S(1)}, u32[]{:S(2)}, u32[]{:S(2)}) collective-permute-start(bf16[1792,256]{1,0:T(8,128)(2,1)S(1)} %pad_maximum_fusion), channel_id=1, source_target_pairs={{0,512},{512,0},{1,513},{513,1},{2,514},{514,2},{3,515},{515,3},{4... | collective-permute-start | bytes 2752520 | tf_op jit(solution)/shard_map/ppermute | solution.py:173
  15.3 2.1 %collective-permute-start.4 = (bf16[1,3,128,256]{3,2,1,0:T(8,128)(2,1)S(1)}, bf16[1,3,128,256]{3,2,1,0:T(8,128)(2,1)S(1)}, u32[]{:S(2)}, u32[]{:S(2)}) collective-permute-start(bf16[1,3,128,256]{3,2,1,0:T(8,128)(2,1)S(1)} %get-tuple-element.37), channel_id=1, source_target_pairs={{64,0},{128,64},{192,128},{256,192},{320,256},{384,320},{448,384},... | collective-permute-start | bytes 589832 | tf_op jit(solution)/shard_map/ppermute | solution.py:10
  17.4 3.3 %collective-permute-start.3 = (bf16[1,3,128,256]{3,2,1,0:T(8,128)(2,1)S(1)}, bf16[1,3,128,256]{3,2,1,0:T(8,128)(2,1)S(1)}, u32[]{:S(2)}, u32[]{:S(2)}) collective-permute-start(bf16[1,3,128,256]{3,2,1,0:T(8,128)(2,1)S(1)} %get-tuple-element.37), channel_id=1, source_target_pairs={{0,64},{64,128},{128,192},{192,256},{256,320},{320,384},{384,448},... | collective-permute-start | bytes 589832 | tf_op jit(solution)/shard_map/ppermute | solution.py:10
  20.7 3.1 %collective-permute-done.4 = bf16[1,3,128,256]{3,2,1,0:T(8,128)(2,1)S(1)} collective-permute-done((bf16[1,3,128,256]{3,2,1,0:T(8,128)(2,1)S(1)}, bf16[1,3,128,256]{3,2,1,0:T(8,128)(2,1)S(1)}, u32[]{:S(2)}, u32[]{:S(2)}) %collective-permute-start.4) | collective-permute-done | bytes 196640 | tf_op jit(solution)/shard_map/ppermute | solution.py:10
  29.9 1.9 %collective-permute-start.6 = (bf16[1,128,256]{2,1,0:T(8,128)(2,1)S(1)}, bf16[1,128,256]{2,1,0:T(8,128)(2,1)S(1)}, u32[]{:S(2)}, u32[]{:S(2)}) collective-permute-start(bf16[1,128,256]{2,1,0:T(8,128)(2,1)S(1)} %bitcast.323), channel_id=1, source_target_pairs={{1,0},{2,1},{3,2},{4,3},{5,4},{6,5},{7,6},{8,7},{9,8},{10,9},{11,1... | collective-permute-start | bytes 196616 | tf_op jit(solution)/shard_map/ppermute | solution.py:10
  31.9 6.7 %collective-permute-start.5 = (bf16[1,128,256]{2,1,0:T(8,128)(2,1)S(1)}, bf16[1,128,256]{2,1,0:T(8,128)(2,1)S(1)}, u32[]{:S(2)}, u32[]{:S(2)}) collective-permute-start(bf16[1,128,256]{2,1,0:T(8,128)(2,1)S(1)} %bitcast.324), channel_id=1, source_target_pairs={{0,1},{1,2},{2,3},{3,4},{4,5},{5,6},{6,7},{7,8},{8,9},{9,10},{10,1... | collective-permute-start | bytes 196616 | tf_op jit(solution)/shard_map/ppermute | solution.py:10
  39.9 2.0 %collective-permute-start.8 = (bf16[1,3,128,256]{3,2,1,0:T(8,128)(2,1)S(1)}, bf16[1,3,128,256]{3,2,1,0:T(8,128)(2,1)S(1)}, u32[]{:S(2)}, u32[]{:S(2)}) collective-permute-start(bf16[1,3,128,256]{3,2,1,0:T(8,128)(2,1)S(1)} %get-tuple-element.35), channel_id=1, source_target_pairs={{64,0},{128,64},{192,128},{256,192},{320,256},{384,320},{448,384},... | collective-permute-start | bytes 589832 | tf_op jit(solution)/shard_map/ppermute | solution.py:10
  41.9 3.7 %collective-permute-start.7 = (bf16[1,3,128,256]{3,2,1,0:T(8,128)(2,1)S(1)}, bf16[1,3,128,256]{3,2,1,0:T(8,128)(2,1)S(1)}, u32[]{:S(2)}, u32[]{:S(2)}) collective-permute-start(bf16[1,3,128,256]{3,2,1,0:T(8,128)(2,1)S(1)} %get-tuple-element.35), channel_id=1, source_target_pairs={{0,64},{64,128},{128,192},{192,256},{256,320},{320,384},{384,448},... | collective-permute-start | bytes 589832 | tf_op jit(solution)/shard_map/ppermute | solution.py:10
  59.0 5.3 %collective-permute-start.9 = (bf16[448,256]{1,0:T(8,128)(2,1)}, bf16[448,256]{1,0:T(8,128)(2,1)}, u32[]{:S(2)}, u32[]{:S(2)}) collective-permute-start(bf16[448,256]{1,0:T(8,128)(2,1)} %maximum_select_fusion.4), channel_id=1, source_target_pairs={{0,512},{512,0},{1,513},{513,1},{2,514},{514,2},{3,515},{515,3},{4... | collective-permute-start | bytes 688136 | tf_op jit(solution)/shard_map/ppermute | solution.py:191
  69.4 4.8 %collective-permute-start.11 = (bf16[1,3,128,256]{3,2,1,0:T(8,128)(2,1)S(1)}, bf16[1,3,128,256]{3,2,1,0:T(8,128)(2,1)S(1)}, u32[]{:S(2)}, u32[]{:S(2)}) collective-permute-start(bf16[1,3,128,256]{3,2,1,0:T(8,128)(2,1)S(1)} %get-tuple-element.29), channel_id=1, source_target_pairs={{0,64},{64,128},{128,192},{192,256},{256,320},{320,384},{384,448},... | collective-permute-start | bytes 589832 | tf_op jit(solution)/shard_map/ppermute | solution.py:10
  74.2 1.9 %collective-permute-start.10 = (bf16[1,3,128,256]{3,2,1,0:T(8,128)(2,1)S(1)}, bf16[1,3,128,256]{3,2,1,0:T(8,128)(2,1)S(1)}, u32[]{:S(2)}, u32[]{:S(2)}) collective-permute-start(bf16[1,3,128,256]{3,2,1,0:T(8,128)(2,1)S(1)} %get-tuple-element.28), channel_id=1, source_target_pairs={{64,0},{128,64},{192,128},{256,192},{320,256},{384,320},{448,384},... | collective-permute-start | bytes 589832 | tf_op jit(solution)/shard_map/ppermute | solution.py:10
  78.5 6.1 %collective-permute-done.10 = bf16[1,3,128,256]{3,2,1,0:T(8,128)(2,1)S(1)} collective-permute-done((bf16[1,3,128,256]{3,2,1,0:T(8,128)(2,1)S(1)}, bf16[1,3,128,256]{3,2,1,0:T(8,128)(2,1)S(1)}, u32[]{:S(2)}, u32[]{:S(2)}) %collective-permute-start.10) | collective-permute-done | bytes 196640 | tf_op jit(solution)/shard_map/ppermute | solution.py:10
  84.7 7.4 %collective-permute-start.13 = (bf16[1,128,256]{2,1,0:T(8,128)(2,1)S(1)}, bf16[1,128,256]{2,1,0:T(8,128)(2,1)S(1)}, u32[]{:S(2)}, u32[]{:S(2)}) collective-permute-start(bf16[1,128,256]{2,1,0:T(8,128)(2,1)S(1)} %get-tuple-element.33), channel_id=1, source_target_pairs={{0,1},{1,2},{2,3},{3,4},{4,5},{5,6},{6,7},{7,8},{8,9},{9,10},{10,1... | collective-permute-start | bytes 196616 | tf_op jit(solution)/shard_map/ppermute | solution.py:10
  92.1 2.1 %collective-permute-start.12 = (bf16[1,128,256]{2,1,0:T(8,128)(2,1)S(1)}, bf16[1,128,256]{2,1,0:T(8,128)(2,1)S(1)}, u32[]{:S(2)}, u32[]{:S(2)}) collective-permute-start(bf16[1,128,256]{2,1,0:T(8,128)(2,1)S(1)} %get-tuple-element.32), channel_id=1, source_target_pairs={{1,0},{2,1},{3,2},{4,3},{5,4},{6,5},{7,6},{8,7},{9,8},{10,9},{11,1... | collective-permute-start | bytes 196616 | tf_op jit(solution)/shard_map/ppermute | solution.py:10
  97.3 3.1 %collective-permute-done.12 = bf16[1,128,256]{2,1,0:T(8,128)(2,1)S(1)} collective-permute-done((bf16[1,128,256]{2,1,0:T(8,128)(2,1)S(1)}, bf16[1,128,256]{2,1,0:T(8,128)(2,1)S(1)}, u32[]{:S(2)}, u32[]{:S(2)}) %collective-permute-start.12) | collective-permute-done | bytes 65568 | tf_op jit(solution)/shard_map/ppermute | solution.py:10
  106.9 4.4 %collective-permute-start.15 = (bf16[1,3,128,256]{3,2,1,0:T(8,128)(2,1)S(1)}, bf16[1,3,128,256]{3,2,1,0:T(8,128)(2,1)S(1)}, u32[]{:S(2)}, u32[]{:S(2)}) collective-permute-start(bf16[1,3,128,256]{3,2,1,0:T(8,128)(2,1)S(1)} %get-tuple-element.27), channel_id=1, source_target_pairs={{0,64},{64,128},{128,192},{192,256},{256,320},{320,384},{384,448},... | collective-permute-start | bytes 589832 | tf_op jit(solution)/shard_map/ppermute | solution.py:10
  111.3 1.9 %collective-permute-start.14 = (bf16[1,3,128,256]{3,2,1,0:T(8,128)(2,1)S(1)}, bf16[1,3,128,256]{3,2,1,0:T(8,128)(2,1)S(1)}, u32[]{:S(2)}, u32[]{:S(2)}) collective-permute-start(bf16[1,3,128,256]{3,2,1,0:T(8,128)(2,1)S(1)} %get-tuple-element.26), channel_id=1, source_target_pairs={{64,0},{128,64},{192,128},{256,192},{320,256},{384,320},{448,384},... | collective-permute-start | bytes 589832 | tf_op jit(solution)/shard_map/ppermute | solution.py:10
  113.9 3.8 %collective-permute-done.14 = bf16[1,3,128,256]{3,2,1,0:T(8,128)(2,1)S(1)} collective-permute-done((bf16[1,3,128,256]{3,2,1,0:T(8,128)(2,1)S(1)}, bf16[1,3,128,256]{3,2,1,0:T(8,128)(2,1)S(1)}, u32[]{:S(2)}, u32[]{:S(2)}) %collective-permute-start.14) | collective-permute-done | bytes 196640 | tf_op jit(solution)/shard_map/ppermute | solution.py:10
  117.8 3.7 %collective-permute-start.17 = (bf16[1,128,256]{2,1,0:T(8,128)(2,1)S(1)}, bf16[1,128,256]{2,1,0:T(8,128)(2,1)S(1)}, u32[]{:S(2)}, u32[]{:S(2)}) collective-permute-start(bf16[1,128,256]{2,1,0:T(8,128)(2,1)S(1)} %get-tuple-element.31), channel_id=1, source_target_pairs={{0,1},{1,2},{2,3},{3,4},{4,5},{5,6},{6,7},{7,8},{8,9},{9,10},{10,1... | collective-permute-start | bytes 196616 | tf_op jit(solution)/shard_map/ppermute | solution.py:10
  121.5 1.9 %collective-permute-start.16 = (bf16[1,128,256]{2,1,0:T(8,128)(2,1)S(1)}, bf16[1,128,256]{2,1,0:T(8,128)(2,1)S(1)}, u32[]{:S(2)}, u32[]{:S(2)}) collective-permute-start(bf16[1,128,256]{2,1,0:T(8,128)(2,1)S(1)} %get-tuple-element.30), channel_id=1, source_target_pairs={{1,0},{2,1},{3,2},{4,3},{5,4},{6,5},{7,6},{8,7},{9,8},{10,9},{11,1... | collective-permute-start | bytes 196616 | tf_op jit(solution)/shard_map/ppermute | solution.py:10
  123.9 5.9 %collective-permute-done.16 = bf16[1,128,256]{2,1,0:T(8,128)(2,1)S(1)} collective-permute-done((bf16[1,128,256]{2,1,0:T(8,128)(2,1)S(1)}, bf16[1,128,256]{2,1,0:T(8,128)(2,1)S(1)}, u32[]{:S(2)}, u32[]{:S(2)}) %collective-permute-start.16) | collective-permute-done | bytes 65568 | tf_op jit(solution)/shard_map/ppermute | solution.py:10
  130.1 6.6 %collective-permute-start.18 = (f32[448,256]{1,0:T(8,128)S(1)}, f32[448,256]{1,0:T(8,128)S(1)}, u32[]{:S(2)}, u32[]{:S(2)}) collective-permute-start(f32[448,256]{1,0:T(8,128)S(1)} %maximum_select_fusion.1), channel_id=1, source_target_pairs={{0,512},{512,0},{1,513},{513,1},{2,514},{514,2},{3,515},{515,3},{4... | collective-permute-start | bytes 1376264 | tf_op jit(solution)/shard_map/ppermute | solution.py:207
  (178 shorter events, 44.7 us)
Async XLA Ops:
  1.6 13.5 %collective-permute-start.2 = (bf16[1,128,256]{2,1,0:T(8,128)(2,1)S(1)}, bf16[1,128,256]{2,1,0:T(8,128)(2,1)S(1)}, u32[]{:S(2)}, u32[]{:S(2)}) collective-permute-start(bf16[1,128,256]{2,1,0:T(8,128)(2,1)S(1)} %fusion.179), channel_id=1, source_target_pairs={{1,0},{2,1},{3,2},{4,3},{5,4},{6,5},{7,6},{8,7},{9,8},{10,9},{11,1... | collective-permute-start | bytes 196616 | tf_op jit(solution)/shard_map/ppermute | solution.py:10
  4.7 10.5 %collective-permute-start.1 = (bf16[1,128,256]{2,1,0:T(8,128)(2,1)S(1)}, bf16[1,128,256]{2,1,0:T(8,128)(2,1)S(1)}, u32[]{:S(2)}, u32[]{:S(2)}) collective-permute-start(bf16[1,128,256]{2,1,0:T(8,128)(2,1)S(1)} %fusion.179), channel_id=1, source_target_pairs={{0,1},{1,2},{2,3},{3,4},{4,5},{5,6},{6,7},{7,8},{8,9},{9,10},{10,1... | collective-permute-start | bytes 196616 | tf_op jit(solution)/shard_map/ppermute | solution.py:10
  11.5 14.7 %collective-permute-start = (bf16[1792,256]{1,0:T(8,128)(2,1)S(1)}, bf16[1792,256]{1,0:T(8,128)(2,1)S(1)}, u32[]{:S(2)}, u32[]{:S(2)}) collective-permute-start(bf16[1792,256]{1,0:T(8,128)(2,1)S(1)} %pad_maximum_fusion), channel_id=1, source_target_pairs={{0,512},{512,0},{1,513},{513,1},{2,514},{514,2},{3,515},{515,3},{4... | collective-permute-start | bytes 2752520 | tf_op jit(solution)/shard_map/ppermute | solution.py:173
  15.3 8.6 %collective-permute-start.4 = (bf16[1,3,128,256]{3,2,1,0:T(8,128)(2,1)S(1)}, bf16[1,3,128,256]{3,2,1,0:T(8,128)(2,1)S(1)}, u32[]{:S(2)}, u32[]{:S(2)}) collective-permute-start(bf16[1,3,128,256]{3,2,1,0:T(8,128)(2,1)S(1)} %get-tuple-element.37), channel_id=1, source_target_pairs={{64,0},{128,64},{192,128},{256,192},{320,256},{384,320},{448,384},... | collective-permute-start | bytes 589832 | tf_op jit(solution)/shard_map/ppermute | solution.py:10
  17.4 8.1 %collective-permute-start.3 = (bf16[1,3,128,256]{3,2,1,0:T(8,128)(2,1)S(1)}, bf16[1,3,128,256]{3,2,1,0:T(8,128)(2,1)S(1)}, u32[]{:S(2)}, u32[]{:S(2)}) collective-permute-start(bf16[1,3,128,256]{3,2,1,0:T(8,128)(2,1)S(1)} %get-tuple-element.37), channel_id=1, source_target_pairs={{0,64},{64,128},{128,192},{192,256},{256,320},{320,384},{384,448},... | collective-permute-start | bytes 589832 | tf_op jit(solution)/shard_map/ppermute | solution.py:10
  29.9 8.9 %collective-permute-start.6 = (bf16[1,128,256]{2,1,0:T(8,128)(2,1)S(1)}, bf16[1,128,256]{2,1,0:T(8,128)(2,1)S(1)}, u32[]{:S(2)}, u32[]{:S(2)}) collective-permute-start(bf16[1,128,256]{2,1,0:T(8,128)(2,1)S(1)} %bitcast.323), channel_id=1, source_target_pairs={{1,0},{2,1},{3,2},{4,3},{5,4},{6,5},{7,6},{8,7},{9,8},{10,9},{11,1... | collective-permute-start | bytes 196616 | tf_op jit(solution)/shard_map/ppermute | solution.py:10
  31.9 8.0 %collective-permute-start.5 = (bf16[1,128,256]{2,1,0:T(8,128)(2,1)S(1)}, bf16[1,128,256]{2,1,0:T(8,128)(2,1)S(1)}, u32[]{:S(2)}, u32[]{:S(2)}) collective-permute-start(bf16[1,128,256]{2,1,0:T(8,128)(2,1)S(1)} %bitcast.324), channel_id=1, source_target_pairs={{0,1},{1,2},{2,3},{3,4},{4,5},{5,6},{6,7},{7,8},{8,9},{9,10},{10,1... | collective-permute-start | bytes 196616 | tf_op jit(solution)/shard_map/ppermute | solution.py:10
  39.9 6.8 %collective-permute-start.8 = (bf16[1,3,128,256]{3,2,1,0:T(8,128)(2,1)S(1)}, bf16[1,3,128,256]{3,2,1,0:T(8,128)(2,1)S(1)}, u32[]{:S(2)}, u32[]{:S(2)}) collective-permute-start(bf16[1,3,128,256]{3,2,1,0:T(8,128)(2,1)S(1)} %get-tuple-element.35), channel_id=1, source_target_pairs={{64,0},{128,64},{192,128},{256,192},{320,256},{384,320},{448,384},... | collective-permute-start | bytes 589832 | tf_op jit(solution)/shard_map/ppermute | solution.py:10
  41.9 6.7 %collective-permute-start.7 = (bf16[1,3,128,256]{3,2,1,0:T(8,128)(2,1)S(1)}, bf16[1,3,128,256]{3,2,1,0:T(8,128)(2,1)S(1)}, u32[]{:S(2)}, u32[]{:S(2)}) collective-permute-start(bf16[1,3,128,256]{3,2,1,0:T(8,128)(2,1)S(1)} %get-tuple-element.35), channel_id=1, source_target_pairs={{0,64},{64,128},{128,192},{192,256},{256,320},{320,384},{384,448},... | collective-permute-start | bytes 589832 | tf_op jit(solution)/shard_map/ppermute | solution.py:10
  59.0 35.2 %collective-permute-start.9 = (bf16[448,256]{1,0:T(8,128)(2,1)}, bf16[448,256]{1,0:T(8,128)(2,1)}, u32[]{:S(2)}, u32[]{:S(2)}) collective-permute-start(bf16[448,256]{1,0:T(8,128)(2,1)} %maximum_select_fusion.4), channel_id=1, source_target_pairs={{0,512},{512,0},{1,513},{513,1},{2,514},{514,2},{3,515},{515,3},{4... | collective-permute-start | bytes 688136 | tf_op jit(solution)/shard_map/ppermute | solution.py:191
  69.4 31.1 %copy-start.8 = (f32[128,256]{1,0:T(8,128)S(1)}, f32[128,256]{1,0:T(8,128)}, u32[]{:S(2)}) copy-start(f32[128,256]{1,0:T(8,128)} %copy-done.7) | copy-start | bytes 393220
  69.4 31.1 %copy-start.19 = (bf16[128,256]{1,0:T(8,128)(2,1)S(1)}, bf16[128,256]{1,0:T(8,128)(2,1)}, u32[]{:S(2)}) copy-start(bf16[128,256]{1,0:T(8,128)(2,1)} %copy-done.18) | copy-start | bytes 196612
  69.4 31.4 %copy-start.24 = (f32[128,256]{1,0:T(8,128)S(1)}, f32[128,256]{1,0:T(8,128)}, u32[]{:S(2)}) copy-start(f32[128,256]{1,0:T(8,128)} %copy-done.23) | copy-start | bytes 393220
  69.4 9.1 %collective-permute-start.11 = (bf16[1,3,128,256]{3,2,1,0:T(8,128)(2,1)S(1)}, bf16[1,3,128,256]{3,2,1,0:T(8,128)(2,1)S(1)}, u32[]{:S(2)}, u32[]{:S(2)}) collective-permute-start(bf16[1,3,128,256]{3,2,1,0:T(8,128)(2,1)S(1)} %get-tuple-element.29), channel_id=1, source_target_pairs={{0,64},{64,128},{128,192},{192,256},{256,320},{320,384},{384,448},... | collective-permute-start | bytes 589832 | tf_op jit(solution)/shard_map/ppermute | solution.py:10
  74.2 10.4 %collective-permute-start.10 = (bf16[1,3,128,256]{3,2,1,0:T(8,128)(2,1)S(1)}, bf16[1,3,128,256]{3,2,1,0:T(8,128)(2,1)S(1)}, u32[]{:S(2)}, u32[]{:S(2)}) collective-permute-start(bf16[1,3,128,256]{3,2,1,0:T(8,128)(2,1)S(1)} %get-tuple-element.28), channel_id=1, source_target_pairs={{64,0},{128,64},{192,128},{256,192},{320,256},{384,320},{448,384},... | collective-permute-start | bytes 589832 | tf_op jit(solution)/shard_map/ppermute | solution.py:10
  84.7 12.6 %collective-permute-start.13 = (bf16[1,128,256]{2,1,0:T(8,128)(2,1)S(1)}, bf16[1,128,256]{2,1,0:T(8,128)(2,1)S(1)}, u32[]{:S(2)}, u32[]{:S(2)}) collective-permute-start(bf16[1,128,256]{2,1,0:T(8,128)(2,1)S(1)} %get-tuple-element.33), channel_id=1, source_target_pairs={{0,1},{1,2},{2,3},{3,4},{4,5},{5,6},{6,7},{7,8},{8,9},{9,10},{10,1... | collective-permute-start | bytes 196616 | tf_op jit(solution)/shard_map/ppermute | solution.py:10
  92.1 8.3 %collective-permute-start.12 = (bf16[1,128,256]{2,1,0:T(8,128)(2,1)S(1)}, bf16[1,128,256]{2,1,0:T(8,128)(2,1)S(1)}, u32[]{:S(2)}, u32[]{:S(2)}) collective-permute-start(bf16[1,128,256]{2,1,0:T(8,128)(2,1)S(1)} %get-tuple-element.32), channel_id=1, source_target_pairs={{1,0},{2,1},{3,2},{4,3},{5,4},{6,5},{7,6},{8,7},{9,8},{10,9},{11,1... | collective-permute-start | bytes 196616 | tf_op jit(solution)/shard_map/ppermute | solution.py:10
  106.9 7.0 %collective-permute-start.15 = (bf16[1,3,128,256]{3,2,1,0:T(8,128)(2,1)S(1)}, bf16[1,3,128,256]{3,2,1,0:T(8,128)(2,1)S(1)}, u32[]{:S(2)}, u32[]{:S(2)}) collective-permute-start(bf16[1,3,128,256]{3,2,1,0:T(8,128)(2,1)S(1)} %get-tuple-element.27), channel_id=1, source_target_pairs={{0,64},{64,128},{128,192},{192,256},{256,320},{320,384},{384,448},... | collective-permute-start | bytes 589832 | tf_op jit(solution)/shard_map/ppermute | solution.py:10
  111.3 6.4 %collective-permute-start.14 = (bf16[1,3,128,256]{3,2,1,0:T(8,128)(2,1)S(1)}, bf16[1,3,128,256]{3,2,1,0:T(8,128)(2,1)S(1)}, u32[]{:S(2)}, u32[]{:S(2)}) collective-permute-start(bf16[1,3,128,256]{3,2,1,0:T(8,128)(2,1)S(1)} %get-tuple-element.26), channel_id=1, source_target_pairs={{64,0},{128,64},{192,128},{256,192},{320,256},{384,320},{448,384},... | collective-permute-start | bytes 589832 | tf_op jit(solution)/shard_map/ppermute | solution.py:10
  113.4 23.3 %copy-start.20 = (bf16[1,1,1,1,128,256]{5,4,3,2,1,0:T(8,128)(2,1)S(1)}, bf16[1,1,1,1,128,256]{5,4,3,2,1,0:T(8,128)(2,1)}, u32[]{:S(2)}) copy-start(bf16[1,1,1,1,128,256]{5,4,3,2,1,0:T(8,128)(2,1)} %get-tuple-element.20) | copy-start | bytes 196612
  113.4 23.3 %copy-start.21 = (bf16[1,1,1,1,128,256]{5,4,3,2,1,0:T(8,128)(2,1)S(1)}, bf16[1,1,1,1,128,256]{5,4,3,2,1,0:T(8,128)(2,1)}, u32[]{:S(2)}) copy-start(bf16[1,1,1,1,128,256]{5,4,3,2,1,0:T(8,128)(2,1)} %slice_bitcast_fusion.13) | copy-start | bytes 196612
  117.8 6.1 %collective-permute-start.17 = (bf16[1,128,256]{2,1,0:T(8,128)(2,1)S(1)}, bf16[1,128,256]{2,1,0:T(8,128)(2,1)S(1)}, u32[]{:S(2)}, u32[]{:S(2)}) collective-permute-start(bf16[1,128,256]{2,1,0:T(8,128)(2,1)S(1)} %get-tuple-element.31), channel_id=1, source_target_pairs={{0,1},{1,2},{2,3},{3,4},{4,5},{5,6},{6,7},{7,8},{8,9},{9,10},{10,1... | collective-permute-start | bytes 196616 | tf_op jit(solution)/shard_map/ppermute | solution.py:10
  121.5 8.3 %collective-permute-start.16 = (bf16[1,128,256]{2,1,0:T(8,128)(2,1)S(1)}, bf16[1,128,256]{2,1,0:T(8,128)(2,1)S(1)}, u32[]{:S(2)}, u32[]{:S(2)}) collective-permute-start(bf16[1,128,256]{2,1,0:T(8,128)(2,1)S(1)} %get-tuple-element.30), channel_id=1, source_target_pairs={{1,0},{2,1},{3,2},{4,3},{5,4},{6,5},{7,6},{8,7},{9,8},{10,9},{11,1... | collective-permute-start | bytes 196616 | tf_op jit(solution)/shard_map/ppermute | solution.py:10
  130.1 8.1 %collective-permute-start.18 = (f32[448,256]{1,0:T(8,128)S(1)}, f32[448,256]{1,0:T(8,128)S(1)}, u32[]{:S(2)}, u32[]{:S(2)}) collective-permute-start(f32[448,256]{1,0:T(8,128)S(1)} %maximum_select_fusion.1), channel_id=1, source_target_pairs={{0,512},{512,0},{1,513},{513,1},{2,514},{514,2},{3,515},{515,3},{4... | collective-permute-start | bytes 1376264 | tf_op jit(solution)/shard_map/ppermute | solution.py:207
  (24 other events, 259.5 us)

commit v3 on v2

--- a/solution.py
+++ b/solution.py
@@ -2,12 +2,6 @@
 import jax.numpy as jnp
 from jax import lax
 from jax.sharding import PartitionSpec as P
-
-
-def shifted(array, axis, by):
-    count = lax.axis_size(axis)
-    pairs = [(i, i + by) for i in range(count) if 0 <= i + by < count]
-    return lax.ppermute(array, axis, pairs)
 
 
 def normalize(values):
@@ -44,30 +38,36 @@
     )
 
 
+OFFSETS = [(dx, dy) for dx in (-1, 0, 1) for dy in (-1, 0, 1)]
+
+
+def from_offset(array, dx, dy):
+    rows = lax.axis_size("px")
+    cols = lax.axis_size("py")
+    pairs = [
+        ((i + dx) * cols + j + dy, i * cols + j)
+        for i in range(rows)
+        for j in range(cols)
+        if 0 <= i + dx < rows and 0 <= j + dy < cols
+    ]
+    return lax.ppermute(array, ("px", "py"), pairs)
+
+
 def neighbourhood(node_blocks):
-    row = jnp.stack(
-        [shifted(node_blocks, "py", 1), node_blocks, shifted(node_blocks, "py", -1)], axis=1
-    )
-    grid = jnp.stack([shifted(row, "px", 1), row, shifted(row, "px", -1)], axis=1)
-    return grid.reshape((grid.shape[0], 9) + grid.shape[3:])
+    parts = [
+        node_blocks if (dx, dy) == (0, 0) else from_offset(node_blocks, dx, dy)
+        for dx, dy in OFFSETS
+    ]
+    return jnp.stack(parts, axis=1)
 
 
 def return_to_owners(table_back):
-    grid = table_back.reshape((table_back.shape[0], 3, 3) + table_back.shape[2:])
-    low = grid[:, 0].astype(jnp.bfloat16)
-    high = grid[:, 2].astype(jnp.bfloat16)
-    row = (
-        grid[:, 1]
-        + shifted(low, "px", -1).astype(jnp.float32)
-        + shifted(high, "px", 1).astype(jnp.float32)
-    )
-    low = row[:, 0].astype(jnp.bfloat16)
-    high = row[:, 2].astype(jnp.bfloat16)
-    return (
-        row[:, 1]
-        + shifted(low, "py", -1).astype(jnp.float32)
-        + shifted(high, "py", 1).astype(jnp.float32)
-    )
+    total = table_back[:, 4]
+    for index, (dx, dy) in enumerate(OFFSETS):
+        if (dx, dy) != (0, 0):
+            sent = table_back[:, index].astype(jnp.bfloat16)
+            total = total + from_offset(sent, -dx, -dy).astype(jnp.float32)
+    return total
 
 
 def forward(weights, tables, node_blocks, edge_rows):

time: 141 us -> 207 us (1.47)
  the two profiles are of different devices: /device:TPU:431 before, /device:TPU:447 now
where the time goes in v3:
time: 207 us; the launch traced here: 205 us
  starting transfers between devices  140 us (68%)
  waiting for transfers between devices  23.6 us (11%)
  matrix products  19.1 us (9%)
  other arithmetic  13.3 us (6%)
  local copies, waits for them, and re-layouts  7.57 us (4%)
  between operations  2.09 us (1%)
    ppermute x32, starting transfers between devices, from_offset(): return lax.ppermute(array, ('px', 'py'), pairs)  116 us
    ppermute x32, waiting for transfers between devices, from_offset(): return lax.ppermute(array, ('px', 'py'), pairs)  23.6 us
    ppermute x1, starting transfers between devices, body(): latent_recv = lax.ppermute(latent_send, 'phase', [(0, 1), (1, 0)])  11.2 us
    ppermute x1, starting transfers between devices, body(): grad_recv = lax.ppermute(grad_send, 'phase', [(0, 1), (1, 0)])  9.24 us
    dot_general x10, matrix products, exact_sum(): jnp.einsum(form, left, right, precision=lax.Precision.HIGHEST, preferred_...  7.39 us
    dot_general x14, matrix products, times_turned(): jnp.einsum('mrd,kd->mrk', left, right, preferred_element_type=jnp.float32)  6.14 us
    another operation x10, local copies, waits for them, and re-layouts, neighbourhood(): return jnp.stack(parts, axis=1)  4.75 us
  transfers between devices with their start and end apart: 35, of which 6 were waited for; matrix products, arithmetic and copies ran while one was open for 6% of the time, Pallas kernels for 0%

profile of v3, /device:TPU:447, one launch (start us, length us, event | category | flops | bytes accessed | tf_op | source)
XLA Modules:
  0.0 205.5 jit_solution(1061525568070528132)
XLA Ops:
  1.6 8.3 %collective-permute-start.1 = (bf16[1,128,256]{2,1,0:T(8,128)(2,1)S(1)}, bf16[1,128,256]{2,1,0:T(8,128)(2,1)S(1)}, u32[]{:S(2)}, u32[]{:S(2)}) collective-permute-start(bf16[1,128,256]{2,1,0:T(8,128)(2,1)S(1)} %fusion.185), channel_id=1, source_target_pairs={{0,65},{1,66},{2,67},{3,68},{4,69},{5,70},{6,71},{7,72},{8,73},{9,... | collective-permute-start | bytes 196616 | tf_op jit(solution)/shard_map/ppermute | solution.py:53
  9.9 2.4 %collective-permute-start.2 = (bf16[1,128,256]{2,1,0:T(8,128)(2,1)S(1)}, bf16[1,128,256]{2,1,0:T(8,128)(2,1)S(1)}, u32[]{:S(2)}, u32[]{:S(2)}) collective-permute-start(bf16[1,128,256]{2,1,0:T(8,128)(2,1)S(1)} %fusion.185), channel_id=1, source_target_pairs={{0,64},{1,65},{2,66},{3,67},{4,68},{5,69},{6,70},{7,71},{8,72},{9,... | collective-permute-start | bytes 196616 | tf_op jit(solution)/shard_map/ppermute | solution.py:53
  14.3 6.9 %collective-permute-start.4 = (bf16[1,128,256]{2,1,0:T(8,128)(2,1)S(1)}, bf16[1,128,256]{2,1,0:T(8,128)(2,1)S(1)}, u32[]{:S(2)}, u32[]{:S(2)}) collective-permute-start(bf16[1,128,256]{2,1,0:T(8,128)(2,1)S(1)} %fusion.185), channel_id=1, source_target_pairs={{0,1},{1,2},{2,3},{3,4},{4,5},{5,6},{6,7},{7,8},{8,9},{9,10},{10,1... | collective-permute-start | bytes 196616 | tf_op jit(solution)/shard_map/ppermute | solution.py:53
  23.4 3.7 %collective-permute-start = (bf16[1792,256]{1,0:T(8,128)(2,1)}, bf16[1792,256]{1,0:T(8,128)(2,1)}, u32[]{:S(2)}, u32[]{:S(2)}) collective-permute-start(bf16[1792,256]{1,0:T(8,128)(2,1)} %pad_maximum_fusion), channel_id=1, source_target_pairs={{0,512},{512,0},{1,513},{513,1},{2,514},{514,2},{3,515},{515,3},{4... | collective-permute-start | bytes 2752520 | tf_op jit(solution)/shard_map/ppermute | solution.py:173
  30.1 7.4 %collective-permute-start.6 = (bf16[1,128,256]{2,1,0:T(8,128)(2,1)S(1)}, bf16[1,128,256]{2,1,0:T(8,128)(2,1)S(1)}, u32[]{:S(2)}, u32[]{:S(2)}) collective-permute-start(bf16[1,128,256]{2,1,0:T(8,128)(2,1)S(1)} %fusion.185), channel_id=1, source_target_pairs={{64,1},{65,2},{66,3},{67,4},{68,5},{69,6},{70,7},{71,8},{72,9},{73... | collective-permute-start | bytes 196616 | tf_op jit(solution)/shard_map/ppermute | solution.py:53
  37.5 2.9 %collective-permute-start.7 = (bf16[1,128,256]{2,1,0:T(8,128)(2,1)S(1)}, bf16[1,128,256]{2,1,0:T(8,128)(2,1)S(1)}, u32[]{:S(2)}, u32[]{:S(2)}) collective-permute-start(bf16[1,128,256]{2,1,0:T(8,128)(2,1)S(1)} %fusion.185), channel_id=1, source_target_pairs={{64,0},{65,1},{66,2},{67,3},{68,4},{69,5},{70,6},{71,7},{72,8},{73... | collective-permute-start | bytes 196616 | tf_op jit(solution)/shard_map/ppermute | solution.py:53
  45.2 5.7 %collective-permute-done.8 = bf16[1,128,256]{2,1,0:T(8,128)(2,1)S(1)} collective-permute-done((bf16[1,128,256]{2,1,0:T(8,128)(2,1)S(1)}, bf16[1,128,256]{2,1,0:T(8,128)(2,1)S(1)}, u32[]{:S(2)}, u32[]{:S(2)}) %collective-permute-start.8) | collective-permute-done | bytes 65568 | tf_op jit(solution)/shard_map/ppermute | solution.py:53
  51.6 3.3 %stack.121 = bf16[1,9,128,256]{3,1,2,0:T(8,128)(2,1)S(1)} concatenate(bf16[1,1,128,256]{3,1,2,0:T(2,128)(2,1)S(1)} %copy.150, bf16[1,1,128,256]{3,1,2,0:T(2,128)(2,1)S(1)} %copy.151, bf16[1,1,128,256]{3,1,2,0:T(2,128)(2,1)S(1)} %copy.152, bf16[1,1,128,256]{3,1,2,0:T(2,128)(2,1)S(1)} %copy.153, bf16[1,1,128,256]{3,1,2,0:T(2,128)(2,1)S(1)} %copy.154, ...), dimensions={1} | concatenate | bytes 1179648 | tf_op jit(solution)/shard_map/stack | solution.py:61
  64.5 3.3 %collective-permute-start.11 = (bf16[1,128,256]{2,1,0:T(8,128)(2,1)S(1)}, bf16[1,128,256]{2,1,0:T(8,128)(2,1)S(1)}, u32[]{:S(2)}, u32[]{:S(2)}) collective-permute-start(bf16[1,128,256]{2,1,0:T(8,128)(2,1)S(1)} %bitcast.360), channel_id=1, source_target_pairs={{1,64},{2,65},{3,66},{4,67},{5,68},{6,69},{7,70},{8,71},{9,72},{10... | collective-permute-start | bytes 196616 | tf_op jit(solution)/shard_map/ppermute | solution.py:53
  67.9 5.5 %collective-permute-start.12 = (bf16[1,128,256]{2,1,0:T(8,128)(2,1)S(1)}, bf16[1,128,256]{2,1,0:T(8,128)(2,1)S(1)}, u32[]{:S(2)}, u32[]{:S(2)}) collective-permute-start(bf16[1,128,256]{2,1,0:T(8,128)(2,1)S(1)} %bitcast.361), channel_id=1, source_target_pairs={{0,1},{1,2},{2,3},{3,4},{4,5},{5,6},{6,7},{7,8},{8,9},{9,10},{10,1... | collective-permute-start | bytes 196616 | tf_op jit(solution)/shard_map/ppermute | solution.py:53
  75.8 7.4 %collective-permute-start.14 = (bf16[1,128,256]{2,1,0:T(8,128)(2,1)S(1)}, bf16[1,128,256]{2,1,0:T(8,128)(2,1)S(1)}, u32[]{:S(2)}, u32[]{:S(2)}) collective-permute-start(bf16[1,128,256]{2,1,0:T(8,128)(2,1)S(1)} %bitcast.363), channel_id=1, source_target_pairs={{64,1},{65,2},{66,3},{67,4},{68,5},{69,6},{70,7},{71,8},{72,9},{73... | collective-permute-start | bytes 196616 | tf_op jit(solution)/shard_map/ppermute | solution.py:53
  83.2 2.9 %collective-permute-start.15 = (bf16[1,128,256]{2,1,0:T(8,128)(2,1)S(1)}, bf16[1,128,256]{2,1,0:T(8,128)(2,1)S(1)}, u32[]{:S(2)}, u32[]{:S(2)}) collective-permute-start(bf16[1,128,256]{2,1,0:T(8,128)(2,1)S(1)} %bitcast.364), channel_id=1, source_target_pairs={{64,0},{65,1},{66,2},{67,3},{68,4},{69,5},{70,6},{71,7},{72,8},{73... | collective-permute-start | bytes 196616 | tf_op jit(solution)/shard_map/ppermute | solution.py:53
  90.1 6.4 %collective-permute-done.16 = bf16[1,128,256]{2,1,0:T(8,128)(2,1)S(1)} collective-permute-done((bf16[1,128,256]{2,1,0:T(8,128)(2,1)S(1)}, bf16[1,128,256]{2,1,0:T(8,128)(2,1)S(1)}, u32[]{:S(2)}, u32[]{:S(2)}) %collective-permute-start.16) | collective-permute-done | bytes 65568 | tf_op jit(solution)/shard_map/ppermute | solution.py:53
  114.9 3.3 %collective-permute-start.23 = (bf16[1,128,256]{2,1,0:T(8,128)(2,1)S(1)}, bf16[1,128,256]{2,1,0:T(8,128)(2,1)S(1)}, u32[]{:S(2)}, u32[]{:S(2)}) collective-permute-start(bf16[1,128,256]{2,1,0:T(8,128)(2,1)S(1)} %get-tuple-element.37), channel_id=1, source_target_pairs={{1,64},{2,65},{3,66},{4,67},{5,68},{6,69},{7,70},{8,71},{9,72},{10... | collective-permute-start | bytes 196616 | tf_op jit(solution)/shard_map/ppermute | solution.py:53
  118.2 5.5 %collective-permute-start.22 = (bf16[1,128,256]{2,1,0:T(8,128)(2,1)S(1)}, bf16[1,128,256]{2,1,0:T(8,128)(2,1)S(1)}, u32[]{:S(2)}, u32[]{:S(2)}) collective-permute-start(bf16[1,128,256]{2,1,0:T(8,128)(2,1)S(1)} %get-tuple-element.38), channel_id=1, source_target_pairs={{0,1},{1,2},{2,3},{3,4},{4,5},{5,6},{6,7},{7,8},{8,9},{9,10},{10,1... | collective-permute-start | bytes 196616 | tf_op jit(solution)/shard_map/ppermute | solution.py:53
  126.2 7.4 %collective-permute-start.20 = (bf16[1,128,256]{2,1,0:T(8,128)(2,1)S(1)}, bf16[1,128,256]{2,1,0:T(8,128)(2,1)S(1)}, u32[]{:S(2)}, u32[]{:S(2)}) collective-permute-start(bf16[1,128,256]{2,1,0:T(8,128)(2,1)S(1)} %get-tuple-element.40), channel_id=1, source_target_pairs={{64,1},{65,2},{66,3},{67,4},{68,5},{69,6},{70,7},{71,8},{72,9},{73... | collective-permute-start | bytes 196616 | tf_op jit(solution)/shard_map/ppermute | solution.py:53
  133.5 2.9 %collective-permute-start.19 = (bf16[1,128,256]{2,1,0:T(8,128)(2,1)S(1)}, bf16[1,128,256]{2,1,0:T(8,128)(2,1)S(1)}, u32[]{:S(2)}, u32[]{:S(2)}) collective-permute-start(bf16[1,128,256]{2,1,0:T(8,128)(2,1)S(1)} %get-tuple-element.41), channel_id=1, source_target_pairs={{64,0},{65,1},{66,2},{67,3},{68,4},{69,5},{70,6},{71,7},{72,8},{73... | collective-permute-start | bytes 196616 | tf_op jit(solution)/shard_map/ppermute | solution.py:53
  140.6 6.3 %collective-permute-done.18 = bf16[1,128,256]{2,1,0:T(8,128)(2,1)S(1)} collective-permute-done((bf16[1,128,256]{2,1,0:T(8,128)(2,1)S(1)}, bf16[1,128,256]{2,1,0:T(8,128)(2,1)S(1)}, u32[]{:S(2)}, u32[]{:S(2)}) %collective-permute-start.18) | collective-permute-done | bytes 65568 | tf_op jit(solution)/shard_map/ppermute | solution.py:53
  157.8 3.3 %collective-permute-start.31 = (bf16[1,128,256]{2,1,0:T(8,128)(2,1)S(1)}, bf16[1,128,256]{2,1,0:T(8,128)(2,1)S(1)}, u32[]{:S(2)}, u32[]{:S(2)}) collective-permute-start(bf16[1,128,256]{2,1,0:T(8,128)(2,1)S(1)} %get-tuple-element.29), channel_id=1, source_target_pairs={{1,64},{2,65},{3,66},{4,67},{5,68},{6,69},{7,70},{8,71},{9,72},{10... | collective-permute-start | bytes 196616 | tf_op jit(solution)/shard_map/ppermute | solution.py:53
  161.3 5.5 %collective-permute-start.30 = (bf16[1,128,256]{2,1,0:T(8,128)(2,1)S(1)}, bf16[1,128,256]{2,1,0:T(8,128)(2,1)S(1)}, u32[]{:S(2)}, u32[]{:S(2)}) collective-permute-start(bf16[1,128,256]{2,1,0:T(8,128)(2,1)S(1)} %get-tuple-element.30), channel_id=1, source_target_pairs={{0,1},{1,2},{2,3},{3,4},{4,5},{5,6},{6,7},{7,8},{8,9},{9,10},{10,1... | collective-permute-start | bytes 196616 | tf_op jit(solution)/shard_map/ppermute | solution.py:53
  168.8 7.4 %collective-permute-start.28 = (bf16[1,128,256]{2,1,0:T(8,128)(2,1)S(1)}, bf16[1,128,256]{2,1,0:T(8,128)(2,1)S(1)}, u32[]{:S(2)}, u32[]{:S(2)}) collective-permute-start(bf16[1,128,256]{2,1,0:T(8,128)(2,1)S(1)} %get-tuple-element.32), channel_id=1, source_target_pairs={{64,1},{65,2},{66,3},{67,4},{68,5},{69,6},{70,7},{71,8},{72,9},{73... | collective-permute-start | bytes 196616 | tf_op jit(solution)/shard_map/ppermute | solution.py:53
  176.1 2.9 %collective-permute-start.27 = (bf16[1,128,256]{2,1,0:T(8,128)(2,1)S(1)}, bf16[1,128,256]{2,1,0:T(8,128)(2,1)S(1)}, u32[]{:S(2)}, u32[]{:S(2)}) collective-permute-start(bf16[1,128,256]{2,1,0:T(8,128)(2,1)S(1)} %get-tuple-element.33), channel_id=1, source_target_pairs={{64,0},{65,1},{66,2},{67,3},{68,4},{69,5},{70,6},{71,7},{72,8},{73... | collective-permute-start | bytes 196616 | tf_op jit(solution)/shard_map/ppermute | solution.py:53
  181.5 11.2 %collective-permute-start.17 = (bf16[448,256]{1,0:T(8,128)(2,1)S(1)}, bf16[448,256]{1,0:T(8,128)(2,1)S(1)}, u32[]{:S(2)}, u32[]{:S(2)}) collective-permute-start(bf16[448,256]{1,0:T(8,128)(2,1)S(1)} %copy-done.24), channel_id=1, source_target_pairs={{0,512},{512,0},{1,513},{513,1},{2,514},{514,2},{3,515},{515,3},{4... | collective-permute-start | bytes 688136 | tf_op jit(solution)/shard_map/ppermute | solution.py:191
  193.1 9.2 %collective-permute-start.34 = (f32[448,256]{1,0:T(8,128)S(1)}, f32[448,256]{1,0:T(8,128)S(1)}, u32[]{:S(2)}, u32[]{:S(2)}) collective-permute-start(f32[448,256]{1,0:T(8,128)S(1)} %maximum_select_fusion.1), channel_id=1, source_target_pairs={{0,512},{512,0},{1,513},{513,1},{2,514},{514,2},{3,515},{515,3},{4... | collective-permute-start | bytes 1376264 | tf_op jit(solution)/shard_map/ppermute | solution.py:207
  (227 shorter events, 72.6 us)
Async XLA Ops:
  1.6 26.6 %collective-permute-start.1 = (bf16[1,128,256]{2,1,0:T(8,128)(2,1)S(1)}, bf16[1,128,256]{2,1,0:T(8,128)(2,1)S(1)}, u32[]{:S(2)}, u32[]{:S(2)}) collective-permute-start(bf16[1,128,256]{2,1,0:T(8,128)(2,1)S(1)} %fusion.185), channel_id=1, source_target_pairs={{0,65},{1,66},{2,67},{3,68},{4,69},{5,70},{6,71},{7,72},{8,73},{9,... | collective-permute-start | bytes 196616 | tf_op jit(solution)/shard_map/ppermute | solution.py:53
  9.9 20.2 %collective-permute-start.2 = (bf16[1,128,256]{2,1,0:T(8,128)(2,1)S(1)}, bf16[1,128,256]{2,1,0:T(8,128)(2,1)S(1)}, u32[]{:S(2)}, u32[]{:S(2)}) collective-permute-start(bf16[1,128,256]{2,1,0:T(8,128)(2,1)S(1)} %fusion.185), channel_id=1, source_target_pairs={{0,64},{1,65},{2,66},{3,67},{4,68},{5,69},{6,70},{7,71},{8,72},{9,... | collective-permute-start | bytes 196616 | tf_op jit(solution)/shard_map/ppermute | solution.py:53
  12.3 25.2 %collective-permute-start.3 = (bf16[1,128,256]{2,1,0:T(8,128)(2,1)S(1)}, bf16[1,128,256]{2,1,0:T(8,128)(2,1)S(1)}, u32[]{:S(2)}, u32[]{:S(2)}) collective-permute-start(bf16[1,128,256]{2,1,0:T(8,128)(2,1)S(1)} %fusion.185), channel_id=1, source_target_pairs={{1,64},{2,65},{3,66},{4,67},{5,68},{6,69},{7,70},{8,71},{9,72},{10... | collective-permute-start | bytes 196616 | tf_op jit(solution)/shard_map/ppermute | solution.py:53
  14.3 26.1 %collective-permute-start.4 = (bf16[1,128,256]{2,1,0:T(8,128)(2,1)S(1)}, bf16[1,128,256]{2,1,0:T(8,128)(2,1)S(1)}, u32[]{:S(2)}, u32[]{:S(2)}) collective-permute-start(bf16[1,128,256]{2,1,0:T(8,128)(2,1)S(1)} %fusion.185), channel_id=1, source_target_pairs={{0,1},{1,2},{2,3},{3,4},{4,5},{5,6},{6,7},{7,8},{8,9},{9,10},{10,1... | collective-permute-start | bytes 196616 | tf_op jit(solution)/shard_map/ppermute | solution.py:53
  23.4 32.1 %collective-permute-start = (bf16[1792,256]{1,0:T(8,128)(2,1)}, bf16[1792,256]{1,0:T(8,128)(2,1)}, u32[]{:S(2)}, u32[]{:S(2)}) collective-permute-start(bf16[1792,256]{1,0:T(8,128)(2,1)} %pad_maximum_fusion), channel_id=1, source_target_pairs={{0,512},{512,0},{1,513},{513,1},{2,514},{514,2},{3,515},{515,3},{4... | collective-permute-start | bytes 2752520 | tf_op jit(solution)/shard_map/ppermute | solution.py:173
  28.2 14.7 %collective-permute-start.5 = (bf16[1,128,256]{2,1,0:T(8,128)(2,1)S(1)}, bf16[1,128,256]{2,1,0:T(8,128)(2,1)S(1)}, u32[]{:S(2)}, u32[]{:S(2)}) collective-permute-start(bf16[1,128,256]{2,1,0:T(8,128)(2,1)S(1)} %fusion.185), channel_id=1, source_target_pairs={{1,0},{2,1},{3,2},{4,3},{5,4},{6,5},{7,6},{8,7},{9,8},{10,9},{11,1... | collective-permute-start | bytes 196616 | tf_op jit(solution)/shard_map/ppermute | solution.py:53
  60.2 15.6 %collective-permute-start.9 = (bf16[1,128,256]{2,1,0:T(8,128)(2,1)S(1)}, bf16[1,128,256]{2,1,0:T(8,128)(2,1)S(1)}, u32[]{:S(2)}, u32[]{:S(2)}) collective-permute-start(bf16[1,128,256]{2,1,0:T(8,128)(2,1)S(1)} %bitcast.358), channel_id=1, source_target_pairs={{0,65},{1,66},{2,67},{3,68},{4,69},{5,70},{6,71},{7,72},{8,73},{9,... | collective-permute-start | bytes 196616 | tf_op jit(solution)/shard_map/ppermute | solution.py:53
  62.1 21.0 %collective-permute-start.10 = (bf16[1,128,256]{2,1,0:T(8,128)(2,1)S(1)}, bf16[1,128,256]{2,1,0:T(8,128)(2,1)S(1)}, u32[]{:S(2)}, u32[]{:S(2)}) collective-permute-start(bf16[1,128,256]{2,1,0:T(8,128)(2,1)S(1)} %bitcast.359), channel_id=1, source_target_pairs={{0,64},{1,65},{2,66},{3,67},{4,68},{5,69},{6,70},{7,71},{8,72},{9,... | collective-permute-start | bytes 196616 | tf_op jit(solution)/shard_map/ppermute | solution.py:53
  64.5 21.5 %collective-permute-start.11 = (bf16[1,128,256]{2,1,0:T(8,128)(2,1)S(1)}, bf16[1,128,256]{2,1,0:T(8,128)(2,1)S(1)}, u32[]{:S(2)}, u32[]{:S(2)}) collective-permute-start(bf16[1,128,256]{2,1,0:T(8,128)(2,1)S(1)} %bitcast.360), channel_id=1, source_target_pairs={{1,64},{2,65},{3,66},{4,67},{5,68},{6,69},{7,70},{8,71},{9,72},{10... | collective-permute-start | bytes 196616 | tf_op jit(solution)/shard_map/ppermute | solution.py:53
  67.9 20.3 %collective-permute-start.12 = (bf16[1,128,256]{2,1,0:T(8,128)(2,1)S(1)}, bf16[1,128,256]{2,1,0:T(8,128)(2,1)S(1)}, u32[]{:S(2)}, u32[]{:S(2)}) collective-permute-start(bf16[1,128,256]{2,1,0:T(8,128)(2,1)S(1)} %bitcast.361), channel_id=1, source_target_pairs={{0,1},{1,2},{2,3},{3,4},{4,5},{5,6},{6,7},{7,8},{8,9},{9,10},{10,1... | collective-permute-start | bytes 196616 | tf_op jit(solution)/shard_map/ppermute | solution.py:53
  73.4 14.8 %collective-permute-start.13 = (bf16[1,128,256]{2,1,0:T(8,128)(2,1)S(1)}, bf16[1,128,256]{2,1,0:T(8,128)(2,1)S(1)}, u32[]{:S(2)}, u32[]{:S(2)}) collective-permute-start(bf16[1,128,256]{2,1,0:T(8,128)(2,1)S(1)} %bitcast.362), channel_id=1, source_target_pairs={{1,0},{2,1},{3,2},{4,3},{5,4},{6,5},{7,6},{8,7},{9,8},{10,9},{11,1... | collective-permute-start | bytes 196616 | tf_op jit(solution)/shard_map/ppermute | solution.py:53
  110.4 15.7 %collective-permute-start.25 = (bf16[1,128,256]{2,1,0:T(8,128)(2,1)S(1)}, bf16[1,128,256]{2,1,0:T(8,128)(2,1)S(1)}, u32[]{:S(2)}, u32[]{:S(2)}) collective-permute-start(bf16[1,128,256]{2,1,0:T(8,128)(2,1)S(1)} %get-tuple-element.35), channel_id=1, source_target_pairs={{0,65},{1,66},{2,67},{3,68},{4,69},{5,70},{6,71},{7,72},{8,73},{9,... | collective-permute-start | bytes 196616 | tf_op jit(solution)/shard_map/ppermute | solution.py:53
  112.5 21.0 %collective-permute-start.24 = (bf16[1,128,256]{2,1,0:T(8,128)(2,1)S(1)}, bf16[1,128,256]{2,1,0:T(8,128)(2,1)S(1)}, u32[]{:S(2)}, u32[]{:S(2)}) collective-permute-start(bf16[1,128,256]{2,1,0:T(8,128)(2,1)S(1)} %get-tuple-element.36), channel_id=1, source_target_pairs={{0,64},{1,65},{2,66},{3,67},{4,68},{5,69},{6,70},{7,71},{8,72},{9,... | collective-permute-start | bytes 196616 | tf_op jit(solution)/shard_map/ppermute | solution.py:53
  114.9 21.5 %collective-permute-start.23 = (bf16[1,128,256]{2,1,0:T(8,128)(2,1)S(1)}, bf16[1,128,256]{2,1,0:T(8,128)(2,1)S(1)}, u32[]{:S(2)}, u32[]{:S(2)}) collective-permute-start(bf16[1,128,256]{2,1,0:T(8,128)(2,1)S(1)} %get-tuple-element.37), channel_id=1, source_target_pairs={{1,64},{2,65},{3,66},{4,67},{5,68},{6,69},{7,70},{8,71},{9,72},{10... | collective-permute-start | bytes 196616 | tf_op jit(solution)/shard_map/ppermute | solution.py:53
  118.2 20.9 %collective-permute-start.22 = (bf16[1,128,256]{2,1,0:T(8,128)(2,1)S(1)}, bf16[1,128,256]{2,1,0:T(8,128)(2,1)S(1)}, u32[]{:S(2)}, u32[]{:S(2)}) collective-permute-start(bf16[1,128,256]{2,1,0:T(8,128)(2,1)S(1)} %get-tuple-element.38), channel_id=1, source_target_pairs={{0,1},{1,2},{2,3},{3,4},{4,5},{5,6},{6,7},{7,8},{8,9},{9,10},{10,1... | collective-permute-start | bytes 196616 | tf_op jit(solution)/shard_map/ppermute | solution.py:53
  123.8 15.4 %collective-permute-start.21 = (bf16[1,128,256]{2,1,0:T(8,128)(2,1)S(1)}, bf16[1,128,256]{2,1,0:T(8,128)(2,1)S(1)}, u32[]{:S(2)}, u32[]{:S(2)}) collective-permute-start(bf16[1,128,256]{2,1,0:T(8,128)(2,1)S(1)} %get-tuple-element.39), channel_id=1, source_target_pairs={{1,0},{2,1},{3,2},{4,3},{5,4},{6,5},{7,6},{8,7},{9,8},{10,9},{11,1... | collective-permute-start | bytes 196616 | tf_op jit(solution)/shard_map/ppermute | solution.py:53
  153.3 15.5 %collective-permute-start.33 = (bf16[1,128,256]{2,1,0:T(8,128)(2,1)S(1)}, bf16[1,128,256]{2,1,0:T(8,128)(2,1)S(1)}, u32[]{:S(2)}, u32[]{:S(2)}) collective-permute-start(bf16[1,128,256]{2,1,0:T(8,128)(2,1)S(1)} %get-tuple-element.27), channel_id=1, source_target_pairs={{0,65},{1,66},{2,67},{3,68},{4,69},{5,70},{6,71},{7,72},{8,73},{9,... | collective-permute-start | bytes 196616 | tf_op jit(solution)/shard_map/ppermute | solution.py:53
  155.3 20.8 %collective-permute-start.32 = (bf16[1,128,256]{2,1,0:T(8,128)(2,1)S(1)}, bf16[1,128,256]{2,1,0:T(8,128)(2,1)S(1)}, u32[]{:S(2)}, u32[]{:S(2)}) collective-permute-start(bf16[1,128,256]{2,1,0:T(8,128)(2,1)S(1)} %get-tuple-element.28), channel_id=1, source_target_pairs={{0,64},{1,65},{2,66},{3,67},{4,68},{5,69},{6,70},{7,71},{8,72},{9,... | collective-permute-start | bytes 196616 | tf_op jit(solution)/shard_map/ppermute | solution.py:53
  157.8 21.3 %collective-permute-start.31 = (bf16[1,128,256]{2,1,0:T(8,128)(2,1)S(1)}, bf16[1,128,256]{2,1,0:T(8,128)(2,1)S(1)}, u32[]{:S(2)}, u32[]{:S(2)}) collective-permute-start(bf16[1,128,256]{2,1,0:T(8,128)(2,1)S(1)} %get-tuple-element.29), channel_id=1, source_target_pairs={{1,64},{2,65},{3,66},{4,67},{5,68},{6,69},{7,70},{8,71},{9,72},{10... | collective-permute-start | bytes 196616 | tf_op jit(solution)/shard_map/ppermute | solution.py:53
  161.3 20.1 %collective-permute-start.30 = (bf16[1,128,256]{2,1,0:T(8,128)(2,1)S(1)}, bf16[1,128,256]{2,1,0:T(8,128)(2,1)S(1)}, u32[]{:S(2)}, u32[]{:S(2)}) collective-permute-start(bf16[1,128,256]{2,1,0:T(8,128)(2,1)S(1)} %get-tuple-element.30), channel_id=1, source_target_pairs={{0,1},{1,2},{2,3},{3,4},{4,5},{5,6},{6,7},{7,8},{8,9},{9,10},{10,1... | collective-permute-start | bytes 196616 | tf_op jit(solution)/shard_map/ppermute | solution.py:53
  166.8 25.9 %collective-permute-start.29 = (bf16[1,128,256]{2,1,0:T(8,128)(2,1)S(1)}, bf16[1,128,256]{2,1,0:T(8,128)(2,1)S(1)}, u32[]{:S(2)}, u32[]{:S(2)}) collective-permute-start(bf16[1,128,256]{2,1,0:T(8,128)(2,1)S(1)} %get-tuple-element.31), channel_id=1, source_target_pairs={{1,0},{2,1},{3,2},{4,3},{5,4},{6,5},{7,6},{8,7},{9,8},{10,9},{11,1... | collective-permute-start | bytes 196616 | tf_op jit(solution)/shard_map/ppermute | solution.py:53
  168.8 23.9 %collective-permute-start.28 = (bf16[1,128,256]{2,1,0:T(8,128)(2,1)S(1)}, bf16[1,128,256]{2,1,0:T(8,128)(2,1)S(1)}, u32[]{:S(2)}, u32[]{:S(2)}) collective-permute-start(bf16[1,128,256]{2,1,0:T(8,128)(2,1)S(1)} %get-tuple-element.32), channel_id=1, source_target_pairs={{64,1},{65,2},{66,3},{67,4},{68,5},{69,6},{70,7},{71,8},{72,9},{73... | collective-permute-start | bytes 196616 | tf_op jit(solution)/shard_map/ppermute | solution.py:53
  176.1 16.6 %collective-permute-start.27 = (bf16[1,128,256]{2,1,0:T(8,128)(2,1)S(1)}, bf16[1,128,256]{2,1,0:T(8,128)(2,1)S(1)}, u32[]{:S(2)}, u32[]{:S(2)}) collective-permute-start(bf16[1,128,256]{2,1,0:T(8,128)(2,1)S(1)} %get-tuple-element.33), channel_id=1, source_target_pairs={{64,0},{65,1},{66,2},{67,3},{68,4},{69,5},{70,6},{71,7},{72,8},{73... | collective-permute-start | bytes 196616 | tf_op jit(solution)/shard_map/ppermute | solution.py:53
  181.5 20.9 %collective-permute-start.17 = (bf16[448,256]{1,0:T(8,128)(2,1)S(1)}, bf16[448,256]{1,0:T(8,128)(2,1)S(1)}, u32[]{:S(2)}, u32[]{:S(2)}) collective-permute-start(bf16[448,256]{1,0:T(8,128)(2,1)S(1)} %copy-done.24), channel_id=1, source_target_pairs={{0,512},{512,0},{1,513},{513,1},{2,514},{514,2},{3,515},{515,3},{4... | collective-permute-start | bytes 688136 | tf_op jit(solution)/shard_map/ppermute | solution.py:191
  (44 other events, 645.9 us)

commit v4 on v2

--- a/solution.py
+++ b/solution.py
@@ -38,9 +38,9 @@
     return jnp.einsum("mrd,kd->mrk", left, right, preferred_element_type=jnp.float32)
 
 
-def exact_sum(form, left, right):
+def onehot_sum(form, left, right):
     return jnp.einsum(
-        form, left, right, precision=lax.Precision.HIGHEST, preferred_element_type=jnp.float32
+        form, left, right, precision=lax.Precision.HIGH, preferred_element_type=jnp.float32
     )
 
 
@@ -72,37 +72,24 @@
 
 def forward(weights, tables, node_blocks, edge_rows):
     edge_in, edge_outer, node_in, node_outer = weights
-    dst_onehot, src_onehot, block_pick = tables
+    dst_onehot, src_onehot = tables
     windows, block_nodes, width = node_blocks.shape
-    tiles, edges_tile = dst_onehot.shape[:2]
-    source_table = neighbourhood(node_blocks)
+    source_table = neighbourhood(node_blocks).reshape(windows, -1, width)
     at_dst = jnp.einsum(
-        "tkn,mnd->mtkd", dst_onehot, node_blocks, preferred_element_type=jnp.float32
-    ).astype(jnp.bfloat16)
-    src_blocks = jnp.einsum(
-        "tb,mbnd->mtnd", block_pick.astype(jnp.bfloat16), source_table,
-        preferred_element_type=jnp.float32,
+        "en,mnd->med", dst_onehot, node_blocks, preferred_element_type=jnp.float32
     ).astype(jnp.bfloat16)
     at_src = jnp.einsum(
-        "tkn,mtnd->mtkd", src_onehot, src_blocks, preferred_element_type=jnp.float32
+        "en,mnd->med", src_onehot, source_table, preferred_element_type=jnp.float32
     ).astype(jnp.bfloat16)
-    at_dst = at_dst.reshape(windows, -1, width)
-    at_src = at_src.reshape(windows, -1, width)
-    act_edge = (
-        times_plain(edge_rows, edge_in[:width])
-        + times_plain(at_dst, edge_in[width : 2 * width])
-        + times_plain(at_src, edge_in[2 * width :])
-    )
+    joined = jnp.concatenate([edge_rows, at_dst, at_src], axis=2)
+    act_edge = times_plain(joined, edge_in)
     hidden_edge = jax.nn.silu(act_edge).astype(jnp.bfloat16)
     edge_pre = times_plain(hidden_edge, edge_outer)
     message = normalize(edge_pre)[0]
     edge_new = (edge_rows.astype(jnp.float32) + message).astype(jnp.bfloat16)
-    summed = exact_sum(
-        "tkn,mtkd->mnd",
-        dst_onehot.astype(jnp.float32),
-        message.reshape(windows, tiles, edges_tile, width),
-    ).astype(jnp.bfloat16)
-    act_node = times_plain(node_blocks, node_in[:width]) + times_plain(summed, node_in[width:])
+    summed = onehot_sum("en,med->mnd", dst_onehot, message).astype(jnp.bfloat16)
+    node_joined = jnp.concatenate([node_blocks, summed], axis=2)
+    act_node = times_plain(node_joined, node_in)
     hidden_node = jax.nn.silu(act_node).astype(jnp.bfloat16)
     node_pre = times_plain(hidden_node, node_outer)
     node_new = (node_blocks.astype(jnp.float32) + normalize(node_pre)[0]).astype(jnp.bfloat16)
@@ -111,37 +98,27 @@
 
 def backward(weights, tables, kept_values, grad_node, grad_edge):
     edge_in, edge_outer, node_in, node_outer = weights
-    dst_onehot, src_onehot, block_pick = tables
+    dst_onehot, src_onehot = tables
     act_edge, edge_pre, act_node, node_pre = kept_values
     windows, block_nodes, width = grad_node.shape
-    tiles, edges_tile = dst_onehot.shape[:2]
-    dst_float = dst_onehot.astype(jnp.float32)
-    src_float = src_onehot.astype(jnp.float32)
     pre_node_grad = norm_back(node_pre, grad_node).astype(jnp.bfloat16)
     act_node_grad = (times_turned(pre_node_grad, node_outer) * silu_slope(act_node)).astype(
         jnp.bfloat16
     )
-    node_self_grad = times_turned(act_node_grad, node_in[:width])
-    summed_grad = times_turned(act_node_grad, node_in[width:])
-    message_grad = grad_edge + exact_sum("tkn,mnd->mtkd", dst_float, summed_grad).reshape(
-        windows, -1, width
-    )
+    joined_node_grad = times_turned(act_node_grad, node_in)
+    message_grad = grad_edge + onehot_sum("en,mnd->med", dst_onehot, joined_node_grad[:, :, width:])
     pre_edge_grad = norm_back(edge_pre, message_grad).astype(jnp.bfloat16)
     act_edge_grad = (times_turned(pre_edge_grad, edge_outer) * silu_slope(act_edge)).astype(
         jnp.bfloat16
     )
-    edge_self_grad = times_turned(act_edge_grad, edge_in[:width])
-    dst_side_grad = times_turned(act_edge_grad, edge_in[width : 2 * width])
-    src_side_grad = times_turned(act_edge_grad, edge_in[2 * width :])
-    edge_back = grad_edge + edge_self_grad
-    dst_sums = exact_sum(
-        "tkn,mtkd->mnd", dst_float, dst_side_grad.reshape(windows, tiles, edges_tile, width)
-    )
-    per_tile = exact_sum(
-        "tkn,mtkd->mtnd", src_float, src_side_grad.reshape(windows, tiles, edges_tile, width)
-    )
-    table_back = exact_sum("tb,mtnd->mbnd", block_pick, per_tile)
-    node_back = grad_node + node_self_grad + dst_sums + return_to_owners(table_back)
+    joined_edge_grad = times_turned(act_edge_grad, edge_in)
+    edge_back = grad_edge + joined_edge_grad[:, :, :width]
+    dst_sums = onehot_sum("en,med->mnd", dst_onehot, joined_edge_grad[:, :, width : 2 * width])
+    table_back = onehot_sum("en,med->mnd", src_onehot, joined_edge_grad[:, :, 2 * width :])
+    table_back = table_back.reshape(windows, 9, block_nodes, width)
+    node_back = (
+        grad_node + joined_node_grad[:, :, :width] + dst_sums + return_to_owners(table_back)
+    )
     return (node_back, edge_back)
 
 
@@ -162,12 +139,13 @@
     block_nodes = node_latents.shape[3]
     width = node_latents.shape[4]
     tile_codes = tile_offsets[0, 0]
-    node_iota = lax.broadcasted_iota(jnp.int32, edge_dst[0, 0].shape + (block_nodes,), 2)
-    dst_onehot = (edge_dst[0, 0][..., None] == node_iota).astype(jnp.bfloat16)
-    src_onehot = (edge_src[0, 0][..., None] == node_iota).astype(jnp.bfloat16)
-    block_iota = lax.broadcasted_iota(jnp.int32, tile_codes.shape + (9,), 1)
-    block_pick = (tile_codes[..., None] == block_iota).astype(jnp.float32)
-    tables = (dst_onehot, src_onehot, block_pick)
+    tiles, edges_tile = edge_dst.shape[2:]
+    node_iota = lax.broadcasted_iota(jnp.int32, (tiles * edges_tile, block_nodes), 1)
+    dst_onehot = (edge_dst.reshape(-1, 1) == node_iota).astype(jnp.bfloat16)
+    source_key = (tile_codes[:, None] * block_nodes + edge_src[0, 0]).reshape(-1, 1)
+    table_iota = lax.broadcasted_iota(jnp.int32, (tiles * edges_tile, 9 * block_nodes), 1)
+    src_onehot = (source_key == table_iota).astype(jnp.bfloat16)
+    tables = (dst_onehot, src_onehot)
     is_first = lax.axis_index("phase") == 0
     own = jnp.concatenate([edge_in_w[0], edge_out_w[0], node_in_w[0], node_out_w[0]], axis=0)
     other = lax.ppermute(own, "phase", [(0, 1), (1, 0)])

time: 141 us -> 128 us (0.908)
  the two profiles are of different devices: /device:TPU:431 before, /device:TPU:593 now
where the time goes in v4:
time: 128 us; the launch traced here: 127 us
  starting transfers between devices  62 us (48%)
  waiting for transfers between devices  33 us (26%)
  matrix products  12 us (9%)
  other arithmetic  11.5 us (9%)
  local copies, waits for them, and re-layouts  6.62 us (5%)
  between operations  1.59 us (1%)
    ppermute x16, starting transfers between devices, shifted(): return lax.ppermute(array, axis, pairs)  46.7 us
    ppermute x16, waiting for transfers between devices, shifted(): return lax.ppermute(array, axis, pairs)  33 us
    ppermute x1, starting transfers between devices, body(): grad_recv = lax.ppermute(grad_send, 'phase', [(0, 1), (1, 0)])  6.43 us
    ppermute x1, starting transfers between devices, body(): latent_recv = lax.ppermute(latent_send, 'phase', [(0, 1), (1, 0)])  5.75 us
    dot_general x8, matrix products, onehot_sum(): jnp.einsum(form, left, right, precision=lax.Precision.HIGH, preferred_ele...  4.58 us
    dot_general x4, matrix products, times_turned(): jnp.einsum('mrd,kd->mrk', left, right, preferred_element_type=jnp.float32)  3.92 us
    unnamed x62, local copies, waits for them, and re-layouts  3.71 us
    ppermute x1, starting transfers between devices, body(): other = lax.ppermute(own, 'phase', [(0, 1), (1, 0)])  3.14 us
  transfers between devices with their start and end apart: 19, of which 12 were waited for; matrix products, arithmetic and copies ran while one was open for 9% of the time, Pallas kernels for 0%

profile of v4, /device:TPU:593, one launch (start us, length us, event | category | flops | bytes accessed | tf_op | source)
XLA Modules:
  0.0 126.8 jit_solution(5986096953890215372)
XLA Ops:
  1.7 2.7 %collective-permute-start.1 = (bf16[1,128,256]{2,1,0:T(8,128)(2,1)S(1)}, bf16[1,128,256]{2,1,0:T(8,128)(2,1)S(1)}, u32[]{:S(2)}, u32[]{:S(2)}) collective-permute-start(bf16[1,128,256]{2,1,0:T(8,128)(2,1)S(1)} %fusion.206), channel_id=1, source_target_pairs={{1,0},{2,1},{3,2},{4,3},{5,4},{6,5},{7,6},{8,7},{9,8},{10,9},{11,1... | collective-permute-start | bytes 196616 | tf_op jit(solution)/shard_map/ppermute | solution.py:10
  4.3 2.6 %collective-permute-start = (bf16[1,128,256]{2,1,0:T(8,128)(2,1)S(1)}, bf16[1,128,256]{2,1,0:T(8,128)(2,1)S(1)}, u32[]{:S(2)}, u32[]{:S(2)}) collective-permute-start(bf16[1,128,256]{2,1,0:T(8,128)(2,1)S(1)} %fusion.206), channel_id=1, source_target_pairs={{0,1},{1,2},{2,3},{3,4},{4,5},{5,6},{6,7},{7,8},{8,9},{9,10},{10,1... | collective-permute-start | bytes 196616 | tf_op jit(solution)/shard_map/ppermute | solution.py:10
  8.3 3.1 %collective-permute-start.4 = (bf16[1792,256]{1,0:T(8,128)(2,1)S(1)}, bf16[1792,256]{1,0:T(8,128)(2,1)}, u32[]{:S(2)}, u32[]{:S(2)}) collective-permute-start(bf16[1792,256]{1,0:T(8,128)(2,1)S(1)} %pad_maximum_fusion), channel_id=1, source_target_pairs={{0,512},{512,0},{1,513},{513,1},{2,514},{514,2},{3,515},{515,3},{4... | collective-permute-start | bytes 2752520 | tf_op jit(solution)/shard_map/ppermute | solution.py:151
  12.7 2.9 %collective-permute-start.3 = (bf16[1,3,128,256]{3,2,1,0:T(8,128)(2,1)S(1)}, bf16[1,3,128,256]{3,2,1,0:T(8,128)(2,1)S(1)}, u32[]{:S(2)}, u32[]{:S(2)}) collective-permute-start(bf16[1,3,128,256]{3,2,1,0:T(8,128)(2,1)S(1)} %get-tuple-element.38), channel_id=1, source_target_pairs={{64,0},{128,64},{192,128},{256,192},{320,256},{384,320},{448,384},... | collective-permute-start | bytes 589832 | tf_op jit(solution)/shard_map/ppermute | solution.py:10
  15.6 2.4 %collective-permute-start.2 = (bf16[1,3,128,256]{3,2,1,0:T(8,128)(2,1)S(1)}, bf16[1,3,128,256]{3,2,1,0:T(8,128)(2,1)S(1)}, u32[]{:S(2)}, u32[]{:S(2)}) collective-permute-start(bf16[1,3,128,256]{3,2,1,0:T(8,128)(2,1)S(1)} %get-tuple-element.38), channel_id=1, source_target_pairs={{0,64},{64,128},{128,192},{192,256},{256,320},{320,384},{384,448},... | collective-permute-start | bytes 589832 | tf_op jit(solution)/shard_map/ppermute | solution.py:10
  19.1 2.9 %collective-permute-done.2 = bf16[1,3,128,256]{3,2,1,0:T(8,128)(2,1)S(1)} collective-permute-done((bf16[1,3,128,256]{3,2,1,0:T(8,128)(2,1)S(1)}, bf16[1,3,128,256]{3,2,1,0:T(8,128)(2,1)S(1)}, u32[]{:S(2)}, u32[]{:S(2)}) %collective-permute-start.2) | collective-permute-done | bytes 196640 | tf_op jit(solution)/shard_map/ppermute | solution.py:10
  27.5 7.3 %collective-permute-start.6 = (bf16[1,128,256]{2,1,0:T(8,128)(2,1)S(1)}, bf16[1,128,256]{2,1,0:T(8,128)(2,1)S(1)}, u32[]{:S(2)}, u32[]{:S(2)}) collective-permute-start(bf16[1,128,256]{2,1,0:T(8,128)(2,1)S(1)} %bitcast.286), channel_id=1, source_target_pairs={{1,0},{2,1},{3,2},{4,3},{5,4},{6,5},{7,6},{8,7},{9,8},{10,9},{11,1... | collective-permute-start | bytes 196616 | tf_op jit(solution)/shard_map/ppermute | solution.py:10
  37.0 6.1 %collective-permute-done.5 = bf16[1,128,256]{2,1,0:T(8,128)(2,1)S(1)} collective-permute-done((bf16[1,128,256]{2,1,0:T(8,128)(2,1)S(1)}, bf16[1,128,256]{2,1,0:T(8,128)(2,1)S(1)}, u32[]{:S(2)}, u32[]{:S(2)}) %collective-permute-start.5) | collective-permute-done | bytes 65568 | tf_op jit(solution)/shard_map/ppermute | solution.py:10
  43.2 3.2 %collective-permute-start.8 = (bf16[1,3,128,256]{3,2,1,0:T(8,128)(2,1)S(1)}, bf16[1,3,128,256]{3,2,1,0:T(8,128)(2,1)S(1)}, u32[]{:S(2)}, u32[]{:S(2)}) collective-permute-start(bf16[1,3,128,256]{3,2,1,0:T(8,128)(2,1)S(1)} %get-tuple-element.36), channel_id=1, source_target_pairs={{64,0},{128,64},{192,128},{256,192},{320,256},{384,320},{448,384},... | collective-permute-start | bytes 589832 | tf_op jit(solution)/shard_map/ppermute | solution.py:10
  46.4 2.1 %collective-permute-start.7 = (bf16[1,3,128,256]{3,2,1,0:T(8,128)(2,1)S(1)}, bf16[1,3,128,256]{3,2,1,0:T(8,128)(2,1)S(1)}, u32[]{:S(2)}, u32[]{:S(2)}) collective-permute-start(bf16[1,3,128,256]{3,2,1,0:T(8,128)(2,1)S(1)} %get-tuple-element.36), channel_id=1, source_target_pairs={{0,64},{64,128},{128,192},{192,256},{256,320},{320,384},{384,448},... | collective-permute-start | bytes 589832 | tf_op jit(solution)/shard_map/ppermute | solution.py:10
  49.6 3.3 %collective-permute-done.7 = bf16[1,3,128,256]{3,2,1,0:T(8,128)(2,1)S(1)} collective-permute-done((bf16[1,3,128,256]{3,2,1,0:T(8,128)(2,1)S(1)}, bf16[1,3,128,256]{3,2,1,0:T(8,128)(2,1)S(1)}, u32[]{:S(2)}, u32[]{:S(2)}) %collective-permute-start.7) | collective-permute-done | bytes 196640 | tf_op jit(solution)/shard_map/ppermute | solution.py:10
  58.0 5.8 %collective-permute-start.9 = (bf16[448,256]{1,0:T(8,128)(2,1)}, bf16[448,256]{1,0:T(8,128)(2,1)}, u32[]{:S(2)}, u32[]{:S(2)}) collective-permute-start(bf16[448,256]{1,0:T(8,128)(2,1)} %maximum_select_fusion.4), channel_id=1, source_target_pairs={{0,512},{512,0},{1,513},{513,1},{2,514},{514,2},{3,515},{515,3},{4... | collective-permute-start | bytes 688136 | tf_op jit(solution)/shard_map/ppermute | solution.py:169
  68.9 3.0 %collective-permute-start.10 = (bf16[1,3,128,256]{3,2,1,0:T(8,128)(2,1)S(1)}, bf16[1,3,128,256]{3,2,1,0:T(8,128)(2,1)S(1)}, u32[]{:S(2)}, u32[]{:S(2)}) collective-permute-start(bf16[1,3,128,256]{3,2,1,0:T(8,128)(2,1)S(1)} %get-tuple-element.29), channel_id=1, source_target_pairs={{64,0},{128,64},{192,128},{256,192},{320,256},{384,320},{448,384},... | collective-permute-start | bytes 589832 | tf_op jit(solution)/shard_map/ppermute | solution.py:10
  71.9 2.4 %collective-permute-start.11 = (bf16[1,3,128,256]{3,2,1,0:T(8,128)(2,1)S(1)}, bf16[1,3,128,256]{3,2,1,0:T(8,128)(2,1)S(1)}, u32[]{:S(2)}, u32[]{:S(2)}) collective-permute-start(bf16[1,3,128,256]{3,2,1,0:T(8,128)(2,1)S(1)} %get-tuple-element.30), channel_id=1, source_target_pairs={{0,64},{64,128},{128,192},{192,256},{256,320},{320,384},{384,448},... | collective-permute-start | bytes 589832 | tf_op jit(solution)/shard_map/ppermute | solution.py:10
  74.4 3.0 %collective-permute-done.10 = bf16[1,3,128,256]{3,2,1,0:T(8,128)(2,1)S(1)} collective-permute-done((bf16[1,3,128,256]{3,2,1,0:T(8,128)(2,1)S(1)}, bf16[1,3,128,256]{3,2,1,0:T(8,128)(2,1)S(1)}, u32[]{:S(2)}, u32[]{:S(2)}) %collective-permute-start.10) | collective-permute-done | bytes 196640 | tf_op jit(solution)/shard_map/ppermute | solution.py:10
  77.5 2.5 %collective-permute-done.11 = bf16[1,3,128,256]{3,2,1,0:T(8,128)(2,1)S(1)} collective-permute-done((bf16[1,3,128,256]{3,2,1,0:T(8,128)(2,1)S(1)}, bf16[1,3,128,256]{3,2,1,0:T(8,128)(2,1)S(1)}, u32[]{:S(2)}, u32[]{:S(2)}) %collective-permute-start.11) | collective-permute-done | bytes 196640 | tf_op jit(solution)/shard_map/ppermute | solution.py:10
  80.1 2.1 %collective-permute-start.12 = (bf16[1,128,256]{2,1,0:T(8,128)(2,1)S(1)}, bf16[1,128,256]{2,1,0:T(8,128)(2,1)S(1)}, u32[]{:S(2)}, u32[]{:S(2)}) collective-permute-start(bf16[1,128,256]{2,1,0:T(8,128)(2,1)S(1)} %get-tuple-element.33), channel_id=1, source_target_pairs={{1,0},{2,1},{3,2},{4,3},{5,4},{6,5},{7,6},{8,7},{9,8},{10,9},{11,1... | collective-permute-start | bytes 196616 | tf_op jit(solution)/shard_map/ppermute | solution.py:10
  82.2 3.4 %collective-permute-start.13 = (bf16[1,128,256]{2,1,0:T(8,128)(2,1)S(1)}, bf16[1,128,256]{2,1,0:T(8,128)(2,1)S(1)}, u32[]{:S(2)}, u32[]{:S(2)}) collective-permute-start(bf16[1,128,256]{2,1,0:T(8,128)(2,1)S(1)} %get-tuple-element.34), channel_id=1, source_target_pairs={{0,1},{1,2},{2,3},{3,4},{4,5},{5,6},{6,7},{7,8},{8,9},{9,10},{10,1... | collective-permute-start | bytes 196616 | tf_op jit(solution)/shard_map/ppermute | solution.py:10
  86.9 3.6 %collective-permute-done.13 = bf16[1,128,256]{2,1,0:T(8,128)(2,1)S(1)} collective-permute-done((bf16[1,128,256]{2,1,0:T(8,128)(2,1)S(1)}, bf16[1,128,256]{2,1,0:T(8,128)(2,1)S(1)}, u32[]{:S(2)}, u32[]{:S(2)}) %collective-permute-start.13) | collective-permute-done | bytes 65568 | tf_op jit(solution)/shard_map/ppermute | solution.py:10
  95.9 3.6 %collective-permute-start.14 = (bf16[1,3,128,256]{3,2,1,0:T(8,128)(2,1)S(1)}, bf16[1,3,128,256]{3,2,1,0:T(8,128)(2,1)S(1)}, u32[]{:S(2)}, u32[]{:S(2)}) collective-permute-start(bf16[1,3,128,256]{3,2,1,0:T(8,128)(2,1)S(1)} %get-tuple-element.27), channel_id=1, source_target_pairs={{64,0},{128,64},{192,128},{256,192},{320,256},{384,320},{448,384},... | collective-permute-start | bytes 589832 | tf_op jit(solution)/shard_map/ppermute | solution.py:10
  102.4 3.5 %collective-permute-done.15 = bf16[1,3,128,256]{3,2,1,0:T(8,128)(2,1)S(1)} collective-permute-done((bf16[1,3,128,256]{3,2,1,0:T(8,128)(2,1)S(1)}, bf16[1,3,128,256]{3,2,1,0:T(8,128)(2,1)S(1)}, u32[]{:S(2)}, u32[]{:S(2)}) %collective-permute-start.15) | collective-permute-done | bytes 196640 | tf_op jit(solution)/shard_map/ppermute | solution.py:10
  107.9 3.4 %collective-permute-start.17 = (bf16[1,128,256]{2,1,0:T(8,128)(2,1)S(1)}, bf16[1,128,256]{2,1,0:T(8,128)(2,1)S(1)}, u32[]{:S(2)}, u32[]{:S(2)}) collective-permute-start(bf16[1,128,256]{2,1,0:T(8,128)(2,1)S(1)} %get-tuple-element.32), channel_id=1, source_target_pairs={{0,1},{1,2},{2,3},{3,4},{4,5},{5,6},{6,7},{7,8},{8,9},{9,10},{10,1... | collective-permute-start | bytes 196616 | tf_op jit(solution)/shard_map/ppermute | solution.py:10
  111.7 4.6 %collective-permute-done.17 = bf16[1,128,256]{2,1,0:T(8,128)(2,1)S(1)} collective-permute-done((bf16[1,128,256]{2,1,0:T(8,128)(2,1)S(1)}, bf16[1,128,256]{2,1,0:T(8,128)(2,1)S(1)}, u32[]{:S(2)}, u32[]{:S(2)}) %collective-permute-start.17) | collective-permute-done | bytes 65568 | tf_op jit(solution)/shard_map/ppermute | solution.py:10
  116.4 6.4 %collective-permute-start.18 = (f32[448,256]{1,0:T(8,128)S(1)}, f32[448,256]{1,0:T(8,128)S(1)}, u32[]{:S(2)}, u32[]{:S(2)}) collective-permute-start(f32[448,256]{1,0:T(8,128)S(1)} %maximum_select_fusion.1), channel_id=1, source_target_pairs={{0,512},{512,0},{1,513},{513,1},{2,514},{514,2},{3,515},{515,3},{4... | collective-permute-start | bytes 1376264 | tf_op jit(solution)/shard_map/ppermute | solution.py:185
  (167 shorter events, 39.3 us)
Async XLA Ops:
  1.7 10.6 %collective-permute-start.1 = (bf16[1,128,256]{2,1,0:T(8,128)(2,1)S(1)}, bf16[1,128,256]{2,1,0:T(8,128)(2,1)S(1)}, u32[]{:S(2)}, u32[]{:S(2)}) collective-permute-start(bf16[1,128,256]{2,1,0:T(8,128)(2,1)S(1)} %fusion.206), channel_id=1, source_target_pairs={{1,0},{2,1},{3,2},{4,3},{5,4},{6,5},{7,6},{8,7},{9,8},{10,9},{11,1... | collective-permute-start | bytes 196616 | tf_op jit(solution)/shard_map/ppermute | solution.py:10
  4.3 8.3 %collective-permute-start = (bf16[1,128,256]{2,1,0:T(8,128)(2,1)S(1)}, bf16[1,128,256]{2,1,0:T(8,128)(2,1)S(1)}, u32[]{:S(2)}, u32[]{:S(2)}) collective-permute-start(bf16[1,128,256]{2,1,0:T(8,128)(2,1)S(1)} %fusion.206), channel_id=1, source_target_pairs={{0,1},{1,2},{2,3},{3,4},{4,5},{5,6},{6,7},{7,8},{8,9},{9,10},{10,1... | collective-permute-start | bytes 196616 | tf_op jit(solution)/shard_map/ppermute | solution.py:10
  8.3 14.2 %collective-permute-start.4 = (bf16[1792,256]{1,0:T(8,128)(2,1)S(1)}, bf16[1792,256]{1,0:T(8,128)(2,1)}, u32[]{:S(2)}, u32[]{:S(2)}) collective-permute-start(bf16[1792,256]{1,0:T(8,128)(2,1)S(1)} %pad_maximum_fusion), channel_id=1, source_target_pairs={{0,512},{512,0},{1,513},{513,1},{2,514},{514,2},{3,515},{515,3},{4... | collective-permute-start | bytes 2752520 | tf_op jit(solution)/shard_map/ppermute | solution.py:151
  12.7 6.4 %collective-permute-start.3 = (bf16[1,3,128,256]{3,2,1,0:T(8,128)(2,1)S(1)}, bf16[1,3,128,256]{3,2,1,0:T(8,128)(2,1)S(1)}, u32[]{:S(2)}, u32[]{:S(2)}) collective-permute-start(bf16[1,3,128,256]{3,2,1,0:T(8,128)(2,1)S(1)} %get-tuple-element.38), channel_id=1, source_target_pairs={{64,0},{128,64},{192,128},{256,192},{320,256},{384,320},{448,384},... | collective-permute-start | bytes 589832 | tf_op jit(solution)/shard_map/ppermute | solution.py:10
  15.6 6.4 %collective-permute-start.2 = (bf16[1,3,128,256]{3,2,1,0:T(8,128)(2,1)S(1)}, bf16[1,3,128,256]{3,2,1,0:T(8,128)(2,1)S(1)}, u32[]{:S(2)}, u32[]{:S(2)}) collective-permute-start(bf16[1,3,128,256]{3,2,1,0:T(8,128)(2,1)S(1)} %get-tuple-element.38), channel_id=1, source_target_pairs={{0,64},{64,128},{128,192},{192,256},{256,320},{320,384},{384,448},... | collective-permute-start | bytes 589832 | tf_op jit(solution)/shard_map/ppermute | solution.py:10
  26.5 16.7 %copy-start.27 = (f32[128,256]{1,0:T(8,128)}, f32[128,256]{1,0:T(8,128)S(1)}, u32[]{:S(2)}) copy-start(f32[128,256]{1,0:T(8,128)S(1)} %fusion.59) | copy-start | bytes 393220
  27.5 9.5 %collective-permute-start.6 = (bf16[1,128,256]{2,1,0:T(8,128)(2,1)S(1)}, bf16[1,128,256]{2,1,0:T(8,128)(2,1)S(1)}, u32[]{:S(2)}, u32[]{:S(2)}) collective-permute-start(bf16[1,128,256]{2,1,0:T(8,128)(2,1)S(1)} %bitcast.286), channel_id=1, source_target_pairs={{1,0},{2,1},{3,2},{4,3},{5,4},{6,5},{7,6},{8,7},{9,8},{10,9},{11,1... | collective-permute-start | bytes 196616 | tf_op jit(solution)/shard_map/ppermute | solution.py:10
  34.8 8.3 %collective-permute-start.5 = (bf16[1,128,256]{2,1,0:T(8,128)(2,1)S(1)}, bf16[1,128,256]{2,1,0:T(8,128)(2,1)S(1)}, u32[]{:S(2)}, u32[]{:S(2)}) collective-permute-start(bf16[1,128,256]{2,1,0:T(8,128)(2,1)S(1)} %bitcast.287), channel_id=1, source_target_pairs={{0,1},{1,2},{2,3},{3,4},{4,5},{5,6},{6,7},{7,8},{8,9},{9,10},{10,1... | collective-permute-start | bytes 196616 | tf_op jit(solution)/shard_map/ppermute | solution.py:10
  43.2 6.4 %collective-permute-start.8 = (bf16[1,3,128,256]{3,2,1,0:T(8,128)(2,1)S(1)}, bf16[1,3,128,256]{3,2,1,0:T(8,128)(2,1)S(1)}, u32[]{:S(2)}, u32[]{:S(2)}) collective-permute-start(bf16[1,3,128,256]{3,2,1,0:T(8,128)(2,1)S(1)} %get-tuple-element.36), channel_id=1, source_target_pairs={{64,0},{128,64},{192,128},{256,192},{320,256},{384,320},{448,384},... | collective-permute-start | bytes 589832 | tf_op jit(solution)/shard_map/ppermute | solution.py:10
  46.4 6.5 %collective-permute-start.7 = (bf16[1,3,128,256]{3,2,1,0:T(8,128)(2,1)S(1)}, bf16[1,3,128,256]{3,2,1,0:T(8,128)(2,1)S(1)}, u32[]{:S(2)}, u32[]{:S(2)}) collective-permute-start(bf16[1,3,128,256]{3,2,1,0:T(8,128)(2,1)S(1)} %get-tuple-element.36), channel_id=1, source_target_pairs={{0,64},{64,128},{128,192},{192,256},{256,320},{320,384},{384,448},... | collective-permute-start | bytes 589832 | tf_op jit(solution)/shard_map/ppermute | solution.py:10
  58.0 27.9 %collective-permute-start.9 = (bf16[448,256]{1,0:T(8,128)(2,1)}, bf16[448,256]{1,0:T(8,128)(2,1)}, u32[]{:S(2)}, u32[]{:S(2)}) collective-permute-start(bf16[448,256]{1,0:T(8,128)(2,1)} %maximum_select_fusion.4), channel_id=1, source_target_pairs={{0,512},{512,0},{1,513},{513,1},{2,514},{514,2},{3,515},{515,3},{4... | collective-permute-start | bytes 688136 | tf_op jit(solution)/shard_map/ppermute | solution.py:169
  68.9 8.6 %collective-permute-start.10 = (bf16[1,3,128,256]{3,2,1,0:T(8,128)(2,1)S(1)}, bf16[1,3,128,256]{3,2,1,0:T(8,128)(2,1)S(1)}, u32[]{:S(2)}, u32[]{:S(2)}) collective-permute-start(bf16[1,3,128,256]{3,2,1,0:T(8,128)(2,1)S(1)} %get-tuple-element.29), channel_id=1, source_target_pairs={{64,0},{128,64},{192,128},{256,192},{320,256},{384,320},{448,384},... | collective-permute-start | bytes 589832 | tf_op jit(solution)/shard_map/ppermute | solution.py:10
  71.9 8.1 %collective-permute-start.11 = (bf16[1,3,128,256]{3,2,1,0:T(8,128)(2,1)S(1)}, bf16[1,3,128,256]{3,2,1,0:T(8,128)(2,1)S(1)}, u32[]{:S(2)}, u32[]{:S(2)}) collective-permute-start(bf16[1,3,128,256]{3,2,1,0:T(8,128)(2,1)S(1)} %get-tuple-element.30), channel_id=1, source_target_pairs={{0,64},{64,128},{128,192},{192,256},{256,320},{320,384},{384,448},... | collective-permute-start | bytes 589832 | tf_op jit(solution)/shard_map/ppermute | solution.py:10
  74.4 16.1 %copy-start.18 = (f32[1,128,512]{2,1,0:T(8,128)S(1)}, f32[1,128,512]{2,1,0:T(8,128)}, u32[]{:S(2)}) copy-start(f32[1,128,512]{2,1,0:T(8,128)} %copy-done.17) | copy-start | bytes 786436
  74.4 16.1 %copy-start.21 = (f32[128]{0:T(128)S(1)}, f32[128]{0:T(128)}, u32[]{:S(2)}) copy-start(f32[128]{0:T(128)} %copy-done.20) | copy-start | bytes 1540
  74.4 16.1 %copy-start.25 = (f32[128]{0:T(128)S(1)}, f32[128]{0:T(128)}, u32[]{:S(2)}) copy-start(f32[128]{0:T(128)} %copy-done.24) | copy-start | bytes 1540
  80.1 6.7 %collective-permute-start.12 = (bf16[1,128,256]{2,1,0:T(8,128)(2,1)S(1)}, bf16[1,128,256]{2,1,0:T(8,128)(2,1)S(1)}, u32[]{:S(2)}, u32[]{:S(2)}) collective-permute-start(bf16[1,128,256]{2,1,0:T(8,128)(2,1)S(1)} %get-tuple-element.33), channel_id=1, source_target_pairs={{1,0},{2,1},{3,2},{4,3},{5,4},{6,5},{7,6},{8,7},{9,8},{10,9},{11,1... | collective-permute-start | bytes 196616 | tf_op jit(solution)/shard_map/ppermute | solution.py:10
  82.2 8.3 %collective-permute-start.13 = (bf16[1,128,256]{2,1,0:T(8,128)(2,1)S(1)}, bf16[1,128,256]{2,1,0:T(8,128)(2,1)S(1)}, u32[]{:S(2)}, u32[]{:S(2)}) collective-permute-start(bf16[1,128,256]{2,1,0:T(8,128)(2,1)S(1)} %get-tuple-element.34), channel_id=1, source_target_pairs={{0,1},{1,2},{2,3},{3,4},{4,5},{5,6},{6,7},{7,8},{8,9},{9,10},{10,1... | collective-permute-start | bytes 196616 | tf_op jit(solution)/shard_map/ppermute | solution.py:10
  95.9 6.5 %collective-permute-start.14 = (bf16[1,3,128,256]{3,2,1,0:T(8,128)(2,1)S(1)}, bf16[1,3,128,256]{3,2,1,0:T(8,128)(2,1)S(1)}, u32[]{:S(2)}, u32[]{:S(2)}) collective-permute-start(bf16[1,3,128,256]{3,2,1,0:T(8,128)(2,1)S(1)} %get-tuple-element.27), channel_id=1, source_target_pairs={{64,0},{128,64},{192,128},{256,192},{320,256},{384,320},{448,384},... | collective-permute-start | bytes 589832 | tf_op jit(solution)/shard_map/ppermute | solution.py:10
  99.5 6.4 %collective-permute-start.15 = (bf16[1,3,128,256]{3,2,1,0:T(8,128)(2,1)S(1)}, bf16[1,3,128,256]{3,2,1,0:T(8,128)(2,1)S(1)}, u32[]{:S(2)}, u32[]{:S(2)}) collective-permute-start(bf16[1,3,128,256]{3,2,1,0:T(8,128)(2,1)S(1)} %get-tuple-element.28), channel_id=1, source_target_pairs={{0,64},{64,128},{128,192},{192,256},{256,320},{320,384},{384,448},... | collective-permute-start | bytes 589832 | tf_op jit(solution)/shard_map/ppermute | solution.py:10
  101.5 14.8 %copy-start.15 = (f32[1,128,512]{2,1,0:T(8,128)S(1)}, f32[1,128,512]{2,1,0:T(8,128)}, u32[]{:S(2)}) copy-start(f32[1,128,512]{2,1,0:T(8,128)} %copy-done.14) | copy-start | bytes 786436
  106.0 5.7 %collective-permute-start.16 = (bf16[1,128,256]{2,1,0:T(8,128)(2,1)S(1)}, bf16[1,128,256]{2,1,0:T(8,128)(2,1)S(1)}, u32[]{:S(2)}, u32[]{:S(2)}) collective-permute-start(bf16[1,128,256]{2,1,0:T(8,128)(2,1)S(1)} %get-tuple-element.31), channel_id=1, source_target_pairs={{1,0},{2,1},{3,2},{4,3},{5,4},{6,5},{7,6},{8,7},{9,8},{10,9},{11,1... | collective-permute-start | bytes 196616 | tf_op jit(solution)/shard_map/ppermute | solution.py:10
  107.9 8.3 %collective-permute-start.17 = (bf16[1,128,256]{2,1,0:T(8,128)(2,1)S(1)}, bf16[1,128,256]{2,1,0:T(8,128)(2,1)S(1)}, u32[]{:S(2)}, u32[]{:S(2)}) collective-permute-start(bf16[1,128,256]{2,1,0:T(8,128)(2,1)S(1)} %get-tuple-element.32), channel_id=1, source_target_pairs={{0,1},{1,2},{2,3},{3,4},{4,5},{5,6},{6,7},{7,8},{8,9},{9,10},{10,1... | collective-permute-start | bytes 196616 | tf_op jit(solution)/shard_map/ppermute | solution.py:10
  116.4 8.7 %collective-permute-start.18 = (f32[448,256]{1,0:T(8,128)S(1)}, f32[448,256]{1,0:T(8,128)S(1)}, u32[]{:S(2)}, u32[]{:S(2)}) collective-permute-start(f32[448,256]{1,0:T(8,128)S(1)} %maximum_select_fusion.1), channel_id=1, source_target_pairs={{0,512},{512,0},{1,513},{513,1},{2,514},{514,2},{3,515},{515,3},{4... | collective-permute-start | bytes 1376264 | tf_op jit(solution)/shard_map/ppermute | solution.py:185
  (26 other events, 125.2 us)

commit v5 on v4

--- a/solution.py
+++ b/solution.py
@@ -39,9 +39,13 @@
 
 
 def onehot_sum(form, left, right):
-    return jnp.einsum(
-        form, left, right, precision=lax.Precision.HIGH, preferred_element_type=jnp.float32
-    )
+    high = right.astype(jnp.bfloat16)
+    low = (right - high.astype(jnp.float32)).astype(jnp.bfloat16)
+    both = jnp.einsum(
+        form, left, jnp.concatenate([high, low], axis=-1), preferred_element_type=jnp.float32
+    )
+    width = right.shape[-1]
+    return both[..., :width] + both[..., width:]
 
 
 def neighbourhood(node_blocks):
@@ -155,7 +159,7 @@
         tuple(packed[cuts[i] : cuts[i + 1]] for i in range(4)) for packed in sections
     ]
     def mine(array):
-        return jnp.where(is_first, array[0], array[1])[None]
+        return lax.dynamic_slice_in_dim(array, lax.axis_index("phase"), 1, axis=0)
 
     node_zero = mine(node_latents).reshape(1, block_nodes, width)
     edge_zero = mine(edge_latents).reshape(1, -1, width)
@@ -185,11 +189,9 @@
     grad_recv = lax.ppermute(grad_send, "phase", [(0, 1), (1, 0)])
 
     def placed(own_first, own_second, received, shape):
-        kept = jnp.where(is_first, own_first, own_second)
-        pair = jnp.where(
-            is_first, jnp.stack([kept, received]), jnp.stack([received, kept])
-        )
-        return pair.reshape(shape)
+        first = jnp.where(is_first, own_first, received)
+        second = jnp.where(is_first, received, own_second)
+        return jnp.stack([first, second]).reshape(shape)
 
     node_shape = (1,) + node_latents.shape
     edge_shape = (1,) + edge_latents.shape

time: 128 us -> 126 us (0.984)
  the two profiles are of different devices: /device:TPU:593 before, /device:TPU:625 now
where the time goes in v5:
time: 126 us
  starting transfers between devices  57.9 us (46%)
  waiting for transfers between devices  31.3 us (25%)
  other arithmetic  15.4 us (12%)
  matrix products  14.5 us (12%)
  local copies, waits for them, and re-layouts  4.63 us (4%)
  between operations  1.85 us (1%)
    ppermute x16, starting transfers between devices, shifted(): return lax.ppermute(array, axis, pairs)  40 us
    ppermute x16, waiting for transfers between devices, shifted(): return lax.ppermute(array, axis, pairs)  31.3 us
    ppermute x1, starting transfers between devices, body(): grad_recv = lax.ppermute(grad_send, 'phase', [(0, 1), (1, 0)])  8.08 us
    ppermute x1, starting transfers between devices, body(): latent_recv = lax.ppermute(latent_send, 'phase', [(0, 1), (1, 0)])  7.21 us
    dot_general x4, matrix products, times_turned(): jnp.einsum('mrd,kd->mrk', left, right, preferred_element_type=jnp.float32)  5.34 us
    dot_general x8, matrix products, onehot_sum(): jnp.einsum(form, left, jnp.concatenate([high, low], axis=-1), preferred_e...  3.89 us
    ppermute x1, starting transfers between devices, body(): other = lax.ppermute(own, 'phase', [(0, 1), (1, 0)])  2.58 us
  transfers between devices with their start and end apart: 19, of which 9 were waited for; matrix products, arithmetic and copies ran while one was open for 13% of the time, Pallas kernels for 0%

profile of v5, /device:TPU:625, one launch (start us, length us, event | category | flops | bytes accessed | tf_op | source)
XLA Modules:
  0.0 125.6 jit_solution(46271651628583525)
XLA Ops:
  2.1 2.6 %collective-permute-start.4 = (bf16[1792,256]{1,0:T(8,128)(2,1)S(1)}, bf16[1792,256]{1,0:T(8,128)(2,1)S(1)}, u32[]{:S(2)}, u32[]{:S(2)}) collective-permute-start(bf16[1792,256]{1,0:T(8,128)(2,1)S(1)} %pad_maximum_fusion), channel_id=1, source_target_pairs={{0,512},{512,0},{1,513},{513,1},{2,514},{514,2},{3,515},{515,3},{4... | collective-permute-start | bytes 2752520 | tf_op jit(solution)/shard_map/ppermute | solution.py:155
  4.8 2.7 %collective-permute-start.1 = (bf16[1,128,256]{1,2,0:T(8,128)(2,1)S(1)}, bf16[1,128,256]{1,2,0:T(8,128)(2,1)S(1)}, u32[]{:S(2)}, u32[]{:S(2)}) collective-permute-start(bf16[1,128,256]{1,2,0:T(8,128)(2,1)S(1)} %bitcast.321), channel_id=1, source_target_pairs={{1,0},{2,1},{3,2},{4,3},{5,4},{6,5},{7,6},{8,7},{9,8},{10,9},{11,1... | collective-permute-start | bytes 196616 | tf_op jit(solution)/shard_map/ppermute | solution.py:10
  7.5 2.6 %collective-permute-start = (bf16[1,128,256]{1,2,0:T(8,128)(2,1)S(1)}, bf16[1,128,256]{1,2,0:T(8,128)(2,1)S(1)}, u32[]{:S(2)}, u32[]{:S(2)}) collective-permute-start(bf16[1,128,256]{1,2,0:T(8,128)(2,1)S(1)} %bitcast.322), channel_id=1, source_target_pairs={{0,1},{1,2},{2,3},{3,4},{4,5},{5,6},{6,7},{7,8},{8,9},{9,10},{10,1... | collective-permute-start | bytes 196616 | tf_op jit(solution)/shard_map/ppermute | solution.py:10
  11.2 4.7 %collective-permute-done = bf16[1,128,256]{1,2,0:T(8,128)(2,1)S(1)} collective-permute-done((bf16[1,128,256]{1,2,0:T(8,128)(2,1)S(1)}, bf16[1,128,256]{1,2,0:T(8,128)(2,1)S(1)}, u32[]{:S(2)}, u32[]{:S(2)}) %collective-permute-start) | collective-permute-done | bytes 65568 | tf_op jit(solution)/shard_map/ppermute | solution.py:10
  15.9 2.9 %collective-permute-start.3 = (bf16[1,3,128,256]{2,3,1,0:T(8,128)(2,1)S(1)}, bf16[1,3,128,256]{2,3,1,0:T(8,128)(2,1)S(1)}, u32[]{:S(2)}, u32[]{:S(2)}) collective-permute-start(bf16[1,3,128,256]{2,3,1,0:T(8,128)(2,1)S(1)} %get-tuple-element.70), channel_id=1, source_target_pairs={{64,0},{128,64},{192,128},{256,192},{320,256},{384,320},{448,384},... | collective-permute-start | bytes 589832 | tf_op jit(solution)/shard_map/ppermute | solution.py:10
  21.7 3.5 %collective-permute-done.2 = bf16[1,3,128,256]{2,3,1,0:T(8,128)(2,1)S(1)} collective-permute-done((bf16[1,3,128,256]{2,3,1,0:T(8,128)(2,1)S(1)}, bf16[1,3,128,256]{2,3,1,0:T(8,128)(2,1)S(1)}, u32[]{:S(2)}, u32[]{:S(2)}) %collective-permute-start.2) | collective-permute-done | bytes 196640 | tf_op jit(solution)/shard_map/ppermute | solution.py:10
  32.2 2.0 %collective-permute-start.6 = (bf16[1,128,256]{2,1,0:T(8,128)(2,1)S(1)}, bf16[1,128,256]{2,1,0:T(8,128)(2,1)S(1)}, u32[]{:S(2)}, u32[]{:S(2)}) collective-permute-start(bf16[1,128,256]{2,1,0:T(8,128)(2,1)S(1)} %bitcast.305), channel_id=1, source_target_pairs={{1,0},{2,1},{3,2},{4,3},{5,4},{6,5},{7,6},{8,7},{9,8},{10,9},{11,1... | collective-permute-start | bytes 196616 | tf_op jit(solution)/shard_map/ppermute | solution.py:10
  34.3 3.2 %collective-permute-start.5 = (bf16[1,128,256]{2,1,0:T(8,128)(2,1)S(1)}, bf16[1,128,256]{2,1,0:T(8,128)(2,1)S(1)}, u32[]{:S(2)}, u32[]{:S(2)}) collective-permute-start(bf16[1,128,256]{2,1,0:T(8,128)(2,1)S(1)} %bitcast.306), channel_id=1, source_target_pairs={{0,1},{1,2},{2,3},{3,4},{4,5},{5,6},{6,7},{7,8},{8,9},{9,10},{10,1... | collective-permute-start | bytes 196616 | tf_op jit(solution)/shard_map/ppermute | solution.py:10
  37.6 5.0 %collective-permute-done.5 = bf16[1,128,256]{2,1,0:T(8,128)(2,1)S(1)} collective-permute-done((bf16[1,128,256]{2,1,0:T(8,128)(2,1)S(1)}, bf16[1,128,256]{2,1,0:T(8,128)(2,1)S(1)}, u32[]{:S(2)}, u32[]{:S(2)}) %collective-permute-start.5) | collective-permute-done | bytes 65568 | tf_op jit(solution)/shard_map/ppermute | solution.py:10
  42.6 2.9 %collective-permute-start.8 = (bf16[1,3,128,256]{3,2,1,0:T(8,128)(2,1)S(1)}, bf16[1,3,128,256]{3,2,1,0:T(8,128)(2,1)S(1)}, u32[]{:S(2)}, u32[]{:S(2)}) collective-permute-start(bf16[1,3,128,256]{3,2,1,0:T(8,128)(2,1)S(1)} %get-tuple-element.68), channel_id=1, source_target_pairs={{64,0},{128,64},{192,128},{256,192},{320,256},{384,320},{448,384},... | collective-permute-start | bytes 589832 | tf_op jit(solution)/shard_map/ppermute | solution.py:10
  48.1 3.8 %collective-permute-done.7 = bf16[1,3,128,256]{3,2,1,0:T(8,128)(2,1)S(1)} collective-permute-done((bf16[1,3,128,256]{3,2,1,0:T(8,128)(2,1)S(1)}, bf16[1,3,128,256]{3,2,1,0:T(8,128)(2,1)S(1)}, u32[]{:S(2)}, u32[]{:S(2)}) %collective-permute-start.7) | collective-permute-done | bytes 196640 | tf_op jit(solution)/shard_map/ppermute | solution.py:10
  57.8 1.7 %convolution_bitcast_fusion.3 = f32[1,320,768]{2,1,0:T(8,128)S(1)} fusion(bf16[1792,256]{1,0:T(8,128)(2,1)} %copy-done.14, f32[320,256]{1,0:T(8,128)S(1)} %fusion.21, f32[320,256]{1,0:T(8,128)S(1)} %get-tuple-element.78, f32[1,320,256]{2,1,0:T(8,128)S(1)} %convert_add_fusion.1, f32[320]{0:T(512)S(1)} %get-tuple-element.81, f32[320]{0:T(512)S(1)} %get-tuple-element.82, ...), kind=kOutput, calls=%fused_computation.6 | convolution fusion | flops 169082880 | bytes 2500608 | tf_op jit(solution)/shard_map/mrd,kd->mrk/dot_general | solution.py:38
  62.2 3.3 %collective-permute-start.10 = (bf16[1,3,128,256]{3,2,1,0:T(8,128)(2,1)S(1)}, bf16[1,3,128,256]{3,2,1,0:T(8,128)(2,1)S(1)}, u32[]{:S(2)}, u32[]{:S(2)}) collective-permute-start(bf16[1,3,128,256]{3,2,1,0:T(8,128)(2,1)S(1)} %get-tuple-element.47), channel_id=1, source_target_pairs={{64,0},{128,64},{192,128},{256,192},{320,256},{384,320},{448,384},... | collective-permute-start | bytes 589832 | tf_op jit(solution)/shard_map/ppermute | solution.py:10
  67.6 7.2 %collective-permute-start.9 = (bf16[448,256]{1,0:T(8,128)(2,1)}, bf16[448,256]{1,0:T(8,128)(2,1)}, u32[]{:S(2)}, u32[]{:S(2)}) collective-permute-start(bf16[448,256]{1,0:T(8,128)(2,1)} %maximum_select_fusion.1), channel_id=1, source_target_pairs={{0,512},{512,0},{1,513},{513,1},{2,514},{514,2},{3,515},{515,3},{4... | collective-permute-start | bytes 688136 | tf_op jit(solution)/shard_map/ppermute | solution.py:173
  74.9 1.9 %collective-permute-start.12 = (bf16[1,128,256]{2,1,0:T(8,128)(2,1)S(1)}, bf16[1,128,256]{2,1,0:T(8,128)(2,1)S(1)}, u32[]{:S(2)}, u32[]{:S(2)}) collective-permute-start(bf16[1,128,256]{2,1,0:T(8,128)(2,1)S(1)} %get-tuple-element.65), channel_id=1, source_target_pairs={{1,0},{2,1},{3,2},{4,3},{5,4},{6,5},{7,6},{8,7},{9,8},{10,9},{11,1... | collective-permute-start | bytes 196616 | tf_op jit(solution)/shard_map/ppermute | solution.py:10
  76.8 3.5 %collective-permute-start.13 = (bf16[1,128,256]{2,1,0:T(8,128)(2,1)S(1)}, bf16[1,128,256]{2,1,0:T(8,128)(2,1)S(1)}, u32[]{:S(2)}, u32[]{:S(2)}) collective-permute-start(bf16[1,128,256]{2,1,0:T(8,128)(2,1)S(1)} %get-tuple-element.66), channel_id=1, source_target_pairs={{0,1},{1,2},{2,3},{3,4},{4,5},{5,6},{6,7},{7,8},{8,9},{9,10},{10,1... | collective-permute-start | bytes 196616 | tf_op jit(solution)/shard_map/ppermute | solution.py:10
  80.8 4.4 %collective-permute-done.13 = bf16[1,128,256]{2,1,0:T(8,128)(2,1)S(1)} collective-permute-done((bf16[1,128,256]{2,1,0:T(8,128)(2,1)S(1)}, bf16[1,128,256]{2,1,0:T(8,128)(2,1)S(1)}, u32[]{:S(2)}, u32[]{:S(2)}) %collective-permute-start.13) | collective-permute-done | bytes 65568 | tf_op jit(solution)/shard_map/ppermute | solution.py:10
  87.7 1.8 %convolution_bitcast_fusion.2 = f32[1,320,768]{2,1,0:T(8,128)S(1)} fusion(bf16[1792,256]{1,0:T(8,128)(2,1)} %copy-done.10, f32[320,256]{1,0:T(8,128)} %copy-done.42, f32[320,256]{1,0:T(8,128)S(1)} %get-tuple-element.74, f32[1,320,256]{2,1,0:T(8,128)S(1)} %fusion.35, f32[320]{0:T(512)S(1)} %broadcast_multiply_fusion, f32[320]{0:T(512)S(1)} %broadcast_multiply_fusion.1, ...), kind=kOutput, calls=%fused_computation.5 | convolution fusion | flops 169082880 | bytes 2500608 | tf_op jit(solution)/shard_map/mrd,kd->mrk/dot_general | solution.py:38
  92.0 4.4 %collective-permute-start.14 = (bf16[1,3,128,256]{3,2,1,0:T(8,128)(2,1)S(1)}, bf16[1,3,128,256]{3,2,1,0:T(8,128)(2,1)S(1)}, u32[]{:S(2)}, u32[]{:S(2)}) collective-permute-start(bf16[1,3,128,256]{3,2,1,0:T(8,128)(2,1)S(1)} %get-tuple-element.45), channel_id=1, source_target_pairs={{64,0},{128,64},{192,128},{256,192},{320,256},{384,320},{448,384},... | collective-permute-start | bytes 589832 | tf_op jit(solution)/shard_map/ppermute | solution.py:10
  99.0 3.8 %collective-permute-done.15 = bf16[1,3,128,256]{3,2,1,0:T(8,128)(2,1)S(1)} collective-permute-done((bf16[1,3,128,256]{3,2,1,0:T(8,128)(2,1)S(1)}, bf16[1,3,128,256]{3,2,1,0:T(8,128)(2,1)S(1)}, u32[]{:S(2)}, u32[]{:S(2)}) %collective-permute-start.15) | collective-permute-done | bytes 196640 | tf_op jit(solution)/shard_map/ppermute | solution.py:10
  102.9 2.1 %collective-permute-start.16 = (bf16[1,128,256]{2,1,0:T(8,128)(2,1)S(1)}, bf16[1,128,256]{2,1,0:T(8,128)(2,1)S(1)}, u32[]{:S(2)}, u32[]{:S(2)}) collective-permute-start(bf16[1,128,256]{2,1,0:T(8,128)(2,1)S(1)} %get-tuple-element.63), channel_id=1, source_target_pairs={{1,0},{2,1},{3,2},{4,3},{5,4},{6,5},{7,6},{8,7},{9,8},{10,9},{11,1... | collective-permute-start | bytes 196616 | tf_op jit(solution)/shard_map/ppermute | solution.py:10
  105.0 3.4 %collective-permute-start.17 = (bf16[1,128,256]{2,1,0:T(8,128)(2,1)S(1)}, bf16[1,128,256]{2,1,0:T(8,128)(2,1)S(1)}, u32[]{:S(2)}, u32[]{:S(2)}) collective-permute-start(bf16[1,128,256]{2,1,0:T(8,128)(2,1)S(1)} %get-tuple-element.64), channel_id=1, source_target_pairs={{0,1},{1,2},{2,3},{3,4},{4,5},{5,6},{6,7},{7,8},{8,9},{9,10},{10,1... | collective-permute-start | bytes 196616 | tf_op jit(solution)/shard_map/ppermute | solution.py:10
  108.7 4.6 %collective-permute-done.17 = bf16[1,128,256]{2,1,0:T(8,128)(2,1)S(1)} collective-permute-done((bf16[1,128,256]{2,1,0:T(8,128)(2,1)S(1)}, bf16[1,128,256]{2,1,0:T(8,128)(2,1)S(1)}, u32[]{:S(2)}, u32[]{:S(2)}) %collective-permute-start.17) | collective-permute-done | bytes 65568 | tf_op jit(solution)/shard_map/ppermute | solution.py:10
  113.4 8.1 %collective-permute-start.18 = (f32[448,256]{1,0:T(8,128)S(1)}, f32[448,256]{1,0:T(8,128)S(1)}, u32[]{:S(2)}, u32[]{:S(2)}) collective-permute-start(f32[448,256]{1,0:T(8,128)S(1)} %maximum_select_fusion), channel_id=1, source_target_pairs={{0,512},{512,0},{1,513},{513,1},{2,514},{514,2},{3,515},{515,3},{4... | collective-permute-start | bytes 1376264 | tf_op jit(solution)/shard_map/ppermute | solution.py:189
  (201 shorter events, 37.7 us)
Async XLA Ops:
  2.1 25.8 %collective-permute-start.4 = (bf16[1792,256]{1,0:T(8,128)(2,1)S(1)}, bf16[1792,256]{1,0:T(8,128)(2,1)S(1)}, u32[]{:S(2)}, u32[]{:S(2)}) collective-permute-start(bf16[1792,256]{1,0:T(8,128)(2,1)S(1)} %pad_maximum_fusion), channel_id=1, source_target_pairs={{0,512},{512,0},{1,513},{513,1},{2,514},{514,2},{3,515},{515,3},{4... | collective-permute-start | bytes 2752520 | tf_op jit(solution)/shard_map/ppermute | solution.py:155
  4.8 6.3 %collective-permute-start.1 = (bf16[1,128,256]{1,2,0:T(8,128)(2,1)S(1)}, bf16[1,128,256]{1,2,0:T(8,128)(2,1)S(1)}, u32[]{:S(2)}, u32[]{:S(2)}) collective-permute-start(bf16[1,128,256]{1,2,0:T(8,128)(2,1)S(1)} %bitcast.321), channel_id=1, source_target_pairs={{1,0},{2,1},{3,2},{4,3},{5,4},{6,5},{7,6},{8,7},{9,8},{10,9},{11,1... | collective-permute-start | bytes 196616 | tf_op jit(solution)/shard_map/ppermute | solution.py:10
  7.5 8.3 %collective-permute-start = (bf16[1,128,256]{1,2,0:T(8,128)(2,1)S(1)}, bf16[1,128,256]{1,2,0:T(8,128)(2,1)S(1)}, u32[]{:S(2)}, u32[]{:S(2)}) collective-permute-start(bf16[1,128,256]{1,2,0:T(8,128)(2,1)S(1)} %bitcast.322), channel_id=1, source_target_pairs={{0,1},{1,2},{2,3},{3,4},{4,5},{5,6},{6,7},{7,8},{8,9},{9,10},{10,1... | collective-permute-start | bytes 196616 | tf_op jit(solution)/shard_map/ppermute | solution.py:10
  15.9 5.8 %collective-permute-start.3 = (bf16[1,3,128,256]{2,3,1,0:T(8,128)(2,1)S(1)}, bf16[1,3,128,256]{2,3,1,0:T(8,128)(2,1)S(1)}, u32[]{:S(2)}, u32[]{:S(2)}) collective-permute-start(bf16[1,3,128,256]{2,3,1,0:T(8,128)(2,1)S(1)} %get-tuple-element.70), channel_id=1, source_target_pairs={{64,0},{128,64},{192,128},{256,192},{320,256},{384,320},{448,384},... | collective-permute-start | bytes 589832 | tf_op jit(solution)/shard_map/ppermute | solution.py:10
  18.8 6.4 %collective-permute-start.2 = (bf16[1,3,128,256]{2,3,1,0:T(8,128)(2,1)S(1)}, bf16[1,3,128,256]{2,3,1,0:T(8,128)(2,1)S(1)}, u32[]{:S(2)}, u32[]{:S(2)}) collective-permute-start(bf16[1,3,128,256]{2,3,1,0:T(8,128)(2,1)S(1)} %get-tuple-element.70), channel_id=1, source_target_pairs={{0,64},{64,128},{128,192},{192,256},{256,320},{320,384},{384,448},... | collective-permute-start | bytes 589832 | tf_op jit(solution)/shard_map/ppermute | solution.py:10
  29.3 26.7 %copy-start.14 = (bf16[1792,256]{1,0:T(8,128)(2,1)}, bf16[1792,256]{1,0:T(8,128)(2,1)S(1)}, u32[]{:S(2)}) copy-start(bf16[1792,256]{1,0:T(8,128)(2,1)S(1)} %get-tuple-element.35) | copy-start | bytes 2752516
  30.8 36.0 %copy-start.3 = (bf16[320,256]{1,0:T(8,128)(2,1)}, bf16[320,256]{1,0:T(8,128)(2,1)S(1)}, u32[]{:S(2)}) copy-start(bf16[320,256]{1,0:T(8,128)(2,1)S(1)} %get-tuple-element.56) | copy-start | bytes 491524
  32.2 34.6 %copy-start.5 = (bf16[128,256]{1,0:T(8,128)(2,1)}, bf16[128,256]{1,0:T(8,128)(2,1)S(1)}, u32[]{:S(2)}) copy-start(bf16[128,256]{1,0:T(8,128)(2,1)S(1)} %add_convert_fusion.2) | copy-start | bytes 196612
  32.2 5.3 %collective-permute-start.6 = (bf16[1,128,256]{2,1,0:T(8,128)(2,1)S(1)}, bf16[1,128,256]{2,1,0:T(8,128)(2,1)S(1)}, u32[]{:S(2)}, u32[]{:S(2)}) collective-permute-start(bf16[1,128,256]{2,1,0:T(8,128)(2,1)S(1)} %bitcast.305), channel_id=1, source_target_pairs={{1,0},{2,1},{3,2},{4,3},{5,4},{6,5},{7,6},{8,7},{9,8},{10,9},{11,1... | collective-permute-start | bytes 196616 | tf_op jit(solution)/shard_map/ppermute | solution.py:10
  34.3 8.3 %collective-permute-start.5 = (bf16[1,128,256]{2,1,0:T(8,128)(2,1)S(1)}, bf16[1,128,256]{2,1,0:T(8,128)(2,1)S(1)}, u32[]{:S(2)}, u32[]{:S(2)}) collective-permute-start(bf16[1,128,256]{2,1,0:T(8,128)(2,1)S(1)} %bitcast.306), channel_id=1, source_target_pairs={{0,1},{1,2},{2,3},{3,4},{4,5},{5,6},{6,7},{7,8},{8,9},{9,10},{10,1... | collective-permute-start | bytes 196616 | tf_op jit(solution)/shard_map/ppermute | solution.py:10
  42.6 5.5 %collective-permute-start.8 = (bf16[1,3,128,256]{3,2,1,0:T(8,128)(2,1)S(1)}, bf16[1,3,128,256]{3,2,1,0:T(8,128)(2,1)S(1)}, u32[]{:S(2)}, u32[]{:S(2)}) collective-permute-start(bf16[1,3,128,256]{3,2,1,0:T(8,128)(2,1)S(1)} %get-tuple-element.68), channel_id=1, source_target_pairs={{64,0},{128,64},{192,128},{256,192},{320,256},{384,320},{448,384},... | collective-permute-start | bytes 589832 | tf_op jit(solution)/shard_map/ppermute | solution.py:10
  45.5 6.4 %collective-permute-start.7 = (bf16[1,3,128,256]{3,2,1,0:T(8,128)(2,1)S(1)}, bf16[1,3,128,256]{3,2,1,0:T(8,128)(2,1)S(1)}, u32[]{:S(2)}, u32[]{:S(2)}) collective-permute-start(bf16[1,3,128,256]{3,2,1,0:T(8,128)(2,1)S(1)} %get-tuple-element.68), channel_id=1, source_target_pairs={{0,64},{64,128},{128,192},{192,256},{256,320},{320,384},{384,448},... | collective-permute-start | bytes 589832 | tf_op jit(solution)/shard_map/ppermute | solution.py:10
  62.1 23.1 %copy-start.21 = (f32[1,128,512]{2,1,0:T(8,128)S(1)}, f32[1,128,512]{2,1,0:T(8,128)}, u32[]{:S(2)}) copy-start(f32[1,128,512]{2,1,0:T(8,128)} %copy-done.20) | copy-start | bytes 786436
  62.1 23.1 %copy-start.24 = (bf16[2,1,1,128,256]{4,3,2,1,0:T(8,128)(2,1)S(1)}, bf16[2,1,1,128,256]{4,3,2,1,0:T(8,128)(2,1)}, u32[]{:S(2)}) copy-start(bf16[2,1,1,128,256]{4,3,2,1,0:T(8,128)(2,1)} %param.20) | copy-start | bytes 393220
  62.2 12.6 %collective-permute-start.10 = (bf16[1,3,128,256]{3,2,1,0:T(8,128)(2,1)S(1)}, bf16[1,3,128,256]{3,2,1,0:T(8,128)(2,1)S(1)}, u32[]{:S(2)}, u32[]{:S(2)}) collective-permute-start(bf16[1,3,128,256]{3,2,1,0:T(8,128)(2,1)S(1)} %get-tuple-element.47), channel_id=1, source_target_pairs={{64,0},{128,64},{192,128},{256,192},{320,256},{384,320},{448,384},... | collective-permute-start | bytes 589832 | tf_op jit(solution)/shard_map/ppermute | solution.py:10
  65.5 9.3 %collective-permute-start.11 = (bf16[1,3,128,256]{3,2,1,0:T(8,128)(2,1)S(1)}, bf16[1,3,128,256]{3,2,1,0:T(8,128)(2,1)S(1)}, u32[]{:S(2)}, u32[]{:S(2)}) collective-permute-start(bf16[1,3,128,256]{3,2,1,0:T(8,128)(2,1)S(1)} %get-tuple-element.48), channel_id=1, source_target_pairs={{0,64},{64,128},{128,192},{192,256},{256,320},{320,384},{384,448},... | collective-permute-start | bytes 589832 | tf_op jit(solution)/shard_map/ppermute | solution.py:10
  67.6 30.1 %collective-permute-start.9 = (bf16[448,256]{1,0:T(8,128)(2,1)}, bf16[448,256]{1,0:T(8,128)(2,1)}, u32[]{:S(2)}, u32[]{:S(2)}) collective-permute-start(bf16[448,256]{1,0:T(8,128)(2,1)} %maximum_select_fusion.1), channel_id=1, source_target_pairs={{0,512},{512,0},{1,513},{513,1},{2,514},{514,2},{3,515},{515,3},{4... | collective-permute-start | bytes 688136 | tf_op jit(solution)/shard_map/ppermute | solution.py:173
  74.9 5.9 %collective-permute-start.12 = (bf16[1,128,256]{2,1,0:T(8,128)(2,1)S(1)}, bf16[1,128,256]{2,1,0:T(8,128)(2,1)S(1)}, u32[]{:S(2)}, u32[]{:S(2)}) collective-permute-start(bf16[1,128,256]{2,1,0:T(8,128)(2,1)S(1)} %get-tuple-element.65), channel_id=1, source_target_pairs={{1,0},{2,1},{3,2},{4,3},{5,4},{6,5},{7,6},{8,7},{9,8},{10,9},{11,1... | collective-permute-start | bytes 196616 | tf_op jit(solution)/shard_map/ppermute | solution.py:10
  76.8 8.3 %collective-permute-start.13 = (bf16[1,128,256]{2,1,0:T(8,128)(2,1)S(1)}, bf16[1,128,256]{2,1,0:T(8,128)(2,1)S(1)}, u32[]{:S(2)}, u32[]{:S(2)}) collective-permute-start(bf16[1,128,256]{2,1,0:T(8,128)(2,1)S(1)} %get-tuple-element.66), channel_id=1, source_target_pairs={{0,1},{1,2},{2,3},{3,4},{4,5},{5,6},{6,7},{7,8},{8,9},{9,10},{10,1... | collective-permute-start | bytes 196616 | tf_op jit(solution)/shard_map/ppermute | solution.py:10
  92.0 7.0 %collective-permute-start.14 = (bf16[1,3,128,256]{3,2,1,0:T(8,128)(2,1)S(1)}, bf16[1,3,128,256]{3,2,1,0:T(8,128)(2,1)S(1)}, u32[]{:S(2)}, u32[]{:S(2)}) collective-permute-start(bf16[1,3,128,256]{3,2,1,0:T(8,128)(2,1)S(1)} %get-tuple-element.45), channel_id=1, source_target_pairs={{64,0},{128,64},{192,128},{256,192},{320,256},{384,320},{448,384},... | collective-permute-start | bytes 589832 | tf_op jit(solution)/shard_map/ppermute | solution.py:10
  96.4 6.4 %collective-permute-start.15 = (bf16[1,3,128,256]{3,2,1,0:T(8,128)(2,1)S(1)}, bf16[1,3,128,256]{3,2,1,0:T(8,128)(2,1)S(1)}, u32[]{:S(2)}, u32[]{:S(2)}) collective-permute-start(bf16[1,3,128,256]{3,2,1,0:T(8,128)(2,1)S(1)} %get-tuple-element.46), channel_id=1, source_target_pairs={{0,64},{64,128},{128,192},{192,256},{256,320},{320,384},{384,448},... | collective-permute-start | bytes 589832 | tf_op jit(solution)/shard_map/ppermute | solution.py:10
  102.9 5.8 %collective-permute-start.16 = (bf16[1,128,256]{2,1,0:T(8,128)(2,1)S(1)}, bf16[1,128,256]{2,1,0:T(8,128)(2,1)S(1)}, u32[]{:S(2)}, u32[]{:S(2)}) collective-permute-start(bf16[1,128,256]{2,1,0:T(8,128)(2,1)S(1)} %get-tuple-element.63), channel_id=1, source_target_pairs={{1,0},{2,1},{3,2},{4,3},{5,4},{6,5},{7,6},{8,7},{9,8},{10,9},{11,1... | collective-permute-start | bytes 196616 | tf_op jit(solution)/shard_map/ppermute | solution.py:10
  105.0 8.3 %collective-permute-start.17 = (bf16[1,128,256]{2,1,0:T(8,128)(2,1)S(1)}, bf16[1,128,256]{2,1,0:T(8,128)(2,1)S(1)}, u32[]{:S(2)}, u32[]{:S(2)}) collective-permute-start(bf16[1,128,256]{2,1,0:T(8,128)(2,1)S(1)} %get-tuple-element.64), channel_id=1, source_target_pairs={{0,1},{1,2},{2,3},{3,4},{4,5},{5,6},{6,7},{7,8},{8,9},{9,10},{10,1... | collective-permute-start | bytes 196616 | tf_op jit(solution)/shard_map/ppermute | solution.py:10
  113.4 10.5 %collective-permute-start.18 = (f32[448,256]{1,0:T(8,128)S(1)}, f32[448,256]{1,0:T(8,128)S(1)}, u32[]{:S(2)}, u32[]{:S(2)}) collective-permute-start(f32[448,256]{1,0:T(8,128)S(1)} %maximum_select_fusion), channel_id=1, source_target_pairs={{0,512},{512,0},{1,513},{513,1},{2,514},{514,2},{3,515},{515,3},{4... | collective-permute-start | bytes 1376264 | tf_op jit(solution)/shard_map/ppermute | solution.py:189
  (38 other events, 371.9 us)

commit v6 on v5

--- a/solution.py
+++ b/solution.py
@@ -39,13 +39,9 @@
 
 
 def onehot_sum(form, left, right):
-    high = right.astype(jnp.bfloat16)
-    low = (right - high.astype(jnp.float32)).astype(jnp.bfloat16)
-    both = jnp.einsum(
-        form, left, jnp.concatenate([high, low], axis=-1), preferred_element_type=jnp.float32
-    )
-    width = right.shape[-1]
-    return both[..., :width] + both[..., width:]
+    return jnp.einsum(
+        form, left, right, precision=lax.Precision.HIGH, preferred_element_type=jnp.float32
+    )
 
 
 def neighbourhood(node_blocks):
@@ -82,11 +78,11 @@
     at_dst = jnp.einsum(
         "en,mnd->med", dst_onehot, node_blocks, preferred_element_type=jnp.float32
     ).astype(jnp.bfloat16)
+    local_part = times_plain(jnp.concatenate([edge_rows, at_dst], axis=2), edge_in[: 2 * width])
     at_src = jnp.einsum(
         "en,mnd->med", src_onehot, source_table, preferred_element_type=jnp.float32
     ).astype(jnp.bfloat16)
-    joined = jnp.concatenate([edge_rows, at_dst, at_src], axis=2)
-    act_edge = times_plain(joined, edge_in)
+    act_edge = local_part + times_plain(at_src, edge_in[2 * width :])
     hidden_edge = jax.nn.silu(act_edge).astype(jnp.bfloat16)
     edge_pre = times_plain(hidden_edge, edge_outer)
     message = normalize(edge_pre)[0]

time: 126 us -> 134 us (1.063)
  the two profiles are of different devices: /device:TPU:625 before, /device:TPU:431 now
where the time goes in v6:
time: 134 us; the launch traced here: 133 us
  starting transfers between devices  73.4 us (55%)
  waiting for transfers between devices  23.7 us (18%)
  matrix products  19.9 us (15%)
  other arithmetic  10.1 us (8%)
  local copies, waits for them, and re-layouts  4.35 us (3%)
  between operations  1.54 us (1%)
    ppermute x16, starting transfers between devices, shifted(): return lax.ppermute(array, axis, pairs)  57.2 us
    ppermute x16, waiting for transfers between devices, shifted(): return lax.ppermute(array, axis, pairs)  23.7 us
    dot_general x8, matrix products, onehot_sum(): jnp.einsum(form, left, right, precision=lax.Precision.HIGH, preferred_ele...  9.13 us
    ppermute x1, starting transfers between devices, body(): grad_recv = lax.ppermute(grad_send, 'phase', [(0, 1), (1, 0)])  7.63 us
    dot_general x4, matrix products, times_turned(): jnp.einsum('mrd,kd->mrk', left, right, preferred_element_type=jnp.float32)  5.63 us
    ppermute x1, starting transfers between devices, body(): latent_recv = lax.ppermute(latent_send, 'phase', [(0, 1), (1, 0)])  5.41 us
    dot_general x10, matrix products, times_plain(): jnp.einsum('mrk,kd->mrd', left, right, preferred_element_type=jnp.float32)  4.66 us
    ppermute x1, starting transfers between devices, body(): other = lax.ppermute(own, 'phase', [(0, 1), (1, 0)])  3.14 us
  transfers between devices with their start and end apart: 19, of which 8 were waited for; matrix products, arithmetic and copies ran while one was open for 6% of the time, Pallas kernels for 0%

profile of v6, /device:TPU:431, one launch (start us, length us, event | category | flops | bytes accessed | tf_op | source)
XLA Modules:
  0.0 133.0 jit_solution(12802539416096256060)
XLA Ops:
  1.7 3.1 %collective-permute-start.2 = (bf16[1,128,256]{1,2,0:T(8,128)(2,1)S(1)}, bf16[1,128,256]{1,2,0:T(8,128)(2,1)S(1)}, u32[]{:S(2)}, u32[]{:S(2)}) collective-permute-start(bf16[1,128,256]{1,2,0:T(8,128)(2,1)S(1)} %bitcast.323), channel_id=1, source_target_pairs={{1,0},{2,1},{3,2},{4,3},{5,4},{6,5},{7,6},{8,7},{9,8},{10,9},{11,1... | collective-permute-start | bytes 196616 | tf_op jit(solution)/shard_map/ppermute | solution.py:10
  4.8 5.5 %collective-permute-start.1 = (bf16[1,128,256]{1,2,0:T(8,128)(2,1)S(1)}, bf16[1,128,256]{1,2,0:T(8,128)(2,1)S(1)}, u32[]{:S(2)}, u32[]{:S(2)}) collective-permute-start(bf16[1,128,256]{1,2,0:T(8,128)(2,1)S(1)} %bitcast.324), channel_id=1, source_target_pairs={{0,1},{1,2},{2,3},{3,4},{4,5},{5,6},{6,7},{7,8},{8,9},{9,10},{10,1... | collective-permute-start | bytes 196616 | tf_op jit(solution)/shard_map/ppermute | solution.py:10
  11.6 3.1 %collective-permute-start = (bf16[1792,256]{1,0:T(8,128)(2,1)S(1)}, bf16[1792,256]{1,0:T(8,128)(2,1)}, u32[]{:S(2)}, u32[]{:S(2)}) collective-permute-start(bf16[1792,256]{1,0:T(8,128)(2,1)S(1)} %pad_maximum_fusion), channel_id=1, source_target_pairs={{0,512},{512,0},{1,513},{513,1},{2,514},{514,2},{3,515},{515,3},{4... | collective-permute-start | bytes 2752520 | tf_op jit(solution)/shard_map/ppermute | solution.py:151
  15.6 2.0 %collective-permute-start.4 = (bf16[1,3,128,256]{2,3,1,0:T(8,128)(2,1)S(1)}, bf16[1,3,128,256]{2,3,1,0:T(8,128)(2,1)S(1)}, u32[]{:S(2)}, u32[]{:S(2)}) collective-permute-start(bf16[1,3,128,256]{2,3,1,0:T(8,128)(2,1)S(1)} %get-tuple-element.46), channel_id=1, source_target_pairs={{64,0},{128,64},{192,128},{256,192},{320,256},{384,320},{448,384},... | collective-permute-start | bytes 589832 | tf_op jit(solution)/shard_map/ppermute | solution.py:10
  17.6 3.3 %collective-permute-start.3 = (bf16[1,3,128,256]{2,3,1,0:T(8,128)(2,1)S(1)}, bf16[1,3,128,256]{2,3,1,0:T(8,128)(2,1)S(1)}, u32[]{:S(2)}, u32[]{:S(2)}) collective-permute-start(bf16[1,3,128,256]{2,3,1,0:T(8,128)(2,1)S(1)} %get-tuple-element.46), channel_id=1, source_target_pairs={{0,64},{64,128},{128,192},{192,256},{256,320},{320,384},{384,448},... | collective-permute-start | bytes 589832 | tf_op jit(solution)/shard_map/ppermute | solution.py:10
  20.9 3.1 %collective-permute-done.4 = bf16[1,3,128,256]{2,3,1,0:T(8,128)(2,1)S(1)} collective-permute-done((bf16[1,3,128,256]{2,3,1,0:T(8,128)(2,1)S(1)}, bf16[1,3,128,256]{2,3,1,0:T(8,128)(2,1)S(1)}, u32[]{:S(2)}, u32[]{:S(2)}) %collective-permute-start.4) | collective-permute-done | bytes 196640 | tf_op jit(solution)/shard_map/ppermute | solution.py:10
  28.4 2.0 %fusion.12 = f32[320,256]{1,0:T(8,128)S(1)} fusion(bf16[1152,256]{1,0:T(8,128)(2,1)} %bitcast.321, s32[320]{0:T(512)S(1)} %add.175, bf16[1792,256]{1,0:T(8,128)(2,1)S(1)} %get-tuple-element.24), kind=kOutput, calls=%fused_computation.27 | convolution fusion | flops 231137280 | bytes 1050624 | tf_op jit(solution)/shard_map/mrk,kd->mrd/dot_general | solution.py:34
  32.7 1.9 %collective-permute-start.6 = (bf16[1,128,256]{2,1,0:T(8,128)(2,1)S(1)}, bf16[1,128,256]{2,1,0:T(8,128)(2,1)S(1)}, u32[]{:S(2)}, u32[]{:S(2)}) collective-permute-start(bf16[1,128,256]{2,1,0:T(8,128)(2,1)S(1)} %bitcast.307), channel_id=1, source_target_pairs={{1,0},{2,1},{3,2},{4,3},{5,4},{6,5},{7,6},{8,7},{9,8},{10,9},{11,1... | collective-permute-start | bytes 196616 | tf_op jit(solution)/shard_map/ppermute | solution.py:10
  34.6 6.7 %collective-permute-start.5 = (bf16[1,128,256]{2,1,0:T(8,128)(2,1)S(1)}, bf16[1,128,256]{2,1,0:T(8,128)(2,1)S(1)}, u32[]{:S(2)}, u32[]{:S(2)}) collective-permute-start(bf16[1,128,256]{2,1,0:T(8,128)(2,1)S(1)} %bitcast.308), channel_id=1, source_target_pairs={{0,1},{1,2},{2,3},{3,4},{4,5},{5,6},{6,7},{7,8},{8,9},{9,10},{10,1... | collective-permute-start | bytes 196616 | tf_op jit(solution)/shard_map/ppermute | solution.py:10
  42.7 2.0 %collective-permute-start.8 = (bf16[1,3,128,256]{3,2,1,0:T(8,128)(2,1)S(1)}, bf16[1,3,128,256]{3,2,1,0:T(8,128)(2,1)S(1)}, u32[]{:S(2)}, u32[]{:S(2)}) collective-permute-start(bf16[1,3,128,256]{3,2,1,0:T(8,128)(2,1)S(1)} %get-tuple-element.44), channel_id=1, source_target_pairs={{64,0},{128,64},{192,128},{256,192},{320,256},{384,320},{448,384},... | collective-permute-start | bytes 589832 | tf_op jit(solution)/shard_map/ppermute | solution.py:10
  44.6 3.7 %collective-permute-start.7 = (bf16[1,3,128,256]{3,2,1,0:T(8,128)(2,1)S(1)}, bf16[1,3,128,256]{3,2,1,0:T(8,128)(2,1)S(1)}, u32[]{:S(2)}, u32[]{:S(2)}) collective-permute-start(bf16[1,3,128,256]{3,2,1,0:T(8,128)(2,1)S(1)} %get-tuple-element.44), channel_id=1, source_target_pairs={{0,64},{64,128},{128,192},{192,256},{256,320},{320,384},{384,448},... | collective-permute-start | bytes 589832 | tf_op jit(solution)/shard_map/ppermute | solution.py:10
  58.4 2.0 %convolution_bitcast_fusion.1 = f32[1,1152,256]{1,2,0:T(8,128)S(1)} fusion(s32[320]{0:T(512)S(1)} %add.175, f32[1,320,768]{2,1,0:T(8,128)} %convolution_bitcast_fusion.3), kind=kOutput, calls=%fused_computation.1 | convolution fusion | flops 566599680 | bytes 1508608 | tf_op jit(solution)/shard_map/en,med->mnd/dot_general | solution.py:42
  60.8 4.9 %collective-permute-start.11 = (bf16[1,3,128,256]{3,2,1,0:T(8,128)(2,1)S(1)}, bf16[1,3,128,256]{3,2,1,0:T(8,128)(2,1)S(1)}, u32[]{:S(2)}, u32[]{:S(2)}) collective-permute-start(bf16[1,3,128,256]{3,2,1,0:T(8,128)(2,1)S(1)} %get-tuple-element.30), channel_id=1, source_target_pairs={{0,64},{64,128},{128,192},{192,256},{256,320},{320,384},{384,448},... | collective-permute-start | bytes 589832 | tf_op jit(solution)/shard_map/ppermute | solution.py:10
  65.8 1.9 %collective-permute-start.10 = (bf16[1,3,128,256]{3,2,1,0:T(8,128)(2,1)S(1)}, bf16[1,3,128,256]{3,2,1,0:T(8,128)(2,1)S(1)}, u32[]{:S(2)}, u32[]{:S(2)}) collective-permute-start(bf16[1,3,128,256]{3,2,1,0:T(8,128)(2,1)S(1)} %get-tuple-element.29), channel_id=1, source_target_pairs={{64,0},{128,64},{192,128},{256,192},{320,256},{384,320},{448,384},... | collective-permute-start | bytes 589832 | tf_op jit(solution)/shard_map/ppermute | solution.py:10
  67.8 5.4 %collective-permute-start.9 = (bf16[448,256]{1,0:T(8,128)(2,1)S(1)}, bf16[448,256]{1,0:T(8,128)(2,1)S(1)}, u32[]{:S(2)}, u32[]{:S(2)}) collective-permute-start(bf16[448,256]{1,0:T(8,128)(2,1)S(1)} %maximum_select_fusion.1), channel_id=1, source_target_pairs={{0,512},{512,0},{1,513},{513,1},{2,514},{514,2},{3,515},{515,3},{4... | collective-permute-start | bytes 688136 | tf_op jit(solution)/shard_map/ppermute | solution.py:169
  74.7 7.4 %collective-permute-start.13 = (bf16[1,128,256]{2,1,0:T(8,128)(2,1)S(1)}, bf16[1,128,256]{2,1,0:T(8,128)(2,1)S(1)}, u32[]{:S(2)}, u32[]{:S(2)}) collective-permute-start(bf16[1,128,256]{2,1,0:T(8,128)(2,1)S(1)} %get-tuple-element.42), channel_id=1, source_target_pairs={{0,1},{1,2},{2,3},{3,4},{4,5},{5,6},{6,7},{7,8},{8,9},{9,10},{10,1... | collective-permute-start | bytes 196616 | tf_op jit(solution)/shard_map/ppermute | solution.py:10
  82.1 2.1 %collective-permute-start.12 = (bf16[1,128,256]{2,1,0:T(8,128)(2,1)S(1)}, bf16[1,128,256]{2,1,0:T(8,128)(2,1)S(1)}, u32[]{:S(2)}, u32[]{:S(2)}) collective-permute-start(bf16[1,128,256]{2,1,0:T(8,128)(2,1)S(1)} %get-tuple-element.41), channel_id=1, source_target_pairs={{1,0},{2,1},{3,2},{4,3},{5,4},{6,5},{7,6},{8,7},{9,8},{10,9},{11,1... | collective-permute-start | bytes 196616 | tf_op jit(solution)/shard_map/ppermute | solution.py:10
  84.9 5.5 %collective-permute-done.12 = bf16[1,128,256]{2,1,0:T(8,128)(2,1)S(1)} collective-permute-done((bf16[1,128,256]{2,1,0:T(8,128)(2,1)S(1)}, bf16[1,128,256]{2,1,0:T(8,128)(2,1)S(1)}, u32[]{:S(2)}, u32[]{:S(2)}) %collective-permute-start.12) | collective-permute-done | bytes 65568 | tf_op jit(solution)/shard_map/ppermute | solution.py:10
  92.0 2.1 %fusion.194 = (f32[320]{0:T(512)S(1)}, f32[320]{0:T(512)S(1)}, f32[1,320,256]{2,1,0:T(8,128)}) fusion(f32[320]{0:T(512)S(1)} %add_rsqrt_fusion.1, f32[320,256]{1,0:T(8,128)S(1)} %get-tuple-element.50, f32[320]{0:T(512)S(1)} %broadcast_multiply_fusion.5, s32[320]{0:T(512)S(1)} %eq.22, f32[1,128,512]{2,1,0:T(8,128)S(1)} %convolution_bitcast_fusion.6, ...), kind=kOutput, calls=%fused_computation.276 | convolution fusion | flops 63610240 | bytes 1286656 | tf_op jit(solution)/shard_map/en,mnd->med/dot_general | solution.py:42
  98.3 5.5 %collective-permute-start.15 = (bf16[1,3,128,256]{3,2,1,0:T(8,128)(2,1)S(1)}, bf16[1,3,128,256]{3,2,1,0:T(8,128)(2,1)S(1)}, u32[]{:S(2)}, u32[]{:S(2)}) collective-permute-start(bf16[1,3,128,256]{3,2,1,0:T(8,128)(2,1)S(1)} %get-tuple-element.28), channel_id=1, source_target_pairs={{0,64},{64,128},{128,192},{192,256},{256,320},{320,384},{384,448},... | collective-permute-start | bytes 589832 | tf_op jit(solution)/shard_map/ppermute | solution.py:10
  106.7 4.9 %collective-permute-done.14 = bf16[1,3,128,256]{3,2,1,0:T(8,128)(2,1)S(1)} collective-permute-done((bf16[1,3,128,256]{3,2,1,0:T(8,128)(2,1)S(1)}, bf16[1,3,128,256]{3,2,1,0:T(8,128)(2,1)S(1)}, u32[]{:S(2)}, u32[]{:S(2)}) %collective-permute-start.14) | collective-permute-done | bytes 196640 | tf_op jit(solution)/shard_map/ppermute | solution.py:10
  113.7 3.4 %collective-permute-start.16 = (bf16[1,128,256]{2,1,0:T(8,128)(2,1)S(1)}, bf16[1,128,256]{2,1,0:T(8,128)(2,1)S(1)}, u32[]{:S(2)}, u32[]{:S(2)}) collective-permute-start(bf16[1,128,256]{2,1,0:T(8,128)(2,1)S(1)} %get-tuple-element.39), channel_id=1, source_target_pairs={{1,0},{2,1},{3,2},{4,3},{5,4},{6,5},{7,6},{8,7},{9,8},{10,9},{11,1... | collective-permute-start | bytes 196616 | tf_op jit(solution)/shard_map/ppermute | solution.py:10
  117.4 4.6 %collective-permute-done.16 = bf16[1,128,256]{2,1,0:T(8,128)(2,1)S(1)} collective-permute-done((bf16[1,128,256]{2,1,0:T(8,128)(2,1)S(1)}, bf16[1,128,256]{2,1,0:T(8,128)(2,1)S(1)}, u32[]{:S(2)}, u32[]{:S(2)}) %collective-permute-start.16) | collective-permute-done | bytes 65568 | tf_op jit(solution)/shard_map/ppermute | solution.py:10
  122.1 7.6 %collective-permute-start.18 = (f32[448,256]{1,0:T(8,128)S(1)}, f32[448,256]{1,0:T(8,128)S(1)}, u32[]{:S(2)}, u32[]{:S(2)}) collective-permute-start(f32[448,256]{1,0:T(8,128)S(1)} %maximum_select_fusion), channel_id=1, source_target_pairs={{0,512},{512,0},{1,513},{513,1},{2,514},{514,2},{3,515},{515,3},{4... | collective-permute-start | bytes 1376264 | tf_op jit(solution)/shard_map/ppermute | solution.py:185
  (154 shorter events, 37.8 us)
Async XLA Ops:
  1.7 13.8 %collective-permute-start.2 = (bf16[1,128,256]{1,2,0:T(8,128)(2,1)S(1)}, bf16[1,128,256]{1,2,0:T(8,128)(2,1)S(1)}, u32[]{:S(2)}, u32[]{:S(2)}) collective-permute-start(bf16[1,128,256]{1,2,0:T(8,128)(2,1)S(1)} %bitcast.323), channel_id=1, source_target_pairs={{1,0},{2,1},{3,2},{4,3},{5,4},{6,5},{7,6},{8,7},{9,8},{10,9},{11,1... | collective-permute-start | bytes 196616 | tf_op jit(solution)/shard_map/ppermute | solution.py:10
  4.8 10.8 %collective-permute-start.1 = (bf16[1,128,256]{1,2,0:T(8,128)(2,1)S(1)}, bf16[1,128,256]{1,2,0:T(8,128)(2,1)S(1)}, u32[]{:S(2)}, u32[]{:S(2)}) collective-permute-start(bf16[1,128,256]{1,2,0:T(8,128)(2,1)S(1)} %bitcast.324), channel_id=1, source_target_pairs={{0,1},{1,2},{2,3},{3,4},{4,5},{5,6},{6,7},{7,8},{8,9},{9,10},{10,1... | collective-permute-start | bytes 196616 | tf_op jit(solution)/shard_map/ppermute | solution.py:10
  11.6 15.2 %collective-permute-start = (bf16[1792,256]{1,0:T(8,128)(2,1)S(1)}, bf16[1792,256]{1,0:T(8,128)(2,1)}, u32[]{:S(2)}, u32[]{:S(2)}) collective-permute-start(bf16[1792,256]{1,0:T(8,128)(2,1)S(1)} %pad_maximum_fusion), channel_id=1, source_target_pairs={{0,512},{512,0},{1,513},{513,1},{2,514},{514,2},{3,515},{515,3},{4... | collective-permute-start | bytes 2752520 | tf_op jit(solution)/shard_map/ppermute | solution.py:151
  15.6 8.4 %collective-permute-start.4 = (bf16[1,3,128,256]{2,3,1,0:T(8,128)(2,1)S(1)}, bf16[1,3,128,256]{2,3,1,0:T(8,128)(2,1)S(1)}, u32[]{:S(2)}, u32[]{:S(2)}) collective-permute-start(bf16[1,3,128,256]{2,3,1,0:T(8,128)(2,1)S(1)} %get-tuple-element.46), channel_id=1, source_target_pairs={{64,0},{128,64},{192,128},{256,192},{320,256},{384,320},{448,384},... | collective-permute-start | bytes 589832 | tf_op jit(solution)/shard_map/ppermute | solution.py:10
  17.6 8.1 %collective-permute-start.3 = (bf16[1,3,128,256]{2,3,1,0:T(8,128)(2,1)S(1)}, bf16[1,3,128,256]{2,3,1,0:T(8,128)(2,1)S(1)}, u32[]{:S(2)}, u32[]{:S(2)}) collective-permute-start(bf16[1,3,128,256]{2,3,1,0:T(8,128)(2,1)S(1)} %get-tuple-element.46), channel_id=1, source_target_pairs={{0,64},{64,128},{128,192},{192,256},{256,320},{320,384},{384,448},... | collective-permute-start | bytes 589832 | tf_op jit(solution)/shard_map/ppermute | solution.py:10
  30.7 20.7 %copy-start.8 = (f32[320,256]{1,0:T(8,128)}, f32[320,256]{1,0:T(8,128)S(1)}, u32[]{:S(2)}) copy-start(f32[320,256]{1,0:T(8,128)S(1)} %convolution_add_fusion.1) | copy-start | bytes 983044
  32.7 8.9 %collective-permute-start.6 = (bf16[1,128,256]{2,1,0:T(8,128)(2,1)S(1)}, bf16[1,128,256]{2,1,0:T(8,128)(2,1)S(1)}, u32[]{:S(2)}, u32[]{:S(2)}) collective-permute-start(bf16[1,128,256]{2,1,0:T(8,128)(2,1)S(1)} %bitcast.307), channel_id=1, source_target_pairs={{1,0},{2,1},{3,2},{4,3},{5,4},{6,5},{7,6},{8,7},{9,8},{10,9},{11,1... | collective-permute-start | bytes 196616 | tf_op jit(solution)/shard_map/ppermute | solution.py:10
  34.6 8.0 %collective-permute-start.5 = (bf16[1,128,256]{2,1,0:T(8,128)(2,1)S(1)}, bf16[1,128,256]{2,1,0:T(8,128)(2,1)S(1)}, u32[]{:S(2)}, u32[]{:S(2)}) collective-permute-start(bf16[1,128,256]{2,1,0:T(8,128)(2,1)S(1)} %bitcast.308), channel_id=1, source_target_pairs={{0,1},{1,2},{2,3},{3,4},{4,5},{5,6},{6,7},{7,8},{8,9},{9,10},{10,1... | collective-permute-start | bytes 196616 | tf_op jit(solution)/shard_map/ppermute | solution.py:10
  42.7 6.8 %collective-permute-start.8 = (bf16[1,3,128,256]{3,2,1,0:T(8,128)(2,1)S(1)}, bf16[1,3,128,256]{3,2,1,0:T(8,128)(2,1)S(1)}, u32[]{:S(2)}, u32[]{:S(2)}) collective-permute-start(bf16[1,3,128,256]{3,2,1,0:T(8,128)(2,1)S(1)} %get-tuple-element.44), channel_id=1, source_target_pairs={{64,0},{128,64},{192,128},{256,192},{320,256},{384,320},{448,384},... | collective-permute-start | bytes 589832 | tf_op jit(solution)/shard_map/ppermute | solution.py:10
  44.6 6.7 %collective-permute-start.7 = (bf16[1,3,128,256]{3,2,1,0:T(8,128)(2,1)S(1)}, bf16[1,3,128,256]{3,2,1,0:T(8,128)(2,1)S(1)}, u32[]{:S(2)}, u32[]{:S(2)}) collective-permute-start(bf16[1,3,128,256]{3,2,1,0:T(8,128)(2,1)S(1)} %get-tuple-element.44), channel_id=1, source_target_pairs={{0,64},{64,128},{128,192},{192,256},{256,320},{320,384},{384,448},... | collective-permute-start | bytes 589832 | tf_op jit(solution)/shard_map/ppermute | solution.py:10
  60.8 13.7 %collective-permute-start.11 = (bf16[1,3,128,256]{3,2,1,0:T(8,128)(2,1)S(1)}, bf16[1,3,128,256]{3,2,1,0:T(8,128)(2,1)S(1)}, u32[]{:S(2)}, u32[]{:S(2)}) collective-permute-start(bf16[1,3,128,256]{3,2,1,0:T(8,128)(2,1)S(1)} %get-tuple-element.30), channel_id=1, source_target_pairs={{0,64},{64,128},{128,192},{192,256},{256,320},{320,384},{384,448},... | collective-permute-start | bytes 589832 | tf_op jit(solution)/shard_map/ppermute | solution.py:10
  65.8 8.8 %collective-permute-start.10 = (bf16[1,3,128,256]{3,2,1,0:T(8,128)(2,1)S(1)}, bf16[1,3,128,256]{3,2,1,0:T(8,128)(2,1)S(1)}, u32[]{:S(2)}, u32[]{:S(2)}) collective-permute-start(bf16[1,3,128,256]{3,2,1,0:T(8,128)(2,1)S(1)} %get-tuple-element.29), channel_id=1, source_target_pairs={{64,0},{128,64},{192,128},{256,192},{320,256},{384,320},{448,384},... | collective-permute-start | bytes 589832 | tf_op jit(solution)/shard_map/ppermute | solution.py:10
  67.8 22.7 %copy-start.11 = (bf16[2,1,1,128,256]{4,3,2,1,0:T(8,128)(2,1)S(1)}, bf16[2,1,1,128,256]{4,3,2,1,0:T(8,128)(2,1)}, u32[]{:S(2)}) copy-start(bf16[2,1,1,128,256]{4,3,2,1,0:T(8,128)(2,1)} %param.20) | copy-start | bytes 393220
  67.8 22.7 %copy-start.15 = (f32[1,128,512]{2,1,0:T(8,128)S(1)}, f32[1,128,512]{2,1,0:T(8,128)}, u32[]{:S(2)}) copy-start(f32[1,128,512]{2,1,0:T(8,128)} %convolution_bitcast_fusion.7) | copy-start | bytes 786436
  67.8 16.4 %collective-permute-start.9 = (bf16[448,256]{1,0:T(8,128)(2,1)S(1)}, bf16[448,256]{1,0:T(8,128)(2,1)S(1)}, u32[]{:S(2)}, u32[]{:S(2)}) collective-permute-start(bf16[448,256]{1,0:T(8,128)(2,1)S(1)} %maximum_select_fusion.1), channel_id=1, source_target_pairs={{0,512},{512,0},{1,513},{513,1},{2,514},{514,2},{3,515},{515,3},{4... | collective-permute-start | bytes 688136 | tf_op jit(solution)/shard_map/ppermute | solution.py:169
  74.5 16.1 %copy-start.1 = (bf16[1792,256]{1,0:T(8,128)(2,1)S(1)}, bf16[1792,256]{1,0:T(8,128)(2,1)}, u32[]{:S(2)}) copy-start(bf16[1792,256]{1,0:T(8,128)(2,1)} %copy-done) | copy-start | bytes 2752516
  74.7 10.3 %collective-permute-start.13 = (bf16[1,128,256]{2,1,0:T(8,128)(2,1)S(1)}, bf16[1,128,256]{2,1,0:T(8,128)(2,1)S(1)}, u32[]{:S(2)}, u32[]{:S(2)}) collective-permute-start(bf16[1,128,256]{2,1,0:T(8,128)(2,1)S(1)} %get-tuple-element.42), channel_id=1, source_target_pairs={{0,1},{1,2},{2,3},{3,4},{4,5},{5,6},{6,7},{7,8},{8,9},{9,10},{10,1... | collective-permute-start | bytes 196616 | tf_op jit(solution)/shard_map/ppermute | solution.py:10
  82.1 8.3 %collective-permute-start.12 = (bf16[1,128,256]{2,1,0:T(8,128)(2,1)S(1)}, bf16[1,128,256]{2,1,0:T(8,128)(2,1)S(1)}, u32[]{:S(2)}, u32[]{:S(2)}) collective-permute-start(bf16[1,128,256]{2,1,0:T(8,128)(2,1)S(1)} %get-tuple-element.41), channel_id=1, source_target_pairs={{1,0},{2,1},{3,2},{4,3},{5,4},{6,5},{7,6},{8,7},{9,8},{10,9},{11,1... | collective-permute-start | bytes 196616 | tf_op jit(solution)/shard_map/ppermute | solution.py:10
  98.3 8.5 %collective-permute-start.15 = (bf16[1,3,128,256]{3,2,1,0:T(8,128)(2,1)S(1)}, bf16[1,3,128,256]{3,2,1,0:T(8,128)(2,1)S(1)}, u32[]{:S(2)}, u32[]{:S(2)}) collective-permute-start(bf16[1,3,128,256]{3,2,1,0:T(8,128)(2,1)S(1)} %get-tuple-element.28), channel_id=1, source_target_pairs={{0,64},{64,128},{128,192},{192,256},{256,320},{320,384},{384,448},... | collective-permute-start | bytes 589832 | tf_op jit(solution)/shard_map/ppermute | solution.py:10
  103.7 7.9 %collective-permute-start.14 = (bf16[1,3,128,256]{3,2,1,0:T(8,128)(2,1)S(1)}, bf16[1,3,128,256]{3,2,1,0:T(8,128)(2,1)S(1)}, u32[]{:S(2)}, u32[]{:S(2)}) collective-permute-start(bf16[1,3,128,256]{3,2,1,0:T(8,128)(2,1)S(1)} %get-tuple-element.27), channel_id=1, source_target_pairs={{64,0},{128,64},{192,128},{256,192},{320,256},{384,320},{448,384},... | collective-permute-start | bytes 589832 | tf_op jit(solution)/shard_map/ppermute | solution.py:10
  106.7 15.3 %copy-start.13 = (f32[1,128,512]{2,1,0:T(8,128)S(1)}, f32[1,128,512]{2,1,0:T(8,128)}, u32[]{:S(2)}) copy-start(f32[1,128,512]{2,1,0:T(8,128)} %copy-done.12) | copy-start | bytes 786436
  111.7 5.7 %collective-permute-start.17 = (bf16[1,128,256]{2,1,0:T(8,128)(2,1)S(1)}, bf16[1,128,256]{2,1,0:T(8,128)(2,1)S(1)}, u32[]{:S(2)}, u32[]{:S(2)}) collective-permute-start(bf16[1,128,256]{2,1,0:T(8,128)(2,1)S(1)} %get-tuple-element.40), channel_id=1, source_target_pairs={{0,1},{1,2},{2,3},{3,4},{4,5},{5,6},{6,7},{7,8},{8,9},{9,10},{10,1... | collective-permute-start | bytes 196616 | tf_op jit(solution)/shard_map/ppermute | solution.py:10
  113.7 8.3 %collective-permute-start.16 = (bf16[1,128,256]{2,1,0:T(8,128)(2,1)S(1)}, bf16[1,128,256]{2,1,0:T(8,128)(2,1)S(1)}, u32[]{:S(2)}, u32[]{:S(2)}) collective-permute-start(bf16[1,128,256]{2,1,0:T(8,128)(2,1)S(1)} %get-tuple-element.39), channel_id=1, source_target_pairs={{1,0},{2,1},{3,2},{4,3},{5,4},{6,5},{7,6},{8,7},{9,8},{10,9},{11,1... | collective-permute-start | bytes 196616 | tf_op jit(solution)/shard_map/ppermute | solution.py:10
  122.1 9.1 %collective-permute-start.18 = (f32[448,256]{1,0:T(8,128)S(1)}, f32[448,256]{1,0:T(8,128)S(1)}, u32[]{:S(2)}, u32[]{:S(2)}) collective-permute-start(f32[448,256]{1,0:T(8,128)S(1)} %maximum_select_fusion), channel_id=1, source_target_pairs={{0,512},{512,0},{1,513},{513,1},{2,514},{514,2},{3,515},{515,3},{4... | collective-permute-start | bytes 1376264 | tf_op jit(solution)/shard_map/ppermute | solution.py:185
  (20 other events, 146.2 us)

commit v7 on v4

--- a/solution.py
+++ b/solution.py
@@ -184,11 +184,12 @@
     )
     grad_recv = lax.ppermute(grad_send, "phase", [(0, 1), (1, 0)])
 
+    other_slot = 1 - lax.axis_index("phase")
+
     def placed(own_first, own_second, received, shape):
         kept = jnp.where(is_first, own_first, own_second)
-        pair = jnp.where(
-            is_first, jnp.stack([kept, received]), jnp.stack([received, kept])
-        )
+        pair = jnp.stack([kept, kept])
+        pair = lax.dynamic_update_index_in_dim(pair, received, other_slot, axis=0)
         return pair.reshape(shape)
 
     node_shape = (1,) + node_latents.shape

time: 128 us -> 130 us (1.016)
  matrix products: 12 us -> 15.3 us
    select_n x4 -> x0, other arithmetic: 3.04 us -> none  [placed(): jnp.where(is_first, jnp.stack([kept, received]), jnp.stack([received, kep...]
    dot_general x8, matrix products: 4.58 us -> 6.84 us  [onehot_sum(): jnp.einsum(form, left, right, precision=lax.Precision.HIGH, preferred_ele...]
    dynamic_update_slice x0 -> x4, local copies, waits for them, and re-layouts: none -> 1.83 us  [placed(): pair = lax.dynamic_update_index_in_dim(pair, received, other_slot, axis=0)]
    unnamed x62 -> x76, local copies, waits for them, and re-layouts: 3.71 us -> 3.8 us
  transfers between devices with their start and end apart: 19 -> 19, of which waited for: 12 -> 13; matrix products, arithmetic and copies ran while one was open for 9% -> 6% of each run, Pallas kernels for 0% -> 0%
where the time goes in v7:
time: 130 us; the launch traced here: 129 us
  starting transfers between devices  61.9 us (48%)
  waiting for transfers between devices  32.3 us (25%)
  matrix products  15.3 us (12%)
  other arithmetic  11.5 us (9%)
  local copies, waits for them, and re-layouts  6.73 us (5%)
  between operations  1.67 us (1%)
    ppermute x16, starting transfers between devices, shifted(): return lax.ppermute(array, axis, pairs)  46.6 us
    ppermute x16, waiting for transfers between devices, shifted(): return lax.ppermute(array, axis, pairs)  31.8 us
    dot_general x8, matrix products, onehot_sum(): jnp.einsum(form, left, right, precision=lax.Precision.HIGH, preferred_ele...  6.84 us
    ppermute x1, starting transfers between devices, body(): grad_recv = lax.ppermute(grad_send, 'phase', [(0, 1), (1, 0)])  6.43 us
    ppermute x1, starting transfers between devices, body(): latent_recv = lax.ppermute(latent_send, 'phase', [(0, 1), (1, 0)])  5.75 us
    dot_general x4, matrix products, times_turned(): jnp.einsum('mrd,kd->mrk', left, right, preferred_element_type=jnp.float32)  4.93 us
    unnamed x76, local copies, waits for them, and re-layouts  3.8 us
    ppermute x1, starting transfers between devices, body(): other = lax.ppermute(own, 'phase', [(0, 1), (1, 0)])  3.14 us
  transfers between devices with their start and end apart: 19, of which 13 were waited for; matrix products, arithmetic and copies ran while one was open for 6% of the time, Pallas kernels for 0%

profile of v7, /device:TPU:593, one launch (start us, length us, event | category | flops | bytes accessed | tf_op | source)
XLA Modules:
  0.0 129.4 jit_solution(10723048301911899588)
XLA Ops:
  1.7 2.7 %collective-permute-start.1 = (bf16[1,128,256]{2,1,0:T(8,128)(2,1)S(1)}, bf16[1,128,256]{2,1,0:T(8,128)(2,1)S(1)}, u32[]{:S(2)}, u32[]{:S(2)}) collective-permute-start(bf16[1,128,256]{2,1,0:T(8,128)(2,1)S(1)} %fusion.210), channel_id=1, source_target_pairs={{1,0},{2,1},{3,2},{4,3},{5,4},{6,5},{7,6},{8,7},{9,8},{10,9},{11,1... | collective-permute-start | bytes 196616 | tf_op jit(solution)/shard_map/ppermute | solution.py:10
  4.3 2.6 %collective-permute-start = (bf16[1,128,256]{2,1,0:T(8,128)(2,1)S(1)}, bf16[1,128,256]{2,1,0:T(8,128)(2,1)S(1)}, u32[]{:S(2)}, u32[]{:S(2)}) collective-permute-start(bf16[1,128,256]{2,1,0:T(8,128)(2,1)S(1)} %fusion.210), channel_id=1, source_target_pairs={{0,1},{1,2},{2,3},{3,4},{4,5},{5,6},{6,7},{7,8},{8,9},{9,10},{10,1... | collective-permute-start | bytes 196616 | tf_op jit(solution)/shard_map/ppermute | solution.py:10
  8.3 3.1 %collective-permute-start.4 = (bf16[1792,256]{1,0:T(8,128)(2,1)S(1)}, bf16[1792,256]{1,0:T(8,128)(2,1)}, u32[]{:S(2)}, u32[]{:S(2)}) collective-permute-start(bf16[1792,256]{1,0:T(8,128)(2,1)S(1)} %pad_maximum_fusion), channel_id=1, source_target_pairs={{0,512},{512,0},{1,513},{513,1},{2,514},{514,2},{3,515},{515,3},{4... | collective-permute-start | bytes 2752520 | tf_op jit(solution)/shard_map/ppermute | solution.py:151
  12.7 2.9 %collective-permute-start.3 = (bf16[1,3,128,256]{3,2,1,0:T(8,128)(2,1)S(1)}, bf16[1,3,128,256]{3,2,1,0:T(8,128)(2,1)S(1)}, u32[]{:S(2)}, u32[]{:S(2)}) collective-permute-start(bf16[1,3,128,256]{3,2,1,0:T(8,128)(2,1)S(1)} %get-tuple-element.42), channel_id=1, source_target_pairs={{64,0},{128,64},{192,128},{256,192},{320,256},{384,320},{448,384},... | collective-permute-start | bytes 589832 | tf_op jit(solution)/shard_map/ppermute | solution.py:10
  15.6 2.4 %collective-permute-start.2 = (bf16[1,3,128,256]{3,2,1,0:T(8,128)(2,1)S(1)}, bf16[1,3,128,256]{3,2,1,0:T(8,128)(2,1)S(1)}, u32[]{:S(2)}, u32[]{:S(2)}) collective-permute-start(bf16[1,3,128,256]{3,2,1,0:T(8,128)(2,1)S(1)} %get-tuple-element.42), channel_id=1, source_target_pairs={{0,64},{64,128},{128,192},{192,256},{256,320},{320,384},{384,448},... | collective-permute-start | bytes 589832 | tf_op jit(solution)/shard_map/ppermute | solution.py:10
  19.1 2.9 %collective-permute-done.2 = bf16[1,3,128,256]{3,2,1,0:T(8,128)(2,1)S(1)} collective-permute-done((bf16[1,3,128,256]{3,2,1,0:T(8,128)(2,1)S(1)}, bf16[1,3,128,256]{3,2,1,0:T(8,128)(2,1)S(1)}, u32[]{:S(2)}, u32[]{:S(2)}) %collective-permute-start.2) | collective-permute-done | bytes 196640 | tf_op jit(solution)/shard_map/ppermute | solution.py:10
  26.9 7.3 %collective-permute-start.6 = (bf16[1,128,256]{2,1,0:T(8,128)(2,1)S(1)}, bf16[1,128,256]{2,1,0:T(8,128)(2,1)S(1)}, u32[]{:S(2)}, u32[]{:S(2)}) collective-permute-start(bf16[1,128,256]{2,1,0:T(8,128)(2,1)S(1)} %bitcast.308), channel_id=1, source_target_pairs={{1,0},{2,1},{3,2},{4,3},{5,4},{6,5},{7,6},{8,7},{9,8},{10,9},{11,1... | collective-permute-start | bytes 196616 | tf_op jit(solution)/shard_map/ppermute | solution.py:10
  34.3 1.9 %collective-permute-start.5 = (bf16[1,128,256]{2,1,0:T(8,128)(2,1)S(1)}, bf16[1,128,256]{2,1,0:T(8,128)(2,1)S(1)}, u32[]{:S(2)}, u32[]{:S(2)}) collective-permute-start(bf16[1,128,256]{2,1,0:T(8,128)(2,1)S(1)} %bitcast.309), channel_id=1, source_target_pairs={{0,1},{1,2},{2,3},{3,4},{4,5},{5,6},{6,7},{7,8},{8,9},{9,10},{10,1... | collective-permute-start | bytes 196616 | tf_op jit(solution)/shard_map/ppermute | solution.py:10
  36.5 6.1 %collective-permute-done.5 = bf16[1,128,256]{2,1,0:T(8,128)(2,1)S(1)} collective-permute-done((bf16[1,128,256]{2,1,0:T(8,128)(2,1)S(1)}, bf16[1,128,256]{2,1,0:T(8,128)(2,1)S(1)}, u32[]{:S(2)}, u32[]{:S(2)}) %collective-permute-start.5) | collective-permute-done | bytes 65568 | tf_op jit(solution)/shard_map/ppermute | solution.py:10
  42.7 3.2 %collective-permute-start.8 = (bf16[1,3,128,256]{3,2,1,0:T(8,128)(2,1)S(1)}, bf16[1,3,128,256]{3,2,1,0:T(8,128)(2,1)S(1)}, u32[]{:S(2)}, u32[]{:S(2)}) collective-permute-start(bf16[1,3,128,256]{3,2,1,0:T(8,128)(2,1)S(1)} %get-tuple-element.40), channel_id=1, source_target_pairs={{64,0},{128,64},{192,128},{256,192},{320,256},{384,320},{448,384},... | collective-permute-start | bytes 589832 | tf_op jit(solution)/shard_map/ppermute | solution.py:10
  45.9 2.1 %collective-permute-start.7 = (bf16[1,3,128,256]{3,2,1,0:T(8,128)(2,1)S(1)}, bf16[1,3,128,256]{3,2,1,0:T(8,128)(2,1)S(1)}, u32[]{:S(2)}, u32[]{:S(2)}) collective-permute-start(bf16[1,3,128,256]{3,2,1,0:T(8,128)(2,1)S(1)} %get-tuple-element.40), channel_id=1, source_target_pairs={{0,64},{64,128},{128,192},{192,256},{256,320},{320,384},{384,448},... | collective-permute-start | bytes 589832 | tf_op jit(solution)/shard_map/ppermute | solution.py:10
  49.1 3.3 %collective-permute-done.7 = bf16[1,3,128,256]{3,2,1,0:T(8,128)(2,1)S(1)} collective-permute-done((bf16[1,3,128,256]{3,2,1,0:T(8,128)(2,1)S(1)}, bf16[1,3,128,256]{3,2,1,0:T(8,128)(2,1)S(1)}, u32[]{:S(2)}, u32[]{:S(2)}) %collective-permute-start.7) | collective-permute-done | bytes 196640 | tf_op jit(solution)/shard_map/ppermute | solution.py:10
  61.9 2.0 %convolution_bitcast_fusion.1 = f32[1,1152,256]{1,2,0:T(8,128)S(1)} fusion(s32[320]{0:T(512)S(1)} %add.171, f32[1,320,768]{2,1,0:T(8,128)} %copy-done.3), kind=kOutput, calls=%fused_computation.1 | convolution fusion | flops 566599680 | bytes 1508608 | tf_op jit(solution)/shard_map/en,med->mnd/dot_general | solution.py:42
  66.1 5.8 %collective-permute-start.9 = (bf16[448,256]{1,0:T(8,128)(2,1)}, bf16[448,256]{1,0:T(8,128)(2,1)}, u32[]{:S(2)}, u32[]{:S(2)}) collective-permute-start(bf16[448,256]{1,0:T(8,128)(2,1)} %maximum_select_fusion.1), channel_id=1, source_target_pairs={{0,512},{512,0},{1,513},{513,1},{2,514},{514,2},{3,515},{515,3},{4... | collective-permute-start | bytes 688136 | tf_op jit(solution)/shard_map/ppermute | solution.py:169
  72.3 2.9 %collective-permute-start.10 = (bf16[1,3,128,256]{3,2,1,0:T(8,128)(2,1)S(1)}, bf16[1,3,128,256]{3,2,1,0:T(8,128)(2,1)S(1)}, u32[]{:S(2)}, u32[]{:S(2)}) collective-permute-start(bf16[1,3,128,256]{3,2,1,0:T(8,128)(2,1)S(1)} %get-tuple-element.33), channel_id=1, source_target_pairs={{64,0},{128,64},{192,128},{256,192},{320,256},{384,320},{448,384},... | collective-permute-start | bytes 589832 | tf_op jit(solution)/shard_map/ppermute | solution.py:10
  75.2 2.6 %collective-permute-start.11 = (bf16[1,3,128,256]{3,2,1,0:T(8,128)(2,1)S(1)}, bf16[1,3,128,256]{3,2,1,0:T(8,128)(2,1)S(1)}, u32[]{:S(2)}, u32[]{:S(2)}) collective-permute-start(bf16[1,3,128,256]{3,2,1,0:T(8,128)(2,1)S(1)} %get-tuple-element.34), channel_id=1, source_target_pairs={{0,64},{64,128},{128,192},{192,256},{256,320},{320,384},{384,448},... | collective-permute-start | bytes 589832 | tf_op jit(solution)/shard_map/ppermute | solution.py:10
  80.7 2.7 %collective-permute-done.11 = bf16[1,3,128,256]{3,2,1,0:T(8,128)(2,1)S(1)} collective-permute-done((bf16[1,3,128,256]{3,2,1,0:T(8,128)(2,1)S(1)}, bf16[1,3,128,256]{3,2,1,0:T(8,128)(2,1)S(1)}, u32[]{:S(2)}, u32[]{:S(2)}) %collective-permute-start.11) | collective-permute-done | bytes 196640 | tf_op jit(solution)/shard_map/ppermute | solution.py:10
  85.4 3.4 %collective-permute-start.13 = (bf16[1,128,256]{2,1,0:T(8,128)(2,1)S(1)}, bf16[1,128,256]{2,1,0:T(8,128)(2,1)S(1)}, u32[]{:S(2)}, u32[]{:S(2)}) collective-permute-start(bf16[1,128,256]{2,1,0:T(8,128)(2,1)S(1)} %get-tuple-element.38), channel_id=1, source_target_pairs={{0,1},{1,2},{2,3},{3,4},{4,5},{5,6},{6,7},{7,8},{8,9},{9,10},{10,1... | collective-permute-start | bytes 196616 | tf_op jit(solution)/shard_map/ppermute | solution.py:10
  89.8 4.0 %collective-permute-done.13 = bf16[1,128,256]{2,1,0:T(8,128)(2,1)S(1)} collective-permute-done((bf16[1,128,256]{2,1,0:T(8,128)(2,1)S(1)}, bf16[1,128,256]{2,1,0:T(8,128)(2,1)S(1)}, u32[]{:S(2)}, u32[]{:S(2)}) %collective-permute-start.13) | collective-permute-done | bytes 65568 | tf_op jit(solution)/shard_map/ppermute | solution.py:10
  100.1 3.6 %collective-permute-start.14 = (bf16[1,3,128,256]{3,2,1,0:T(8,128)(2,1)S(1)}, bf16[1,3,128,256]{3,2,1,0:T(8,128)(2,1)S(1)}, u32[]{:S(2)}, u32[]{:S(2)}) collective-permute-start(bf16[1,3,128,256]{3,2,1,0:T(8,128)(2,1)S(1)} %get-tuple-element.31), channel_id=1, source_target_pairs={{64,0},{128,64},{192,128},{256,192},{320,256},{384,320},{448,384},... | collective-permute-start | bytes 589832 | tf_op jit(solution)/shard_map/ppermute | solution.py:10
  106.6 3.5 %collective-permute-done.15 = bf16[1,3,128,256]{3,2,1,0:T(8,128)(2,1)S(1)} collective-permute-done((bf16[1,3,128,256]{3,2,1,0:T(8,128)(2,1)S(1)}, bf16[1,3,128,256]{3,2,1,0:T(8,128)(2,1)S(1)}, u32[]{:S(2)}, u32[]{:S(2)}) %collective-permute-start.15) | collective-permute-done | bytes 196640 | tf_op jit(solution)/shard_map/ppermute | solution.py:10
  112.1 3.4 %collective-permute-start.17 = (bf16[1,128,256]{2,1,0:T(8,128)(2,1)S(1)}, bf16[1,128,256]{2,1,0:T(8,128)(2,1)S(1)}, u32[]{:S(2)}, u32[]{:S(2)}) collective-permute-start(bf16[1,128,256]{2,1,0:T(8,128)(2,1)S(1)} %get-tuple-element.36), channel_id=1, source_target_pairs={{0,1},{1,2},{2,3},{3,4},{4,5},{5,6},{6,7},{7,8},{8,9},{9,10},{10,1... | collective-permute-start | bytes 196616 | tf_op jit(solution)/shard_map/ppermute | solution.py:10
  115.8 4.6 %collective-permute-done.17 = bf16[1,128,256]{2,1,0:T(8,128)(2,1)S(1)} collective-permute-done((bf16[1,128,256]{2,1,0:T(8,128)(2,1)S(1)}, bf16[1,128,256]{2,1,0:T(8,128)(2,1)S(1)}, u32[]{:S(2)}, u32[]{:S(2)}) %collective-permute-start.17) | collective-permute-done | bytes 65568 | tf_op jit(solution)/shard_map/ppermute | solution.py:10
  120.6 6.4 %collective-permute-start.18 = (f32[448,256]{1,0:T(8,128)S(1)}, f32[448,256]{1,0:T(8,128)S(1)}, u32[]{:S(2)}, u32[]{:S(2)}) collective-permute-start(f32[448,256]{1,0:T(8,128)S(1)} %maximum_select_fusion), channel_id=1, source_target_pairs={{0,512},{512,0},{1,513},{513,1},{2,514},{514,2},{3,515},{515,3},{4... | collective-permute-start | bytes 1376264 | tf_op jit(solution)/shard_map/ppermute | solution.py:185
  (181 shorter events, 42.5 us)
Async XLA Ops:
  1.7 10.6 %collective-permute-start.1 = (bf16[1,128,256]{2,1,0:T(8,128)(2,1)S(1)}, bf16[1,128,256]{2,1,0:T(8,128)(2,1)S(1)}, u32[]{:S(2)}, u32[]{:S(2)}) collective-permute-start(bf16[1,128,256]{2,1,0:T(8,128)(2,1)S(1)} %fusion.210), channel_id=1, source_target_pairs={{1,0},{2,1},{3,2},{4,3},{5,4},{6,5},{7,6},{8,7},{9,8},{10,9},{11,1... | collective-permute-start | bytes 196616 | tf_op jit(solution)/shard_map/ppermute | solution.py:10
  4.3 8.3 %collective-permute-start = (bf16[1,128,256]{2,1,0:T(8,128)(2,1)S(1)}, bf16[1,128,256]{2,1,0:T(8,128)(2,1)S(1)}, u32[]{:S(2)}, u32[]{:S(2)}) collective-permute-start(bf16[1,128,256]{2,1,0:T(8,128)(2,1)S(1)} %fusion.210), channel_id=1, source_target_pairs={{0,1},{1,2},{2,3},{3,4},{4,5},{5,6},{6,7},{7,8},{8,9},{9,10},{10,1... | collective-permute-start | bytes 196616 | tf_op jit(solution)/shard_map/ppermute | solution.py:10
  8.3 14.2 %collective-permute-start.4 = (bf16[1792,256]{1,0:T(8,128)(2,1)S(1)}, bf16[1792,256]{1,0:T(8,128)(2,1)}, u32[]{:S(2)}, u32[]{:S(2)}) collective-permute-start(bf16[1792,256]{1,0:T(8,128)(2,1)S(1)} %pad_maximum_fusion), channel_id=1, source_target_pairs={{0,512},{512,0},{1,513},{513,1},{2,514},{514,2},{3,515},{515,3},{4... | collective-permute-start | bytes 2752520 | tf_op jit(solution)/shard_map/ppermute | solution.py:151
  12.7 6.4 %collective-permute-start.3 = (bf16[1,3,128,256]{3,2,1,0:T(8,128)(2,1)S(1)}, bf16[1,3,128,256]{3,2,1,0:T(8,128)(2,1)S(1)}, u32[]{:S(2)}, u32[]{:S(2)}) collective-permute-start(bf16[1,3,128,256]{3,2,1,0:T(8,128)(2,1)S(1)} %get-tuple-element.42), channel_id=1, source_target_pairs={{64,0},{128,64},{192,128},{256,192},{320,256},{384,320},{448,384},... | collective-permute-start | bytes 589832 | tf_op jit(solution)/shard_map/ppermute | solution.py:10
  15.6 6.4 %collective-permute-start.2 = (bf16[1,3,128,256]{3,2,1,0:T(8,128)(2,1)S(1)}, bf16[1,3,128,256]{3,2,1,0:T(8,128)(2,1)S(1)}, u32[]{:S(2)}, u32[]{:S(2)}) collective-permute-start(bf16[1,3,128,256]{3,2,1,0:T(8,128)(2,1)S(1)} %get-tuple-element.42), channel_id=1, source_target_pairs={{0,64},{64,128},{128,192},{192,256},{256,320},{320,384},{384,448},... | collective-permute-start | bytes 589832 | tf_op jit(solution)/shard_map/ppermute | solution.py:10
  25.0 17.6 %copy-start.36 = (f32[320,256]{1,0:T(8,128)}, f32[320,256]{1,0:T(8,128)S(1)}, u32[]{:S(2)}) copy-start(f32[320,256]{1,0:T(8,128)S(1)} %fusion.20) | copy-start | bytes 983044
  26.3 16.3 %copy-start.35 = (f32[128,256]{1,0:T(8,128)}, f32[128,256]{1,0:T(8,128)S(1)}, u32[]{:S(2)}) copy-start(f32[128,256]{1,0:T(8,128)S(1)} %fusion.60) | copy-start | bytes 393220
  26.6 16.0 %copy-start.27 = (f32[128]{0:T(128)}, f32[128]{0:T(128)S(1)}, u32[]{:S(2)}) copy-start(f32[128]{0:T(128)S(1)} %broadcast_multiply_fusion.11) | copy-start | bytes 1540
  26.8 15.8 %copy-start.31 = (f32[128]{0:T(128)}, f32[128]{0:T(128)S(1)}, u32[]{:S(2)}) copy-start(f32[128]{0:T(128)S(1)} %add_rsqrt_fusion.3) | copy-start | bytes 1540
  26.9 9.5 %collective-permute-start.6 = (bf16[1,128,256]{2,1,0:T(8,128)(2,1)S(1)}, bf16[1,128,256]{2,1,0:T(8,128)(2,1)S(1)}, u32[]{:S(2)}, u32[]{:S(2)}) collective-permute-start(bf16[1,128,256]{2,1,0:T(8,128)(2,1)S(1)} %bitcast.308), channel_id=1, source_target_pairs={{1,0},{2,1},{3,2},{4,3},{5,4},{6,5},{7,6},{8,7},{9,8},{10,9},{11,1... | collective-permute-start | bytes 196616 | tf_op jit(solution)/shard_map/ppermute | solution.py:10
  34.3 8.3 %collective-permute-start.5 = (bf16[1,128,256]{2,1,0:T(8,128)(2,1)S(1)}, bf16[1,128,256]{2,1,0:T(8,128)(2,1)S(1)}, u32[]{:S(2)}, u32[]{:S(2)}) collective-permute-start(bf16[1,128,256]{2,1,0:T(8,128)(2,1)S(1)} %bitcast.309), channel_id=1, source_target_pairs={{0,1},{1,2},{2,3},{3,4},{4,5},{5,6},{6,7},{7,8},{8,9},{9,10},{10,1... | collective-permute-start | bytes 196616 | tf_op jit(solution)/shard_map/ppermute | solution.py:10
  42.7 6.4 %collective-permute-start.8 = (bf16[1,3,128,256]{3,2,1,0:T(8,128)(2,1)S(1)}, bf16[1,3,128,256]{3,2,1,0:T(8,128)(2,1)S(1)}, u32[]{:S(2)}, u32[]{:S(2)}) collective-permute-start(bf16[1,3,128,256]{3,2,1,0:T(8,128)(2,1)S(1)} %get-tuple-element.40), channel_id=1, source_target_pairs={{64,0},{128,64},{192,128},{256,192},{320,256},{384,320},{448,384},... | collective-permute-start | bytes 589832 | tf_op jit(solution)/shard_map/ppermute | solution.py:10
  45.9 6.5 %collective-permute-start.7 = (bf16[1,3,128,256]{3,2,1,0:T(8,128)(2,1)S(1)}, bf16[1,3,128,256]{3,2,1,0:T(8,128)(2,1)S(1)}, u32[]{:S(2)}, u32[]{:S(2)}) collective-permute-start(bf16[1,3,128,256]{3,2,1,0:T(8,128)(2,1)S(1)} %get-tuple-element.40), channel_id=1, source_target_pairs={{0,64},{64,128},{128,192},{192,256},{256,320},{320,384},{384,448},... | collective-permute-start | bytes 589832 | tf_op jit(solution)/shard_map/ppermute | solution.py:10
  66.1 22.7 %collective-permute-start.9 = (bf16[448,256]{1,0:T(8,128)(2,1)}, bf16[448,256]{1,0:T(8,128)(2,1)}, u32[]{:S(2)}, u32[]{:S(2)}) collective-permute-start(bf16[448,256]{1,0:T(8,128)(2,1)} %maximum_select_fusion.1), channel_id=1, source_target_pairs={{0,512},{512,0},{1,513},{513,1},{2,514},{514,2},{3,515},{515,3},{4... | collective-permute-start | bytes 688136 | tf_op jit(solution)/shard_map/ppermute | solution.py:169
  72.3 8.4 %collective-permute-start.10 = (bf16[1,3,128,256]{3,2,1,0:T(8,128)(2,1)S(1)}, bf16[1,3,128,256]{3,2,1,0:T(8,128)(2,1)S(1)}, u32[]{:S(2)}, u32[]{:S(2)}) collective-permute-start(bf16[1,3,128,256]{3,2,1,0:T(8,128)(2,1)S(1)} %get-tuple-element.33), channel_id=1, source_target_pairs={{64,0},{128,64},{192,128},{256,192},{320,256},{384,320},{448,384},... | collective-permute-start | bytes 589832 | tf_op jit(solution)/shard_map/ppermute | solution.py:10
  75.2 8.2 %collective-permute-start.11 = (bf16[1,3,128,256]{3,2,1,0:T(8,128)(2,1)S(1)}, bf16[1,3,128,256]{3,2,1,0:T(8,128)(2,1)S(1)}, u32[]{:S(2)}, u32[]{:S(2)}) collective-permute-start(bf16[1,3,128,256]{3,2,1,0:T(8,128)(2,1)S(1)} %get-tuple-element.34), channel_id=1, source_target_pairs={{0,64},{64,128},{128,192},{192,256},{256,320},{320,384},{384,448},... | collective-permute-start | bytes 589832 | tf_op jit(solution)/shard_map/ppermute | solution.py:10
  78.8 15.2 %copy-start.7 = (bf16[1792,256]{1,0:T(8,128)(2,1)S(1)}, bf16[1792,256]{1,0:T(8,128)(2,1)}, u32[]{:S(2)}) copy-start(bf16[1792,256]{1,0:T(8,128)(2,1)} %copy-done.6) | copy-start | bytes 2752516
  83.5 6.3 %collective-permute-start.12 = (bf16[1,128,256]{2,1,0:T(8,128)(2,1)S(1)}, bf16[1,128,256]{2,1,0:T(8,128)(2,1)S(1)}, u32[]{:S(2)}, u32[]{:S(2)}) collective-permute-start(bf16[1,128,256]{2,1,0:T(8,128)(2,1)S(1)} %get-tuple-element.37), channel_id=1, source_target_pairs={{1,0},{2,1},{3,2},{4,3},{5,4},{6,5},{7,6},{8,7},{9,8},{10,9},{11,1... | collective-permute-start | bytes 196616 | tf_op jit(solution)/shard_map/ppermute | solution.py:10
  85.4 8.3 %collective-permute-start.13 = (bf16[1,128,256]{2,1,0:T(8,128)(2,1)S(1)}, bf16[1,128,256]{2,1,0:T(8,128)(2,1)S(1)}, u32[]{:S(2)}, u32[]{:S(2)}) collective-permute-start(bf16[1,128,256]{2,1,0:T(8,128)(2,1)S(1)} %get-tuple-element.38), channel_id=1, source_target_pairs={{0,1},{1,2},{2,3},{3,4},{4,5},{5,6},{6,7},{7,8},{8,9},{9,10},{10,1... | collective-permute-start | bytes 196616 | tf_op jit(solution)/shard_map/ppermute | solution.py:10
  100.1 6.5 %collective-permute-start.14 = (bf16[1,3,128,256]{3,2,1,0:T(8,128)(2,1)S(1)}, bf16[1,3,128,256]{3,2,1,0:T(8,128)(2,1)S(1)}, u32[]{:S(2)}, u32[]{:S(2)}) collective-permute-start(bf16[1,3,128,256]{3,2,1,0:T(8,128)(2,1)S(1)} %get-tuple-element.31), channel_id=1, source_target_pairs={{64,0},{128,64},{192,128},{256,192},{320,256},{384,320},{448,384},... | collective-permute-start | bytes 589832 | tf_op jit(solution)/shard_map/ppermute | solution.py:10
  103.7 6.4 %collective-permute-start.15 = (bf16[1,3,128,256]{3,2,1,0:T(8,128)(2,1)S(1)}, bf16[1,3,128,256]{3,2,1,0:T(8,128)(2,1)S(1)}, u32[]{:S(2)}, u32[]{:S(2)}) collective-permute-start(bf16[1,3,128,256]{3,2,1,0:T(8,128)(2,1)S(1)} %get-tuple-element.32), channel_id=1, source_target_pairs={{0,64},{64,128},{128,192},{192,256},{256,320},{320,384},{384,448},... | collective-permute-start | bytes 589832 | tf_op jit(solution)/shard_map/ppermute | solution.py:10
  110.2 5.7 %collective-permute-start.16 = (bf16[1,128,256]{2,1,0:T(8,128)(2,1)S(1)}, bf16[1,128,256]{2,1,0:T(8,128)(2,1)S(1)}, u32[]{:S(2)}, u32[]{:S(2)}) collective-permute-start(bf16[1,128,256]{2,1,0:T(8,128)(2,1)S(1)} %get-tuple-element.35), channel_id=1, source_target_pairs={{1,0},{2,1},{3,2},{4,3},{5,4},{6,5},{7,6},{8,7},{9,8},{10,9},{11,1... | collective-permute-start | bytes 196616 | tf_op jit(solution)/shard_map/ppermute | solution.py:10
  112.1 8.3 %collective-permute-start.17 = (bf16[1,128,256]{2,1,0:T(8,128)(2,1)S(1)}, bf16[1,128,256]{2,1,0:T(8,128)(2,1)S(1)}, u32[]{:S(2)}, u32[]{:S(2)}) collective-permute-start(bf16[1,128,256]{2,1,0:T(8,128)(2,1)S(1)} %get-tuple-element.36), channel_id=1, source_target_pairs={{0,1},{1,2},{2,3},{3,4},{4,5},{5,6},{6,7},{7,8},{8,9},{9,10},{10,1... | collective-permute-start | bytes 196616 | tf_op jit(solution)/shard_map/ppermute | solution.py:10
  120.6 7.9 %collective-permute-start.18 = (f32[448,256]{1,0:T(8,128)S(1)}, f32[448,256]{1,0:T(8,128)S(1)}, u32[]{:S(2)}, u32[]{:S(2)}) collective-permute-start(f32[448,256]{1,0:T(8,128)S(1)} %maximum_select_fusion), channel_id=1, source_target_pairs={{0,512},{512,0},{1,513},{513,1},{2,514},{514,2},{3,515},{515,3},{4... | collective-permute-start | bytes 1376264 | tf_op jit(solution)/shard_map/ppermute | solution.py:185
  (33 other events, 199.1 us)

commit v8 on v4

--- a/solution.py
+++ b/solution.py
@@ -161,12 +161,6 @@
     edge_zero = mine(edge_latents).reshape(1, -1, width)
     node_one, edge_one, kept_one = forward(weights[0], tables, node_zero, edge_zero)
     node_two, edge_two, kept_two = forward(weights[1], tables, node_one, edge_one)
-    latent_send = jnp.where(
-        is_first,
-        jnp.concatenate([node_two[0], edge_two[0]], axis=0),
-        jnp.concatenate([node_one[0], edge_one[0]], axis=0),
-    )
-    latent_recv = lax.ppermute(latent_send, "phase", [(0, 1), (1, 0)])
     grad_node_one, grad_edge_one = backward(
         weights[1],
         tables,
@@ -177,12 +171,19 @@
     grad_node_zero, grad_edge_zero = backward(
         weights[0], tables, kept_one, grad_node_one, grad_edge_one
     )
-    grad_send = jnp.where(
+    swap_send = jnp.where(
         is_first,
-        jnp.concatenate([grad_node_one[0], grad_edge_one[0]], axis=0),
-        jnp.concatenate([grad_node_zero[0], grad_edge_zero[0]], axis=0),
-    )
-    grad_recv = lax.ppermute(grad_send, "phase", [(0, 1), (1, 0)])
+        jnp.concatenate(
+            [node_two[0], edge_two[0], grad_node_one[0], grad_edge_one[0]], axis=0
+        ),
+        jnp.concatenate(
+            [node_one[0], edge_one[0], grad_node_zero[0], grad_edge_zero[0]], axis=0
+        ),
+    )
+    swap_recv = lax.ppermute(swap_send, "phase", [(0, 1), (1, 0)])
+    rows = block_nodes + edge_zero.shape[1]
+    latent_recv = swap_recv[:rows].astype(jnp.bfloat16)
+    grad_recv = swap_recv[rows:]
 
     def placed(own_first, own_second, received, shape):
         kept = jnp.where(is_first, own_first, own_second)

time: 128 us -> 126 us (0.984)
  the two profiles are of different devices: /device:TPU:593 before, /device:TPU:625 now
where the time goes in v8:
time: 126 us; the launch traced here: 125 us
  starting transfers between devices  56.3 us (45%)
  waiting for transfers between devices  36.4 us (29%)
  matrix products  13.3 us (11%)
  other arithmetic  12.6 us (10%)
  local copies, waits for them, and re-layouts  4.48 us (4%)
  between operations  1.84 us (1%)
    ppermute x16, starting transfers between devices, shifted(): return lax.ppermute(array, axis, pairs)  42.5 us
    ppermute x16, waiting for transfers between devices, shifted(): return lax.ppermute(array, axis, pairs)  34.6 us
    ppermute x1, starting transfers between devices, body(): swap_recv = lax.ppermute(swap_send, 'phase', [(0, 1), (1, 0)])  10.7 us
    dot_general x4, matrix products, times_turned(): jnp.einsum('mrd,kd->mrk', left, right, preferred_element_type=jnp.float32)  5.24 us
    dot_general x8, matrix products, onehot_sum(): jnp.einsum(form, left, right, precision=lax.Precision.HIGH, preferred_ele...  4.58 us
    unnamed x100, local copies, waits for them, and re-layouts  3.32 us
    ppermute x1, starting transfers between devices, body(): other = lax.ppermute(own, 'phase', [(0, 1), (1, 0)])  3.14 us
    select_n x4, other arithmetic, placed(): jnp.where(is_first, jnp.stack([kept, received]), jnp.stack([received, kep...  3.05 us
  transfers between devices with their start and end apart: 18, of which 13 were waited for; matrix products, arithmetic and copies ran while one was open for 5% of the time, Pallas kernels for 0%

profile of v8, /device:TPU:625, one launch (start us, length us, event | category | flops | bytes accessed | tf_op | source)
XLA Modules:
  0.0 125.0 jit_solution(14441329547109559670)
XLA Ops:
  1.7 2.7 %collective-permute-start.1 = (bf16[1,128,256]{2,1,0:T(8,128)(2,1)S(1)}, bf16[1,128,256]{2,1,0:T(8,128)(2,1)}, u32[]{:S(2)}, u32[]{:S(2)}) collective-permute-start(bf16[1,128,256]{2,1,0:T(8,128)(2,1)S(1)} %fusion.211), channel_id=1, source_target_pairs={{1,0},{2,1},{3,2},{4,3},{5,4},{6,5},{7,6},{8,7},{9,8},{10,9},{11,1... | collective-permute-start | bytes 196616 | tf_op jit(solution)/shard_map/ppermute | solution.py:10
  4.4 2.6 %collective-permute-start = (bf16[1,128,256]{2,1,0:T(8,128)(2,1)S(1)}, bf16[1,128,256]{2,1,0:T(8,128)(2,1)}, u32[]{:S(2)}, u32[]{:S(2)}) collective-permute-start(bf16[1,128,256]{2,1,0:T(8,128)(2,1)S(1)} %fusion.211), channel_id=1, source_target_pairs={{0,1},{1,2},{2,3},{3,4},{4,5},{5,6},{6,7},{7,8},{8,9},{9,10},{10,1... | collective-permute-start | bytes 196616 | tf_op jit(solution)/shard_map/ppermute | solution.py:10
  8.3 3.1 %collective-permute-start.4 = (bf16[1792,256]{1,0:T(8,128)(2,1)S(1)}, bf16[1792,256]{1,0:T(8,128)(2,1)S(1)}, u32[]{:S(2)}, u32[]{:S(2)}) collective-permute-start(bf16[1792,256]{1,0:T(8,128)(2,1)S(1)} %pad_maximum_fusion), channel_id=1, source_target_pairs={{0,512},{512,0},{1,513},{513,1},{2,514},{514,2},{3,515},{515,3},{4... | collective-permute-start | bytes 2752520 | tf_op jit(solution)/shard_map/ppermute | solution.py:151
  13.7 2.9 %collective-permute-start.3 = (bf16[1,3,128,256]{3,2,1,0:T(8,128)(2,1)S(1)}, bf16[1,3,128,256]{3,2,1,0:T(8,128)(2,1)S(1)}, u32[]{:S(2)}, u32[]{:S(2)}) collective-permute-start(bf16[1,3,128,256]{3,2,1,0:T(8,128)(2,1)S(1)} %get-tuple-element.38), channel_id=1, source_target_pairs={{64,0},{128,64},{192,128},{256,192},{320,256},{384,320},{448,384},... | collective-permute-start | bytes 589832 | tf_op jit(solution)/shard_map/ppermute | solution.py:10
  19.2 3.8 %collective-permute-done.2 = bf16[1,3,128,256]{3,2,1,0:T(8,128)(2,1)S(1)} collective-permute-done((bf16[1,3,128,256]{3,2,1,0:T(8,128)(2,1)S(1)}, bf16[1,3,128,256]{3,2,1,0:T(8,128)(2,1)S(1)}, u32[]{:S(2)}, u32[]{:S(2)}) %collective-permute-start.2) | collective-permute-done | bytes 196640 | tf_op jit(solution)/shard_map/ppermute | solution.py:10
  27.6 7.2 %collective-permute-start.6 = (bf16[1,128,256]{2,1,0:T(8,128)(2,1)S(1)}, bf16[1,128,256]{2,1,0:T(8,128)(2,1)S(1)}, u32[]{:S(2)}, u32[]{:S(2)}) collective-permute-start(bf16[1,128,256]{2,1,0:T(8,128)(2,1)S(1)} %bitcast.288), channel_id=1, source_target_pairs={{1,0},{2,1},{3,2},{4,3},{5,4},{6,5},{7,6},{8,7},{9,8},{10,9},{11,1... | collective-permute-start | bytes 196616 | tf_op jit(solution)/shard_map/ppermute | solution.py:10
  34.7 1.9 %collective-permute-start.5 = (bf16[1,128,256]{2,1,0:T(8,128)(2,1)S(1)}, bf16[1,128,256]{2,1,0:T(8,128)(2,1)S(1)}, u32[]{:S(2)}, u32[]{:S(2)}) collective-permute-start(bf16[1,128,256]{2,1,0:T(8,128)(2,1)S(1)} %bitcast.289), channel_id=1, source_target_pairs={{0,1},{1,2},{2,3},{3,4},{4,5},{5,6},{6,7},{7,8},{8,9},{9,10},{10,1... | collective-permute-start | bytes 196616 | tf_op jit(solution)/shard_map/ppermute | solution.py:10
  36.9 6.1 %collective-permute-done.5 = bf16[1,128,256]{2,1,0:T(8,128)(2,1)S(1)} collective-permute-done((bf16[1,128,256]{2,1,0:T(8,128)(2,1)S(1)}, bf16[1,128,256]{2,1,0:T(8,128)(2,1)S(1)}, u32[]{:S(2)}, u32[]{:S(2)}) %collective-permute-start.5) | collective-permute-done | bytes 65568 | tf_op jit(solution)/shard_map/ppermute | solution.py:10
  43.1 2.9 %collective-permute-start.8 = (bf16[1,3,128,256]{3,2,1,0:T(8,128)(2,1)S(1)}, bf16[1,3,128,256]{3,2,1,0:T(8,128)(2,1)S(1)}, u32[]{:S(2)}, u32[]{:S(2)}) collective-permute-start(bf16[1,3,128,256]{3,2,1,0:T(8,128)(2,1)S(1)} %get-tuple-element.36), channel_id=1, source_target_pairs={{64,0},{128,64},{192,128},{256,192},{320,256},{384,320},{448,384},... | collective-permute-start | bytes 589832 | tf_op jit(solution)/shard_map/ppermute | solution.py:10
  48.6 3.9 %collective-permute-done.7 = bf16[1,3,128,256]{3,2,1,0:T(8,128)(2,1)S(1)} collective-permute-done((bf16[1,3,128,256]{3,2,1,0:T(8,128)(2,1)S(1)}, bf16[1,3,128,256]{3,2,1,0:T(8,128)(2,1)S(1)}, u32[]{:S(2)}, u32[]{:S(2)}) %collective-permute-start.7) | collective-permute-done | bytes 196640 | tf_op jit(solution)/shard_map/ppermute | solution.py:10
  57.8 1.7 %convolution_bitcast_fusion.3 = f32[1,320,768]{2,1,0:T(8,128)S(1)} fusion(bf16[1792,256]{1,0:T(8,128)(2,1)} %copy-done.16, f32[320,256]{1,0:T(8,128)S(1)} %fusion.25, f32[320,256]{1,0:T(8,128)S(1)} %get-tuple-element.46, f32[1,320,256]{2,1,0:T(8,128)S(1)} %get-tuple-element.49, f32[320]{0:T(512)S(1)} %broadcast_multiply_fusion.2, ...), kind=kOutput, calls=%fused_computation.6 | convolution fusion | flops 169082880 | bytes 2500608 | tf_op jit(solution)/shard_map/mrd,kd->mrk/dot_general | solution.py:38
  61.9 3.3 %collective-permute-start.9 = (bf16[1,3,128,256]{3,2,1,0:T(8,128)(2,1)S(1)}, bf16[1,3,128,256]{3,2,1,0:T(8,128)(2,1)S(1)}, u32[]{:S(2)}, u32[]{:S(2)}) collective-permute-start(bf16[1,3,128,256]{3,2,1,0:T(8,128)(2,1)S(1)} %get-tuple-element.29), channel_id=1, source_target_pairs={{64,0},{128,64},{192,128},{256,192},{320,256},{384,320},{448,384},... | collective-permute-start | bytes 589832 | tf_op jit(solution)/shard_map/ppermute | solution.py:10
  67.8 3.8 %collective-permute-done.10 = bf16[1,3,128,256]{3,2,1,0:T(8,128)(2,1)S(1)} collective-permute-done((bf16[1,3,128,256]{3,2,1,0:T(8,128)(2,1)S(1)}, bf16[1,3,128,256]{3,2,1,0:T(8,128)(2,1)S(1)}, u32[]{:S(2)}, u32[]{:S(2)}) %collective-permute-start.10) | collective-permute-done | bytes 196640 | tf_op jit(solution)/shard_map/ppermute | solution.py:10
  71.8 1.9 %collective-permute-start.11 = (bf16[1,128,256]{2,1,0:T(8,128)(2,1)S(1)}, bf16[1,128,256]{2,1,0:T(8,128)(2,1)S(1)}, u32[]{:S(2)}, u32[]{:S(2)}) collective-permute-start(bf16[1,128,256]{2,1,0:T(8,128)(2,1)S(1)} %get-tuple-element.33), channel_id=1, source_target_pairs={{1,0},{2,1},{3,2},{4,3},{5,4},{6,5},{7,6},{8,7},{9,8},{10,9},{11,1... | collective-permute-start | bytes 196616 | tf_op jit(solution)/shard_map/ppermute | solution.py:10
  73.7 3.4 %collective-permute-start.12 = (bf16[1,128,256]{2,1,0:T(8,128)(2,1)S(1)}, bf16[1,128,256]{2,1,0:T(8,128)(2,1)S(1)}, u32[]{:S(2)}, u32[]{:S(2)}) collective-permute-start(bf16[1,128,256]{2,1,0:T(8,128)(2,1)S(1)} %get-tuple-element.34), channel_id=1, source_target_pairs={{0,1},{1,2},{2,3},{3,4},{4,5},{5,6},{6,7},{7,8},{8,9},{9,10},{10,1... | collective-permute-start | bytes 196616 | tf_op jit(solution)/shard_map/ppermute | solution.py:10
  77.4 4.6 %collective-permute-done.12 = bf16[1,128,256]{2,1,0:T(8,128)(2,1)S(1)} collective-permute-done((bf16[1,128,256]{2,1,0:T(8,128)(2,1)S(1)}, bf16[1,128,256]{2,1,0:T(8,128)(2,1)S(1)}, u32[]{:S(2)}, u32[]{:S(2)}) %collective-permute-start.12) | collective-permute-done | bytes 65568 | tf_op jit(solution)/shard_map/ppermute | solution.py:10
  84.5 1.7 %convolution_bitcast_fusion.2 = f32[1,320,768]{2,1,0:T(8,128)S(1)} fusion(bf16[1792,256]{1,0:T(8,128)(2,1)} %copy-done.15, f32[320,256]{1,0:T(8,128)S(1)} %copy-done.49, f32[320,256]{1,0:T(8,128)S(1)} %get-tuple-element.42, f32[1,320,256]{2,1,0:T(8,128)S(1)} %get-tuple-element.50, f32[320]{0:T(512)S(1)} %broadcast_multiply_fusion, ...), kind=kOutput, calls=%fused_computation.5 | convolution fusion | flops 169082880 | bytes 2500608 | tf_op jit(solution)/shard_map/mrd,kd->mrk/dot_general | solution.py:38
  88.6 3.4 %collective-permute-start.13 = (bf16[1,3,128,256]{3,2,1,0:T(8,128)(2,1)S(1)}, bf16[1,3,128,256]{3,2,1,0:T(8,128)(2,1)S(1)}, u32[]{:S(2)}, u32[]{:S(2)}) collective-permute-start(bf16[1,3,128,256]{3,2,1,0:T(8,128)(2,1)S(1)} %get-tuple-element.27), channel_id=1, source_target_pairs={{64,0},{128,64},{192,128},{256,192},{320,256},{384,320},{448,384},... | collective-permute-start | bytes 589832 | tf_op jit(solution)/shard_map/ppermute | solution.py:10
  94.6 3.8 %collective-permute-done.14 = bf16[1,3,128,256]{3,2,1,0:T(8,128)(2,1)S(1)} collective-permute-done((bf16[1,3,128,256]{3,2,1,0:T(8,128)(2,1)S(1)}, bf16[1,3,128,256]{3,2,1,0:T(8,128)(2,1)S(1)}, u32[]{:S(2)}, u32[]{:S(2)}) %collective-permute-start.14) | collective-permute-done | bytes 196640 | tf_op jit(solution)/shard_map/ppermute | solution.py:10
  98.5 1.9 %collective-permute-start.15 = (bf16[1,128,256]{2,1,0:T(8,128)(2,1)S(1)}, bf16[1,128,256]{2,1,0:T(8,128)(2,1)S(1)}, u32[]{:S(2)}, u32[]{:S(2)}) collective-permute-start(bf16[1,128,256]{2,1,0:T(8,128)(2,1)S(1)} %get-tuple-element.31), channel_id=1, source_target_pairs={{1,0},{2,1},{3,2},{4,3},{5,4},{6,5},{7,6},{8,7},{9,8},{10,9},{11,1... | collective-permute-start | bytes 196616 | tf_op jit(solution)/shard_map/ppermute | solution.py:10
  100.5 3.4 %collective-permute-start.16 = (bf16[1,128,256]{2,1,0:T(8,128)(2,1)S(1)}, bf16[1,128,256]{2,1,0:T(8,128)(2,1)S(1)}, u32[]{:S(2)}, u32[]{:S(2)}) collective-permute-start(bf16[1,128,256]{2,1,0:T(8,128)(2,1)S(1)} %get-tuple-element.32), channel_id=1, source_target_pairs={{0,1},{1,2},{2,3},{3,4},{4,5},{5,6},{6,7},{7,8},{8,9},{9,10},{10,1... | collective-permute-start | bytes 196616 | tf_op jit(solution)/shard_map/ppermute | solution.py:10
  104.2 4.6 %collective-permute-done.16 = bf16[1,128,256]{2,1,0:T(8,128)(2,1)S(1)} collective-permute-done((bf16[1,128,256]{2,1,0:T(8,128)(2,1)S(1)}, bf16[1,128,256]{2,1,0:T(8,128)(2,1)S(1)}, u32[]{:S(2)}, u32[]{:S(2)}) %collective-permute-start.16) | collective-permute-done | bytes 65568 | tf_op jit(solution)/shard_map/ppermute | solution.py:10
  109.1 10.7 %collective-permute-start.17 = (f32[896,256]{1,0:T(8,128)S(1)}, f32[896,256]{1,0:T(8,128)S(1)}, u32[]{:S(2)}, u32[]{:S(2)}) collective-permute-start(f32[896,256]{1,0:T(8,128)S(1)} %maximum_select_fusion), channel_id=1, source_target_pairs={{0,512},{512,0},{1,513},{513,1},{2,514},{514,2},{3,515},{515,3},{4... | collective-permute-start | bytes 2752520 | tf_op jit(solution)/shard_map/ppermute | solution.py:183
  120.0 1.8 %collective-permute-done.17 = f32[896,256]{1,0:T(8,128)S(1)} collective-permute-done((f32[896,256]{1,0:T(8,128)S(1)}, f32[896,256]{1,0:T(8,128)S(1)}, u32[]{:S(2)}, u32[]{:S(2)}) %collective-permute-start.17) | collective-permute-done | bytes 917536 | tf_op jit(solution)/shard_map/ppermute | solution.py:183
  (204 shorter events, 36.2 us)
Async XLA Ops:
  1.7 10.6 %collective-permute-start.1 = (bf16[1,128,256]{2,1,0:T(8,128)(2,1)S(1)}, bf16[1,128,256]{2,1,0:T(8,128)(2,1)}, u32[]{:S(2)}, u32[]{:S(2)}) collective-permute-start(bf16[1,128,256]{2,1,0:T(8,128)(2,1)S(1)} %fusion.211), channel_id=1, source_target_pairs={{1,0},{2,1},{3,2},{4,3},{5,4},{6,5},{7,6},{8,7},{9,8},{10,9},{11,1... | collective-permute-start | bytes 196616 | tf_op jit(solution)/shard_map/ppermute | solution.py:10
  4.4 8.4 %collective-permute-start = (bf16[1,128,256]{2,1,0:T(8,128)(2,1)S(1)}, bf16[1,128,256]{2,1,0:T(8,128)(2,1)}, u32[]{:S(2)}, u32[]{:S(2)}) collective-permute-start(bf16[1,128,256]{2,1,0:T(8,128)(2,1)S(1)} %fusion.211), channel_id=1, source_target_pairs={{0,1},{1,2},{2,3},{3,4},{4,5},{5,6},{6,7},{7,8},{8,9},{9,10},{10,1... | collective-permute-start | bytes 196616 | tf_op jit(solution)/shard_map/ppermute | solution.py:10
  8.3 15.2 %collective-permute-start.4 = (bf16[1792,256]{1,0:T(8,128)(2,1)S(1)}, bf16[1792,256]{1,0:T(8,128)(2,1)S(1)}, u32[]{:S(2)}, u32[]{:S(2)}) collective-permute-start(bf16[1792,256]{1,0:T(8,128)(2,1)S(1)} %pad_maximum_fusion), channel_id=1, source_target_pairs={{0,512},{512,0},{1,513},{513,1},{2,514},{514,2},{3,515},{515,3},{4... | collective-permute-start | bytes 2752520 | tf_op jit(solution)/shard_map/ppermute | solution.py:151
  11.8 40.7 %copy-start.32 = (s32[320]{0:T(512)}, s32[320]{0:T(512)S(1)}, u32[]{:S(2)}) copy-start(s32[320]{0:T(512)S(1)} %add.160) | copy-start | bytes 3844
  11.9 45.2 %copy-start.2 = (bf16[1,1,1,5,64,256]{5,4,3,2,1,0:T(8,128)(2,1)}, bf16[1,1,1,5,64,256]{5,4,3,2,1,0:T(8,128)(2,1)S(1)}, u32[]{:S(2)}) copy-start(bf16[1,1,1,5,64,256]{5,4,3,2,1,0:T(8,128)(2,1)S(1)} %get-tuple-element.51) | copy-start | bytes 491524
  12.0 44.7 %copy-start.17 = (bf16[1,1,1,128,256]{4,3,2,1,0:T(8,128)(2,1)}, bf16[1,1,1,128,256]{4,3,2,1,0:T(8,128)(2,1)S(1)}, u32[]{:S(2)}) copy-start(bf16[1,1,1,128,256]{4,3,2,1,0:T(8,128)(2,1)S(1)} %get-tuple-element.22) | copy-start | bytes 196612
  13.7 5.5 %collective-permute-start.3 = (bf16[1,3,128,256]{3,2,1,0:T(8,128)(2,1)S(1)}, bf16[1,3,128,256]{3,2,1,0:T(8,128)(2,1)S(1)}, u32[]{:S(2)}, u32[]{:S(2)}) collective-permute-start(bf16[1,3,128,256]{3,2,1,0:T(8,128)(2,1)S(1)} %get-tuple-element.38), channel_id=1, source_target_pairs={{64,0},{128,64},{192,128},{256,192},{320,256},{384,320},{448,384},... | collective-permute-start | bytes 589832 | tf_op jit(solution)/shard_map/ppermute | solution.py:10
  16.6 6.4 %collective-permute-start.2 = (bf16[1,3,128,256]{3,2,1,0:T(8,128)(2,1)S(1)}, bf16[1,3,128,256]{3,2,1,0:T(8,128)(2,1)S(1)}, u32[]{:S(2)}, u32[]{:S(2)}) collective-permute-start(bf16[1,3,128,256]{3,2,1,0:T(8,128)(2,1)S(1)} %get-tuple-element.38), channel_id=1, source_target_pairs={{0,64},{64,128},{128,192},{192,256},{256,320},{320,384},{384,448},... | collective-permute-start | bytes 589832 | tf_op jit(solution)/shard_map/ppermute | solution.py:10
  24.5 32.2 %copy-start.16 = (bf16[1792,256]{1,0:T(8,128)(2,1)}, bf16[1792,256]{1,0:T(8,128)(2,1)S(1)}, u32[]{:S(2)}) copy-start(bf16[1792,256]{1,0:T(8,128)(2,1)S(1)} %get-tuple-element.24) | copy-start | bytes 2752516
  25.4 21.9 %copy-start.30 = (f32[320]{0:T(512)}, f32[320]{0:T(512)S(1)}, u32[]{:S(2)}) copy-start(f32[320]{0:T(512)S(1)} %add_rsqrt_fusion.1) | copy-start | bytes 3844
  26.4 19.6 %copy-start.8 = (f32[128,256]{1,0:T(8,128)}, f32[128,256]{1,0:T(8,128)S(1)}, u32[]{:S(2)}) copy-start(f32[128,256]{1,0:T(8,128)S(1)} %get-tuple-element.44) | copy-start | bytes 393220
  27.6 9.4 %collective-permute-start.6 = (bf16[1,128,256]{2,1,0:T(8,128)(2,1)S(1)}, bf16[1,128,256]{2,1,0:T(8,128)(2,1)S(1)}, u32[]{:S(2)}, u32[]{:S(2)}) collective-permute-start(bf16[1,128,256]{2,1,0:T(8,128)(2,1)S(1)} %bitcast.288), channel_id=1, source_target_pairs={{1,0},{2,1},{3,2},{4,3},{5,4},{6,5},{7,6},{8,7},{9,8},{10,9},{11,1... | collective-permute-start | bytes 196616 | tf_op jit(solution)/shard_map/ppermute | solution.py:10
  34.7 8.3 %collective-permute-start.5 = (bf16[1,128,256]{2,1,0:T(8,128)(2,1)S(1)}, bf16[1,128,256]{2,1,0:T(8,128)(2,1)S(1)}, u32[]{:S(2)}, u32[]{:S(2)}) collective-permute-start(bf16[1,128,256]{2,1,0:T(8,128)(2,1)S(1)} %bitcast.289), channel_id=1, source_target_pairs={{0,1},{1,2},{2,3},{3,4},{4,5},{5,6},{6,7},{7,8},{8,9},{9,10},{10,1... | collective-permute-start | bytes 196616 | tf_op jit(solution)/shard_map/ppermute | solution.py:10
  43.1 5.5 %collective-permute-start.8 = (bf16[1,3,128,256]{3,2,1,0:T(8,128)(2,1)S(1)}, bf16[1,3,128,256]{3,2,1,0:T(8,128)(2,1)S(1)}, u32[]{:S(2)}, u32[]{:S(2)}) collective-permute-start(bf16[1,3,128,256]{3,2,1,0:T(8,128)(2,1)S(1)} %get-tuple-element.36), channel_id=1, source_target_pairs={{64,0},{128,64},{192,128},{256,192},{320,256},{384,320},{448,384},... | collective-permute-start | bytes 589832 | tf_op jit(solution)/shard_map/ppermute | solution.py:10
  46.0 6.4 %collective-permute-start.7 = (bf16[1,3,128,256]{3,2,1,0:T(8,128)(2,1)S(1)}, bf16[1,3,128,256]{3,2,1,0:T(8,128)(2,1)S(1)}, u32[]{:S(2)}, u32[]{:S(2)}) collective-permute-start(bf16[1,3,128,256]{3,2,1,0:T(8,128)(2,1)S(1)} %get-tuple-element.36), channel_id=1, source_target_pairs={{0,64},{64,128},{128,192},{192,256},{256,320},{320,384},{384,448},... | collective-permute-start | bytes 589832 | tf_op jit(solution)/shard_map/ppermute | solution.py:10
  61.9 5.9 %collective-permute-start.9 = (bf16[1,3,128,256]{3,2,1,0:T(8,128)(2,1)S(1)}, bf16[1,3,128,256]{3,2,1,0:T(8,128)(2,1)S(1)}, u32[]{:S(2)}, u32[]{:S(2)}) collective-permute-start(bf16[1,3,128,256]{3,2,1,0:T(8,128)(2,1)S(1)} %get-tuple-element.29), channel_id=1, source_target_pairs={{64,0},{128,64},{192,128},{256,192},{320,256},{384,320},{448,384},... | collective-permute-start | bytes 589832 | tf_op jit(solution)/shard_map/ppermute | solution.py:10
  65.2 6.4 %collective-permute-start.10 = (bf16[1,3,128,256]{3,2,1,0:T(8,128)(2,1)S(1)}, bf16[1,3,128,256]{3,2,1,0:T(8,128)(2,1)S(1)}, u32[]{:S(2)}, u32[]{:S(2)}) collective-permute-start(bf16[1,3,128,256]{3,2,1,0:T(8,128)(2,1)S(1)} %get-tuple-element.30), channel_id=1, source_target_pairs={{0,64},{64,128},{128,192},{192,256},{256,320},{320,384},{384,448},... | collective-permute-start | bytes 589832 | tf_op jit(solution)/shard_map/ppermute | solution.py:10
  71.8 5.7 %collective-permute-start.11 = (bf16[1,128,256]{2,1,0:T(8,128)(2,1)S(1)}, bf16[1,128,256]{2,1,0:T(8,128)(2,1)S(1)}, u32[]{:S(2)}, u32[]{:S(2)}) collective-permute-start(bf16[1,128,256]{2,1,0:T(8,128)(2,1)S(1)} %get-tuple-element.33), channel_id=1, source_target_pairs={{1,0},{2,1},{3,2},{4,3},{5,4},{6,5},{7,6},{8,7},{9,8},{10,9},{11,1... | collective-permute-start | bytes 196616 | tf_op jit(solution)/shard_map/ppermute | solution.py:10
  73.7 8.3 %collective-permute-start.12 = (bf16[1,128,256]{2,1,0:T(8,128)(2,1)S(1)}, bf16[1,128,256]{2,1,0:T(8,128)(2,1)S(1)}, u32[]{:S(2)}, u32[]{:S(2)}) collective-permute-start(bf16[1,128,256]{2,1,0:T(8,128)(2,1)S(1)} %get-tuple-element.34), channel_id=1, source_target_pairs={{0,1},{1,2},{2,3},{3,4},{4,5},{5,6},{6,7},{7,8},{8,9},{9,10},{10,1... | collective-permute-start | bytes 196616 | tf_op jit(solution)/shard_map/ppermute | solution.py:10
  88.6 6.0 %collective-permute-start.13 = (bf16[1,3,128,256]{3,2,1,0:T(8,128)(2,1)S(1)}, bf16[1,3,128,256]{3,2,1,0:T(8,128)(2,1)S(1)}, u32[]{:S(2)}, u32[]{:S(2)}) collective-permute-start(bf16[1,3,128,256]{3,2,1,0:T(8,128)(2,1)S(1)} %get-tuple-element.27), channel_id=1, source_target_pairs={{64,0},{128,64},{192,128},{256,192},{320,256},{384,320},{448,384},... | collective-permute-start | bytes 589832 | tf_op jit(solution)/shard_map/ppermute | solution.py:10
  92.0 6.4 %collective-permute-start.14 = (bf16[1,3,128,256]{3,2,1,0:T(8,128)(2,1)S(1)}, bf16[1,3,128,256]{3,2,1,0:T(8,128)(2,1)S(1)}, u32[]{:S(2)}, u32[]{:S(2)}) collective-permute-start(bf16[1,3,128,256]{3,2,1,0:T(8,128)(2,1)S(1)} %get-tuple-element.28), channel_id=1, source_target_pairs={{0,64},{64,128},{128,192},{192,256},{256,320},{320,384},{384,448},... | collective-permute-start | bytes 589832 | tf_op jit(solution)/shard_map/ppermute | solution.py:10
  98.5 5.7 %collective-permute-start.15 = (bf16[1,128,256]{2,1,0:T(8,128)(2,1)S(1)}, bf16[1,128,256]{2,1,0:T(8,128)(2,1)S(1)}, u32[]{:S(2)}, u32[]{:S(2)}) collective-permute-start(bf16[1,128,256]{2,1,0:T(8,128)(2,1)S(1)} %get-tuple-element.31), channel_id=1, source_target_pairs={{1,0},{2,1},{3,2},{4,3},{5,4},{6,5},{7,6},{8,7},{9,8},{10,9},{11,1... | collective-permute-start | bytes 196616 | tf_op jit(solution)/shard_map/ppermute | solution.py:10
  100.5 8.3 %collective-permute-start.16 = (bf16[1,128,256]{2,1,0:T(8,128)(2,1)S(1)}, bf16[1,128,256]{2,1,0:T(8,128)(2,1)S(1)}, u32[]{:S(2)}, u32[]{:S(2)}) collective-permute-start(bf16[1,128,256]{2,1,0:T(8,128)(2,1)S(1)} %get-tuple-element.32), channel_id=1, source_target_pairs={{0,1},{1,2},{2,3},{3,4},{4,5},{5,6},{6,7},{7,8},{8,9},{9,10},{10,1... | collective-permute-start | bytes 196616 | tf_op jit(solution)/shard_map/ppermute | solution.py:10
  109.1 12.7 %collective-permute-start.17 = (f32[896,256]{1,0:T(8,128)S(1)}, f32[896,256]{1,0:T(8,128)S(1)}, u32[]{:S(2)}, u32[]{:S(2)}) collective-permute-start(f32[896,256]{1,0:T(8,128)S(1)} %maximum_select_fusion), channel_id=1, source_target_pairs={{0,512},{512,0},{1,513},{513,1},{2,514},{514,2},{3,515},{515,3},{4... | collective-permute-start | bytes 2752520 | tf_op jit(solution)/shard_map/ppermute | solution.py:183
  (44 other events, 364.7 us)

commit v9 on v8

--- a/solution.py
+++ b/solution.py
@@ -185,11 +185,12 @@
     latent_recv = swap_recv[:rows].astype(jnp.bfloat16)
     grad_recv = swap_recv[rows:]
 
+    other_slot = 1 - lax.axis_index("phase")
+
     def placed(own_first, own_second, received, shape):
         kept = jnp.where(is_first, own_first, own_second)
-        pair = jnp.where(
-            is_first, jnp.stack([kept, received]), jnp.stack([received, kept])
-        )
+        pair = jnp.stack([kept, kept])
+        pair = lax.dynamic_update_index_in_dim(pair, received, other_slot, axis=0)
         return pair.reshape(shape)
 
     node_shape = (1,) + node_latents.shape

time: 126 us -> 124 us (0.984)
  other arithmetic: 12.6 us -> 9.67 us
    select_n x5 -> x1, other arithmetic: 3.41 us -> 0.36 us  [body(): jnp.where(is_first, other, own)]
    unnamed x100 -> x108, local copies, waits for them, and re-layouts: 3.32 us -> 4.27 us
where the time goes in v9:
time: 124 us; the launch traced here: 123 us
  starting transfers between devices  56.3 us (45%)
  waiting for transfers between devices  36.3 us (29%)
  matrix products  13.3 us (11%)
  other arithmetic  9.67 us (8%)
  local copies, waits for them, and re-layouts  5.45 us (4%)
  between operations  1.91 us (2%)
    ppermute x16, starting transfers between devices, shifted(): return lax.ppermute(array, axis, pairs)  42.5 us
    ppermute x16, waiting for transfers between devices, shifted(): return lax.ppermute(array, axis, pairs)  34.6 us
    ppermute x1, starting transfers between devices, body(): swap_recv = lax.ppermute(swap_send, 'phase', [(0, 1), (1, 0)])  10.7 us
    dot_general x4, matrix products, times_turned(): jnp.einsum('mrd,kd->mrk', left, right, preferred_element_type=jnp.float32)  5.24 us
    dot_general x8, matrix products, onehot_sum(): jnp.einsum(form, left, right, precision=lax.Precision.HIGH, preferred_ele...  4.59 us
    unnamed x108, local copies, waits for them, and re-layouts  4.27 us
    ppermute x1, starting transfers between devices, body(): other = lax.ppermute(own, 'phase', [(0, 1), (1, 0)])  3.14 us
  transfers between devices with their start and end apart: 18, of which 13 were waited for; matrix products, arithmetic and copies ran while one was open for 5% of the time, Pallas kernels for 0%

profile of v9, /device:TPU:625, one launch (start us, length us, event | category | flops | bytes accessed | tf_op | source)
XLA Modules:
  0.0 123.0 jit_solution(6338158165970878633)
XLA Ops:
  1.7 2.7 %collective-permute-start.1 = (bf16[1,128,256]{2,1,0:T(8,128)(2,1)S(1)}, bf16[1,128,256]{2,1,0:T(8,128)(2,1)}, u32[]{:S(2)}, u32[]{:S(2)}) collective-permute-start(bf16[1,128,256]{2,1,0:T(8,128)(2,1)S(1)} %fusion.215), channel_id=1, source_target_pairs={{1,0},{2,1},{3,2},{4,3},{5,4},{6,5},{7,6},{8,7},{9,8},{10,9},{11,1... | collective-permute-start | bytes 196616 | tf_op jit(solution)/shard_map/ppermute | solution.py:10
  4.4 2.6 %collective-permute-start = (bf16[1,128,256]{2,1,0:T(8,128)(2,1)S(1)}, bf16[1,128,256]{2,1,0:T(8,128)(2,1)}, u32[]{:S(2)}, u32[]{:S(2)}) collective-permute-start(bf16[1,128,256]{2,1,0:T(8,128)(2,1)S(1)} %fusion.215), channel_id=1, source_target_pairs={{0,1},{1,2},{2,3},{3,4},{4,5},{5,6},{6,7},{7,8},{8,9},{9,10},{10,1... | collective-permute-start | bytes 196616 | tf_op jit(solution)/shard_map/ppermute | solution.py:10
  8.3 3.1 %collective-permute-start.4 = (bf16[1792,256]{1,0:T(8,128)(2,1)S(1)}, bf16[1792,256]{1,0:T(8,128)(2,1)S(1)}, u32[]{:S(2)}, u32[]{:S(2)}) collective-permute-start(bf16[1792,256]{1,0:T(8,128)(2,1)S(1)} %pad_maximum_fusion), channel_id=1, source_target_pairs={{0,512},{512,0},{1,513},{513,1},{2,514},{514,2},{3,515},{515,3},{4... | collective-permute-start | bytes 2752520 | tf_op jit(solution)/shard_map/ppermute | solution.py:151
  13.7 2.9 %collective-permute-start.3 = (bf16[1,3,128,256]{3,2,1,0:T(8,128)(2,1)S(1)}, bf16[1,3,128,256]{3,2,1,0:T(8,128)(2,1)S(1)}, u32[]{:S(2)}, u32[]{:S(2)}) collective-permute-start(bf16[1,3,128,256]{3,2,1,0:T(8,128)(2,1)S(1)} %get-tuple-element.42), channel_id=1, source_target_pairs={{64,0},{128,64},{192,128},{256,192},{320,256},{384,320},{448,384},... | collective-permute-start | bytes 589832 | tf_op jit(solution)/shard_map/ppermute | solution.py:10
  19.2 3.8 %collective-permute-done.2 = bf16[1,3,128,256]{3,2,1,0:T(8,128)(2,1)S(1)} collective-permute-done((bf16[1,3,128,256]{3,2,1,0:T(8,128)(2,1)S(1)}, bf16[1,3,128,256]{3,2,1,0:T(8,128)(2,1)S(1)}, u32[]{:S(2)}, u32[]{:S(2)}) %collective-permute-start.2) | collective-permute-done | bytes 196640 | tf_op jit(solution)/shard_map/ppermute | solution.py:10
  27.6 7.2 %collective-permute-start.6 = (bf16[1,128,256]{2,1,0:T(8,128)(2,1)S(1)}, bf16[1,128,256]{2,1,0:T(8,128)(2,1)S(1)}, u32[]{:S(2)}, u32[]{:S(2)}) collective-permute-start(bf16[1,128,256]{2,1,0:T(8,128)(2,1)S(1)} %bitcast.312), channel_id=1, source_target_pairs={{1,0},{2,1},{3,2},{4,3},{5,4},{6,5},{7,6},{8,7},{9,8},{10,9},{11,1... | collective-permute-start | bytes 196616 | tf_op jit(solution)/shard_map/ppermute | solution.py:10
  34.7 1.9 %collective-permute-start.5 = (bf16[1,128,256]{2,1,0:T(8,128)(2,1)S(1)}, bf16[1,128,256]{2,1,0:T(8,128)(2,1)S(1)}, u32[]{:S(2)}, u32[]{:S(2)}) collective-permute-start(bf16[1,128,256]{2,1,0:T(8,128)(2,1)S(1)} %bitcast.313), channel_id=1, source_target_pairs={{0,1},{1,2},{2,3},{3,4},{4,5},{5,6},{6,7},{7,8},{8,9},{9,10},{10,1... | collective-permute-start | bytes 196616 | tf_op jit(solution)/shard_map/ppermute | solution.py:10
  36.9 6.1 %collective-permute-done.5 = bf16[1,128,256]{2,1,0:T(8,128)(2,1)S(1)} collective-permute-done((bf16[1,128,256]{2,1,0:T(8,128)(2,1)S(1)}, bf16[1,128,256]{2,1,0:T(8,128)(2,1)S(1)}, u32[]{:S(2)}, u32[]{:S(2)}) %collective-permute-start.5) | collective-permute-done | bytes 65568 | tf_op jit(solution)/shard_map/ppermute | solution.py:10
  43.1 2.9 %collective-permute-start.8 = (bf16[1,3,128,256]{3,2,1,0:T(8,128)(2,1)S(1)}, bf16[1,3,128,256]{3,2,1,0:T(8,128)(2,1)S(1)}, u32[]{:S(2)}, u32[]{:S(2)}) collective-permute-start(bf16[1,3,128,256]{3,2,1,0:T(8,128)(2,1)S(1)} %get-tuple-element.40), channel_id=1, source_target_pairs={{64,0},{128,64},{192,128},{256,192},{320,256},{384,320},{448,384},... | collective-permute-start | bytes 589832 | tf_op jit(solution)/shard_map/ppermute | solution.py:10
  48.6 3.9 %collective-permute-done.7 = bf16[1,3,128,256]{3,2,1,0:T(8,128)(2,1)S(1)} collective-permute-done((bf16[1,3,128,256]{3,2,1,0:T(8,128)(2,1)S(1)}, bf16[1,3,128,256]{3,2,1,0:T(8,128)(2,1)S(1)}, u32[]{:S(2)}, u32[]{:S(2)}) %collective-permute-start.7) | collective-permute-done | bytes 196640 | tf_op jit(solution)/shard_map/ppermute | solution.py:10
  57.8 1.7 %convolution_bitcast_fusion.3 = f32[1,320,768]{2,1,0:T(8,128)S(1)} fusion(bf16[1792,256]{1,0:T(8,128)(2,1)} %copy-done.16, f32[320,256]{1,0:T(8,128)S(1)} %fusion.25, f32[320,256]{1,0:T(8,128)S(1)} %get-tuple-element.50, f32[1,320,256]{2,1,0:T(8,128)S(1)} %get-tuple-element.53, f32[320]{0:T(512)S(1)} %broadcast_multiply_fusion.2, ...), kind=kOutput, calls=%fused_computation.6 | convolution fusion | flops 169082880 | bytes 2500608 | tf_op jit(solution)/shard_map/mrd,kd->mrk/dot_general | solution.py:38
  62.0 3.3 %collective-permute-start.9 = (bf16[1,3,128,256]{3,2,1,0:T(8,128)(2,1)S(1)}, bf16[1,3,128,256]{3,2,1,0:T(8,128)(2,1)S(1)}, u32[]{:S(2)}, u32[]{:S(2)}) collective-permute-start(bf16[1,3,128,256]{3,2,1,0:T(8,128)(2,1)S(1)} %get-tuple-element.33), channel_id=1, source_target_pairs={{64,0},{128,64},{192,128},{256,192},{320,256},{384,320},{448,384},... | collective-permute-start | bytes 589832 | tf_op jit(solution)/shard_map/ppermute | solution.py:10
  67.8 3.8 %collective-permute-done.10 = bf16[1,3,128,256]{3,2,1,0:T(8,128)(2,1)S(1)} collective-permute-done((bf16[1,3,128,256]{3,2,1,0:T(8,128)(2,1)S(1)}, bf16[1,3,128,256]{3,2,1,0:T(8,128)(2,1)S(1)}, u32[]{:S(2)}, u32[]{:S(2)}) %collective-permute-start.10) | collective-permute-done | bytes 196640 | tf_op jit(solution)/shard_map/ppermute | solution.py:10
  71.8 1.9 %collective-permute-start.11 = (bf16[1,128,256]{2,1,0:T(8,128)(2,1)S(1)}, bf16[1,128,256]{2,1,0:T(8,128)(2,1)S(1)}, u32[]{:S(2)}, u32[]{:S(2)}) collective-permute-start(bf16[1,128,256]{2,1,0:T(8,128)(2,1)S(1)} %get-tuple-element.37), channel_id=1, source_target_pairs={{1,0},{2,1},{3,2},{4,3},{5,4},{6,5},{7,6},{8,7},{9,8},{10,9},{11,1... | collective-permute-start | bytes 196616 | tf_op jit(solution)/shard_map/ppermute | solution.py:10
  73.7 3.4 %collective-permute-start.12 = (bf16[1,128,256]{2,1,0:T(8,128)(2,1)S(1)}, bf16[1,128,256]{2,1,0:T(8,128)(2,1)S(1)}, u32[]{:S(2)}, u32[]{:S(2)}) collective-permute-start(bf16[1,128,256]{2,1,0:T(8,128)(2,1)S(1)} %get-tuple-element.38), channel_id=1, source_target_pairs={{0,1},{1,2},{2,3},{3,4},{4,5},{5,6},{6,7},{7,8},{8,9},{9,10},{10,1... | collective-permute-start | bytes 196616 | tf_op jit(solution)/shard_map/ppermute | solution.py:10
  77.4 4.6 %collective-permute-done.12 = bf16[1,128,256]{2,1,0:T(8,128)(2,1)S(1)} collective-permute-done((bf16[1,128,256]{2,1,0:T(8,128)(2,1)S(1)}, bf16[1,128,256]{2,1,0:T(8,128)(2,1)S(1)}, u32[]{:S(2)}, u32[]{:S(2)}) %collective-permute-start.12) | collective-permute-done | bytes 65568 | tf_op jit(solution)/shard_map/ppermute | solution.py:10
  84.5 1.7 %convolution_bitcast_fusion.2 = f32[1,320,768]{2,1,0:T(8,128)S(1)} fusion(bf16[1792,256]{1,0:T(8,128)(2,1)} %copy-done.15, f32[320,256]{1,0:T(8,128)S(1)} %copy-done.53, f32[320,256]{1,0:T(8,128)S(1)} %get-tuple-element.46, f32[1,320,256]{2,1,0:T(8,128)S(1)} %get-tuple-element.54, f32[320]{0:T(512)S(1)} %broadcast_multiply_fusion, ...), kind=kOutput, calls=%fused_computation.5 | convolution fusion | flops 169082880 | bytes 2500608 | tf_op jit(solution)/shard_map/mrd,kd->mrk/dot_general | solution.py:38
  88.6 3.4 %collective-permute-start.13 = (bf16[1,3,128,256]{3,2,1,0:T(8,128)(2,1)S(1)}, bf16[1,3,128,256]{3,2,1,0:T(8,128)(2,1)S(1)}, u32[]{:S(2)}, u32[]{:S(2)}) collective-permute-start(bf16[1,3,128,256]{3,2,1,0:T(8,128)(2,1)S(1)} %get-tuple-element.31), channel_id=1, source_target_pairs={{64,0},{128,64},{192,128},{256,192},{320,256},{384,320},{448,384},... | collective-permute-start | bytes 589832 | tf_op jit(solution)/shard_map/ppermute | solution.py:10
  94.6 3.8 %collective-permute-done.14 = bf16[1,3,128,256]{3,2,1,0:T(8,128)(2,1)S(1)} collective-permute-done((bf16[1,3,128,256]{3,2,1,0:T(8,128)(2,1)S(1)}, bf16[1,3,128,256]{3,2,1,0:T(8,128)(2,1)S(1)}, u32[]{:S(2)}, u32[]{:S(2)}) %collective-permute-start.14) | collective-permute-done | bytes 196640 | tf_op jit(solution)/shard_map/ppermute | solution.py:10
  98.5 1.9 %collective-permute-start.15 = (bf16[1,128,256]{2,1,0:T(8,128)(2,1)S(1)}, bf16[1,128,256]{2,1,0:T(8,128)(2,1)S(1)}, u32[]{:S(2)}, u32[]{:S(2)}) collective-permute-start(bf16[1,128,256]{2,1,0:T(8,128)(2,1)S(1)} %get-tuple-element.35), channel_id=1, source_target_pairs={{1,0},{2,1},{3,2},{4,3},{5,4},{6,5},{7,6},{8,7},{9,8},{10,9},{11,1... | collective-permute-start | bytes 196616 | tf_op jit(solution)/shard_map/ppermute | solution.py:10
  100.5 3.4 %collective-permute-start.16 = (bf16[1,128,256]{2,1,0:T(8,128)(2,1)S(1)}, bf16[1,128,256]{2,1,0:T(8,128)(2,1)S(1)}, u32[]{:S(2)}, u32[]{:S(2)}) collective-permute-start(bf16[1,128,256]{2,1,0:T(8,128)(2,1)S(1)} %get-tuple-element.36), channel_id=1, source_target_pairs={{0,1},{1,2},{2,3},{3,4},{4,5},{5,6},{6,7},{7,8},{8,9},{9,10},{10,1... | collective-permute-start | bytes 196616 | tf_op jit(solution)/shard_map/ppermute | solution.py:10
  104.2 4.6 %collective-permute-done.16 = bf16[1,128,256]{2,1,0:T(8,128)(2,1)S(1)} collective-permute-done((bf16[1,128,256]{2,1,0:T(8,128)(2,1)S(1)}, bf16[1,128,256]{2,1,0:T(8,128)(2,1)S(1)}, u32[]{:S(2)}, u32[]{:S(2)}) %collective-permute-start.16) | collective-permute-done | bytes 65568 | tf_op jit(solution)/shard_map/ppermute | solution.py:10
  109.1 10.7 %collective-permute-start.17 = (f32[896,256]{1,0:T(8,128)S(1)}, f32[896,256]{1,0:T(8,128)S(1)}, u32[]{:S(2)}, u32[]{:S(2)}) collective-permute-start(f32[896,256]{1,0:T(8,128)S(1)} %maximum_select_fusion), channel_id=1, source_target_pairs={{0,512},{512,0},{1,513},{513,1},{2,514},{514,2},{3,515},{515,3},{4... | collective-permute-start | bytes 2752520 | tf_op jit(solution)/shard_map/ppermute | solution.py:183
  120.2 1.6 %collective-permute-done.17 = f32[896,256]{1,0:T(8,128)S(1)} collective-permute-done((f32[896,256]{1,0:T(8,128)S(1)}, f32[896,256]{1,0:T(8,128)S(1)}, u32[]{:S(2)}, u32[]{:S(2)}) %collective-permute-start.17) | collective-permute-done | bytes 917536 | tf_op jit(solution)/shard_map/ppermute | solution.py:183
  (212 shorter events, 34.3 us)
Async XLA Ops:
  1.7 10.6 %collective-permute-start.1 = (bf16[1,128,256]{2,1,0:T(8,128)(2,1)S(1)}, bf16[1,128,256]{2,1,0:T(8,128)(2,1)}, u32[]{:S(2)}, u32[]{:S(2)}) collective-permute-start(bf16[1,128,256]{2,1,0:T(8,128)(2,1)S(1)} %fusion.215), channel_id=1, source_target_pairs={{1,0},{2,1},{3,2},{4,3},{5,4},{6,5},{7,6},{8,7},{9,8},{10,9},{11,1... | collective-permute-start | bytes 196616 | tf_op jit(solution)/shard_map/ppermute | solution.py:10
  4.4 8.4 %collective-permute-start = (bf16[1,128,256]{2,1,0:T(8,128)(2,1)S(1)}, bf16[1,128,256]{2,1,0:T(8,128)(2,1)}, u32[]{:S(2)}, u32[]{:S(2)}) collective-permute-start(bf16[1,128,256]{2,1,0:T(8,128)(2,1)S(1)} %fusion.215), channel_id=1, source_target_pairs={{0,1},{1,2},{2,3},{3,4},{4,5},{5,6},{6,7},{7,8},{8,9},{9,10},{10,1... | collective-permute-start | bytes 196616 | tf_op jit(solution)/shard_map/ppermute | solution.py:10
  8.3 15.2 %collective-permute-start.4 = (bf16[1792,256]{1,0:T(8,128)(2,1)S(1)}, bf16[1792,256]{1,0:T(8,128)(2,1)S(1)}, u32[]{:S(2)}, u32[]{:S(2)}) collective-permute-start(bf16[1792,256]{1,0:T(8,128)(2,1)S(1)} %pad_maximum_fusion), channel_id=1, source_target_pairs={{0,512},{512,0},{1,513},{513,1},{2,514},{514,2},{3,515},{515,3},{4... | collective-permute-start | bytes 2752520 | tf_op jit(solution)/shard_map/ppermute | solution.py:151
  11.8 40.7 %copy-start.36 = (s32[320]{0:T(512)}, s32[320]{0:T(512)S(1)}, u32[]{:S(2)}) copy-start(s32[320]{0:T(512)S(1)} %add.171) | copy-start | bytes 3844
  11.9 45.2 %copy-start.2 = (bf16[1,1,1,5,64,256]{5,4,3,2,1,0:T(8,128)(2,1)}, bf16[1,1,1,5,64,256]{5,4,3,2,1,0:T(8,128)(2,1)S(1)}, u32[]{:S(2)}) copy-start(bf16[1,1,1,5,64,256]{5,4,3,2,1,0:T(8,128)(2,1)S(1)} %get-tuple-element.55) | copy-start | bytes 491524
  12.0 44.7 %copy-start.18 = (bf16[1,1,1,128,256]{4,3,2,1,0:T(8,128)(2,1)}, bf16[1,1,1,128,256]{4,3,2,1,0:T(8,128)(2,1)S(1)}, u32[]{:S(2)}) copy-start(bf16[1,1,1,128,256]{4,3,2,1,0:T(8,128)(2,1)S(1)} %get-tuple-element.26) | copy-start | bytes 196612
  13.7 5.5 %collective-permute-start.3 = (bf16[1,3,128,256]{3,2,1,0:T(8,128)(2,1)S(1)}, bf16[1,3,128,256]{3,2,1,0:T(8,128)(2,1)S(1)}, u32[]{:S(2)}, u32[]{:S(2)}) collective-permute-start(bf16[1,3,128,256]{3,2,1,0:T(8,128)(2,1)S(1)} %get-tuple-element.42), channel_id=1, source_target_pairs={{64,0},{128,64},{192,128},{256,192},{320,256},{384,320},{448,384},... | collective-permute-start | bytes 589832 | tf_op jit(solution)/shard_map/ppermute | solution.py:10
  16.6 6.4 %collective-permute-start.2 = (bf16[1,3,128,256]{3,2,1,0:T(8,128)(2,1)S(1)}, bf16[1,3,128,256]{3,2,1,0:T(8,128)(2,1)S(1)}, u32[]{:S(2)}, u32[]{:S(2)}) collective-permute-start(bf16[1,3,128,256]{3,2,1,0:T(8,128)(2,1)S(1)} %get-tuple-element.42), channel_id=1, source_target_pairs={{0,64},{64,128},{128,192},{192,256},{256,320},{320,384},{384,448},... | collective-permute-start | bytes 589832 | tf_op jit(solution)/shard_map/ppermute | solution.py:10
  24.5 32.2 %copy-start.16 = (bf16[1792,256]{1,0:T(8,128)(2,1)}, bf16[1792,256]{1,0:T(8,128)(2,1)S(1)}, u32[]{:S(2)}) copy-start(bf16[1792,256]{1,0:T(8,128)(2,1)S(1)} %get-tuple-element.27) | copy-start | bytes 2752516
  25.4 21.9 %copy-start.34 = (f32[320]{0:T(512)}, f32[320]{0:T(512)S(1)}, u32[]{:S(2)}) copy-start(f32[320]{0:T(512)S(1)} %add_rsqrt_fusion.1) | copy-start | bytes 3844
  26.4 19.6 %copy-start.8 = (f32[128,256]{1,0:T(8,128)}, f32[128,256]{1,0:T(8,128)S(1)}, u32[]{:S(2)}) copy-start(f32[128,256]{1,0:T(8,128)S(1)} %get-tuple-element.48) | copy-start | bytes 393220
  27.6 9.4 %collective-permute-start.6 = (bf16[1,128,256]{2,1,0:T(8,128)(2,1)S(1)}, bf16[1,128,256]{2,1,0:T(8,128)(2,1)S(1)}, u32[]{:S(2)}, u32[]{:S(2)}) collective-permute-start(bf16[1,128,256]{2,1,0:T(8,128)(2,1)S(1)} %bitcast.312), channel_id=1, source_target_pairs={{1,0},{2,1},{3,2},{4,3},{5,4},{6,5},{7,6},{8,7},{9,8},{10,9},{11,1... | collective-permute-start | bytes 196616 | tf_op jit(solution)/shard_map/ppermute | solution.py:10
  34.7 8.3 %collective-permute-start.5 = (bf16[1,128,256]{2,1,0:T(8,128)(2,1)S(1)}, bf16[1,128,256]{2,1,0:T(8,128)(2,1)S(1)}, u32[]{:S(2)}, u32[]{:S(2)}) collective-permute-start(bf16[1,128,256]{2,1,0:T(8,128)(2,1)S(1)} %bitcast.313), channel_id=1, source_target_pairs={{0,1},{1,2},{2,3},{3,4},{4,5},{5,6},{6,7},{7,8},{8,9},{9,10},{10,1... | collective-permute-start | bytes 196616 | tf_op jit(solution)/shard_map/ppermute | solution.py:10
  43.1 5.5 %collective-permute-start.8 = (bf16[1,3,128,256]{3,2,1,0:T(8,128)(2,1)S(1)}, bf16[1,3,128,256]{3,2,1,0:T(8,128)(2,1)S(1)}, u32[]{:S(2)}, u32[]{:S(2)}) collective-permute-start(bf16[1,3,128,256]{3,2,1,0:T(8,128)(2,1)S(1)} %get-tuple-element.40), channel_id=1, source_target_pairs={{64,0},{128,64},{192,128},{256,192},{320,256},{384,320},{448,384},... | collective-permute-start | bytes 589832 | tf_op jit(solution)/shard_map/ppermute | solution.py:10
  46.0 6.4 %collective-permute-start.7 = (bf16[1,3,128,256]{3,2,1,0:T(8,128)(2,1)S(1)}, bf16[1,3,128,256]{3,2,1,0:T(8,128)(2,1)S(1)}, u32[]{:S(2)}, u32[]{:S(2)}) collective-permute-start(bf16[1,3,128,256]{3,2,1,0:T(8,128)(2,1)S(1)} %get-tuple-element.40), channel_id=1, source_target_pairs={{0,64},{64,128},{128,192},{192,256},{256,320},{320,384},{384,448},... | collective-permute-start | bytes 589832 | tf_op jit(solution)/shard_map/ppermute | solution.py:10
  62.0 5.9 %collective-permute-start.9 = (bf16[1,3,128,256]{3,2,1,0:T(8,128)(2,1)S(1)}, bf16[1,3,128,256]{3,2,1,0:T(8,128)(2,1)S(1)}, u32[]{:S(2)}, u32[]{:S(2)}) collective-permute-start(bf16[1,3,128,256]{3,2,1,0:T(8,128)(2,1)S(1)} %get-tuple-element.33), channel_id=1, source_target_pairs={{64,0},{128,64},{192,128},{256,192},{320,256},{384,320},{448,384},... | collective-permute-start | bytes 589832 | tf_op jit(solution)/shard_map/ppermute | solution.py:10
  65.2 6.4 %collective-permute-start.10 = (bf16[1,3,128,256]{3,2,1,0:T(8,128)(2,1)S(1)}, bf16[1,3,128,256]{3,2,1,0:T(8,128)(2,1)S(1)}, u32[]{:S(2)}, u32[]{:S(2)}) collective-permute-start(bf16[1,3,128,256]{3,2,1,0:T(8,128)(2,1)S(1)} %get-tuple-element.34), channel_id=1, source_target_pairs={{0,64},{64,128},{128,192},{192,256},{256,320},{320,384},{384,448},... | collective-permute-start | bytes 589832 | tf_op jit(solution)/shard_map/ppermute | solution.py:10
  71.8 5.7 %collective-permute-start.11 = (bf16[1,128,256]{2,1,0:T(8,128)(2,1)S(1)}, bf16[1,128,256]{2,1,0:T(8,128)(2,1)S(1)}, u32[]{:S(2)}, u32[]{:S(2)}) collective-permute-start(bf16[1,128,256]{2,1,0:T(8,128)(2,1)S(1)} %get-tuple-element.37), channel_id=1, source_target_pairs={{1,0},{2,1},{3,2},{4,3},{5,4},{6,5},{7,6},{8,7},{9,8},{10,9},{11,1... | collective-permute-start | bytes 196616 | tf_op jit(solution)/shard_map/ppermute | solution.py:10
  73.7 8.3 %collective-permute-start.12 = (bf16[1,128,256]{2,1,0:T(8,128)(2,1)S(1)}, bf16[1,128,256]{2,1,0:T(8,128)(2,1)S(1)}, u32[]{:S(2)}, u32[]{:S(2)}) collective-permute-start(bf16[1,128,256]{2,1,0:T(8,128)(2,1)S(1)} %get-tuple-element.38), channel_id=1, source_target_pairs={{0,1},{1,2},{2,3},{3,4},{4,5},{5,6},{6,7},{7,8},{8,9},{9,10},{10,1... | collective-permute-start | bytes 196616 | tf_op jit(solution)/shard_map/ppermute | solution.py:10
  88.6 6.0 %collective-permute-start.13 = (bf16[1,3,128,256]{3,2,1,0:T(8,128)(2,1)S(1)}, bf16[1,3,128,256]{3,2,1,0:T(8,128)(2,1)S(1)}, u32[]{:S(2)}, u32[]{:S(2)}) collective-permute-start(bf16[1,3,128,256]{3,2,1,0:T(8,128)(2,1)S(1)} %get-tuple-element.31), channel_id=1, source_target_pairs={{64,0},{128,64},{192,128},{256,192},{320,256},{384,320},{448,384},... | collective-permute-start | bytes 589832 | tf_op jit(solution)/shard_map/ppermute | solution.py:10
  92.0 6.4 %collective-permute-start.14 = (bf16[1,3,128,256]{3,2,1,0:T(8,128)(2,1)S(1)}, bf16[1,3,128,256]{3,2,1,0:T(8,128)(2,1)S(1)}, u32[]{:S(2)}, u32[]{:S(2)}) collective-permute-start(bf16[1,3,128,256]{3,2,1,0:T(8,128)(2,1)S(1)} %get-tuple-element.32), channel_id=1, source_target_pairs={{0,64},{64,128},{128,192},{192,256},{256,320},{320,384},{384,448},... | collective-permute-start | bytes 589832 | tf_op jit(solution)/shard_map/ppermute | solution.py:10
  98.5 5.7 %collective-permute-start.15 = (bf16[1,128,256]{2,1,0:T(8,128)(2,1)S(1)}, bf16[1,128,256]{2,1,0:T(8,128)(2,1)S(1)}, u32[]{:S(2)}, u32[]{:S(2)}) collective-permute-start(bf16[1,128,256]{2,1,0:T(8,128)(2,1)S(1)} %get-tuple-element.35), channel_id=1, source_target_pairs={{1,0},{2,1},{3,2},{4,3},{5,4},{6,5},{7,6},{8,7},{9,8},{10,9},{11,1... | collective-permute-start | bytes 196616 | tf_op jit(solution)/shard_map/ppermute | solution.py:10
  100.5 8.3 %collective-permute-start.16 = (bf16[1,128,256]{2,1,0:T(8,128)(2,1)S(1)}, bf16[1,128,256]{2,1,0:T(8,128)(2,1)S(1)}, u32[]{:S(2)}, u32[]{:S(2)}) collective-permute-start(bf16[1,128,256]{2,1,0:T(8,128)(2,1)S(1)} %get-tuple-element.36), channel_id=1, source_target_pairs={{0,1},{1,2},{2,3},{3,4},{4,5},{5,6},{6,7},{7,8},{8,9},{9,10},{10,1... | collective-permute-start | bytes 196616 | tf_op jit(solution)/shard_map/ppermute | solution.py:10
  109.1 12.7 %collective-permute-start.17 = (f32[896,256]{1,0:T(8,128)S(1)}, f32[896,256]{1,0:T(8,128)S(1)}, u32[]{:S(2)}, u32[]{:S(2)}) collective-permute-start(f32[896,256]{1,0:T(8,128)S(1)} %maximum_select_fusion), channel_id=1, source_target_pairs={{0,512},{512,0},{1,513},{513,1},{2,514},{514,2},{3,515},{515,3},{4... | collective-permute-start | bytes 2752520 | tf_op jit(solution)/shard_map/ppermute | solution.py:183
  (48 other events, 368.1 us)

commit v10 on v9

--- a/solution.py
+++ b/solution.py
@@ -155,7 +155,7 @@
         tuple(packed[cuts[i] : cuts[i + 1]] for i in range(4)) for packed in sections
     ]
     def mine(array):
-        return jnp.where(is_first, array[0], array[1])[None]
+        return lax.dynamic_slice_in_dim(array, lax.axis_index("phase"), 1, axis=0)
 
     node_zero = mine(node_latents).reshape(1, block_nodes, width)
     edge_zero = mine(edge_latents).reshape(1, -1, width)

time: 124 us -> 126 us (1.016)
  local copies, waits for them, and re-layouts: 5.45 us -> 7.18 us
    unnamed x108 -> x114, local copies, waits for them, and re-layouts: 4.27 us -> 4.69 us
  transfers between devices with their start and end apart: 18 -> 18, of which waited for: 13 -> 12; matrix products, arithmetic and copies ran while one was open for 5% -> 5% of each run, Pallas kernels for 0% -> 0%
where the time goes in v10:
time: 126 us; the launch traced here: 125 us
  starting transfers between devices  56.8 us (45%)
  waiting for transfers between devices  35.8 us (28%)
  matrix products  14.4 us (11%)
  other arithmetic  8.94 us (7%)
  local copies, waits for them, and re-layouts  7.18 us (6%)
  between operations  1.97 us (2%)
    ppermute x16, starting transfers between devices, shifted(): return lax.ppermute(array, axis, pairs)  43.1 us
    ppermute x16, waiting for transfers between devices, shifted(): return lax.ppermute(array, axis, pairs)  34.1 us
    ppermute x1, starting transfers between devices, body(): swap_recv = lax.ppermute(swap_send, 'phase', [(0, 1), (1, 0)])  10.6 us
    dot_general x8, matrix products, onehot_sum(): jnp.einsum(form, left, right, precision=lax.Precision.HIGH, preferred_ele...  5.23 us
    dot_general x4, matrix products, times_turned(): jnp.einsum('mrd,kd->mrk', left, right, preferred_element_type=jnp.float32)  5.01 us
    unnamed x114, local copies, waits for them, and re-layouts  4.69 us
    ppermute x1, starting transfers between devices, body(): other = lax.ppermute(own, 'phase', [(0, 1), (1, 0)])  3.14 us
  transfers between devices with their start and end apart: 18, of which 12 were waited for; matrix products, arithmetic and copies ran while one was open for 5% of the time, Pallas kernels for 0%

profile of v10, /device:TPU:625, one launch (start us, length us, event | category | flops | bytes accessed | tf_op | source)
XLA Modules:
  0.0 125.1 jit_solution(11574047725224560330)
XLA Ops:
  1.7 2.7 %collective-permute-start.1 = (bf16[1,128,256]{1,2,0:T(8,128)(2,1)S(1)}, bf16[1,128,256]{1,2,0:T(8,128)(2,1)S(1)}, u32[]{:S(2)}, u32[]{:S(2)}) collective-permute-start(bf16[1,128,256]{1,2,0:T(8,128)(2,1)S(1)} %bitcast.325), channel_id=1, source_target_pairs={{1,0},{2,1},{3,2},{4,3},{5,4},{6,5},{7,6},{8,7},{9,8},{10,9},{11,1... | collective-permute-start | bytes 196616 | tf_op jit(solution)/shard_map/ppermute | solution.py:10
  4.4 2.6 %collective-permute-start = (bf16[1,128,256]{1,2,0:T(8,128)(2,1)S(1)}, bf16[1,128,256]{1,2,0:T(8,128)(2,1)S(1)}, u32[]{:S(2)}, u32[]{:S(2)}) collective-permute-start(bf16[1,128,256]{1,2,0:T(8,128)(2,1)S(1)} %bitcast.326), channel_id=1, source_target_pairs={{0,1},{1,2},{2,3},{3,4},{4,5},{5,6},{6,7},{7,8},{8,9},{9,10},{10,1... | collective-permute-start | bytes 196616 | tf_op jit(solution)/shard_map/ppermute | solution.py:10
  8.3 3.1 %collective-permute-start.4 = (bf16[1792,256]{1,0:T(8,128)(2,1)S(1)}, bf16[1792,256]{1,0:T(8,128)(2,1)}, u32[]{:S(2)}, u32[]{:S(2)}) collective-permute-start(bf16[1792,256]{1,0:T(8,128)(2,1)S(1)} %pad_maximum_fusion), channel_id=1, source_target_pairs={{0,512},{512,0},{1,513},{513,1},{2,514},{514,2},{3,515},{515,3},{4... | collective-permute-start | bytes 2752520 | tf_op jit(solution)/shard_map/ppermute | solution.py:151
  13.0 2.9 %collective-permute-start.3 = (bf16[1,3,128,256]{2,3,1,0:T(8,128)(2,1)S(1)}, bf16[1,3,128,256]{2,3,1,0:T(8,128)(2,1)S(1)}, u32[]{:S(2)}, u32[]{:S(2)}) collective-permute-start(bf16[1,3,128,256]{2,3,1,0:T(8,128)(2,1)S(1)} %get-tuple-element.44), channel_id=1, source_target_pairs={{64,0},{128,64},{192,128},{256,192},{320,256},{384,320},{448,384},... | collective-permute-start | bytes 589832 | tf_op jit(solution)/shard_map/ppermute | solution.py:10
  18.5 3.8 %collective-permute-done.2 = bf16[1,3,128,256]{2,3,1,0:T(8,128)(2,1)S(1)} collective-permute-done((bf16[1,3,128,256]{2,3,1,0:T(8,128)(2,1)S(1)}, bf16[1,3,128,256]{2,3,1,0:T(8,128)(2,1)S(1)}, u32[]{:S(2)}, u32[]{:S(2)}) %collective-permute-start.2) | collective-permute-done | bytes 196640 | tf_op jit(solution)/shard_map/ppermute | solution.py:10
  29.1 7.7 %collective-permute-start.6 = (bf16[1,128,256]{2,1,0:T(8,128)(2,1)S(1)}, bf16[1,128,256]{2,1,0:T(8,128)(2,1)S(1)}, u32[]{:S(2)}, u32[]{:S(2)}) collective-permute-start(bf16[1,128,256]{2,1,0:T(8,128)(2,1)S(1)} %bitcast.310), channel_id=1, source_target_pairs={{1,0},{2,1},{3,2},{4,3},{5,4},{6,5},{7,6},{8,7},{9,8},{10,9},{11,1... | collective-permute-start | bytes 196616 | tf_op jit(solution)/shard_map/ppermute | solution.py:10
  36.8 1.9 %collective-permute-start.5 = (bf16[1,128,256]{2,1,0:T(8,128)(2,1)S(1)}, bf16[1,128,256]{2,1,0:T(8,128)(2,1)S(1)}, u32[]{:S(2)}, u32[]{:S(2)}) collective-permute-start(bf16[1,128,256]{2,1,0:T(8,128)(2,1)S(1)} %bitcast.311), channel_id=1, source_target_pairs={{0,1},{1,2},{2,3},{3,4},{4,5},{5,6},{6,7},{7,8},{8,9},{9,10},{10,1... | collective-permute-start | bytes 196616 | tf_op jit(solution)/shard_map/ppermute | solution.py:10
  38.9 6.1 %collective-permute-done.5 = bf16[1,128,256]{2,1,0:T(8,128)(2,1)S(1)} collective-permute-done((bf16[1,128,256]{2,1,0:T(8,128)(2,1)S(1)}, bf16[1,128,256]{2,1,0:T(8,128)(2,1)S(1)}, u32[]{:S(2)}, u32[]{:S(2)}) %collective-permute-start.5) | collective-permute-done | bytes 65568 | tf_op jit(solution)/shard_map/ppermute | solution.py:10
  45.1 2.9 %collective-permute-start.8 = (bf16[1,3,128,256]{3,2,1,0:T(8,128)(2,1)S(1)}, bf16[1,3,128,256]{3,2,1,0:T(8,128)(2,1)S(1)}, u32[]{:S(2)}, u32[]{:S(2)}) collective-permute-start(bf16[1,3,128,256]{3,2,1,0:T(8,128)(2,1)S(1)} %get-tuple-element.42), channel_id=1, source_target_pairs={{64,0},{128,64},{192,128},{256,192},{320,256},{384,320},{448,384},... | collective-permute-start | bytes 589832 | tf_op jit(solution)/shard_map/ppermute | solution.py:10
  50.6 3.8 %collective-permute-done.7 = bf16[1,3,128,256]{3,2,1,0:T(8,128)(2,1)S(1)} collective-permute-done((bf16[1,3,128,256]{3,2,1,0:T(8,128)(2,1)S(1)}, bf16[1,3,128,256]{3,2,1,0:T(8,128)(2,1)S(1)}, u32[]{:S(2)}, u32[]{:S(2)}) %collective-permute-start.7) | collective-permute-done | bytes 196640 | tf_op jit(solution)/shard_map/ppermute | solution.py:10
  59.8 1.6 %convolution_bitcast_fusion.3 = f32[1,320,768]{2,1,0:T(8,128)S(1)} fusion(bf16[1792,256]{1,0:T(8,128)(2,1)S(1)} %get-tuple-element.29, f32[320,256]{1,0:T(8,128)} %copy-done.56, f32[320,256]{1,0:T(8,128)S(1)} %get-tuple-element.52, f32[1,320,256]{2,1,0:T(8,128)S(1)} %get-tuple-element.55, f32[320]{0:T(512)S(1)} %broadcast_multiply_fusion.2, ...), kind=kOutput, calls=%fused_computation.6 | convolution fusion | flops 169082880 | bytes 2500608 | tf_op jit(solution)/shard_map/mrd,kd->mrk/dot_general | solution.py:38
  63.9 3.3 %collective-permute-start.9 = (bf16[1,3,128,256]{3,2,1,0:T(8,128)(2,1)S(1)}, bf16[1,3,128,256]{3,2,1,0:T(8,128)(2,1)S(1)}, u32[]{:S(2)}, u32[]{:S(2)}) collective-permute-start(bf16[1,3,128,256]{3,2,1,0:T(8,128)(2,1)S(1)} %get-tuple-element.35), channel_id=1, source_target_pairs={{64,0},{128,64},{192,128},{256,192},{320,256},{384,320},{448,384},... | collective-permute-start | bytes 589832 | tf_op jit(solution)/shard_map/ppermute | solution.py:10
  69.8 3.8 %collective-permute-done.10 = bf16[1,3,128,256]{3,2,1,0:T(8,128)(2,1)S(1)} collective-permute-done((bf16[1,3,128,256]{3,2,1,0:T(8,128)(2,1)S(1)}, bf16[1,3,128,256]{3,2,1,0:T(8,128)(2,1)S(1)}, u32[]{:S(2)}, u32[]{:S(2)}) %collective-permute-start.10) | collective-permute-done | bytes 196640 | tf_op jit(solution)/shard_map/ppermute | solution.py:10
  73.7 1.9 %collective-permute-start.11 = (bf16[1,128,256]{2,1,0:T(8,128)(2,1)S(1)}, bf16[1,128,256]{2,1,0:T(8,128)(2,1)S(1)}, u32[]{:S(2)}, u32[]{:S(2)}) collective-permute-start(bf16[1,128,256]{2,1,0:T(8,128)(2,1)S(1)} %get-tuple-element.39), channel_id=1, source_target_pairs={{1,0},{2,1},{3,2},{4,3},{5,4},{6,5},{7,6},{8,7},{9,8},{10,9},{11,1... | collective-permute-start | bytes 196616 | tf_op jit(solution)/shard_map/ppermute | solution.py:10
  75.6 3.4 %collective-permute-start.12 = (bf16[1,128,256]{2,1,0:T(8,128)(2,1)S(1)}, bf16[1,128,256]{2,1,0:T(8,128)(2,1)S(1)}, u32[]{:S(2)}, u32[]{:S(2)}) collective-permute-start(bf16[1,128,256]{2,1,0:T(8,128)(2,1)S(1)} %get-tuple-element.40), channel_id=1, source_target_pairs={{0,1},{1,2},{2,3},{3,4},{4,5},{5,6},{6,7},{7,8},{8,9},{9,10},{10,1... | collective-permute-start | bytes 196616 | tf_op jit(solution)/shard_map/ppermute | solution.py:10
  79.4 4.6 %collective-permute-done.12 = bf16[1,128,256]{2,1,0:T(8,128)(2,1)S(1)} collective-permute-done((bf16[1,128,256]{2,1,0:T(8,128)(2,1)S(1)}, bf16[1,128,256]{2,1,0:T(8,128)(2,1)S(1)}, u32[]{:S(2)}, u32[]{:S(2)}) %collective-permute-start.12) | collective-permute-done | bytes 65568 | tf_op jit(solution)/shard_map/ppermute | solution.py:10
  86.7 1.7 %convolution_bitcast_fusion.2 = f32[1,320,768]{2,1,0:T(8,128)S(1)} fusion(bf16[1792,256]{1,0:T(8,128)(2,1)S(1)} %copy-done.2, f32[320,256]{1,0:T(8,128)} %copy-done.55, f32[320,256]{1,0:T(8,128)S(1)} %get-tuple-element.48, f32[1,320,256]{2,1,0:T(8,128)} %get-tuple-element.56, f32[320]{0:T(512)S(1)} %broadcast_multiply_fusion, ...), kind=kOutput, calls=%fused_computation.5 | convolution fusion | flops 169082880 | bytes 2500608 | tf_op jit(solution)/shard_map/mrd,kd->mrk/dot_general | solution.py:38
  90.8 3.4 %collective-permute-start.13 = (bf16[1,3,128,256]{3,2,1,0:T(8,128)(2,1)S(1)}, bf16[1,3,128,256]{3,2,1,0:T(8,128)(2,1)S(1)}, u32[]{:S(2)}, u32[]{:S(2)}) collective-permute-start(bf16[1,3,128,256]{3,2,1,0:T(8,128)(2,1)S(1)} %get-tuple-element.33), channel_id=1, source_target_pairs={{64,0},{128,64},{192,128},{256,192},{320,256},{384,320},{448,384},... | collective-permute-start | bytes 589832 | tf_op jit(solution)/shard_map/ppermute | solution.py:10
  96.8 3.8 %collective-permute-done.14 = bf16[1,3,128,256]{3,2,1,0:T(8,128)(2,1)S(1)} collective-permute-done((bf16[1,3,128,256]{3,2,1,0:T(8,128)(2,1)S(1)}, bf16[1,3,128,256]{3,2,1,0:T(8,128)(2,1)S(1)}, u32[]{:S(2)}, u32[]{:S(2)}) %collective-permute-start.14) | collective-permute-done | bytes 196640 | tf_op jit(solution)/shard_map/ppermute | solution.py:10
  100.7 1.9 %collective-permute-start.15 = (bf16[1,128,256]{2,1,0:T(8,128)(2,1)S(1)}, bf16[1,128,256]{2,1,0:T(8,128)(2,1)S(1)}, u32[]{:S(2)}, u32[]{:S(2)}) collective-permute-start(bf16[1,128,256]{2,1,0:T(8,128)(2,1)S(1)} %get-tuple-element.37), channel_id=1, source_target_pairs={{1,0},{2,1},{3,2},{4,3},{5,4},{6,5},{7,6},{8,7},{9,8},{10,9},{11,1... | collective-permute-start | bytes 196616 | tf_op jit(solution)/shard_map/ppermute | solution.py:10
  102.7 3.4 %collective-permute-start.16 = (bf16[1,128,256]{2,1,0:T(8,128)(2,1)S(1)}, bf16[1,128,256]{2,1,0:T(8,128)(2,1)S(1)}, u32[]{:S(2)}, u32[]{:S(2)}) collective-permute-start(bf16[1,128,256]{2,1,0:T(8,128)(2,1)S(1)} %get-tuple-element.38), channel_id=1, source_target_pairs={{0,1},{1,2},{2,3},{3,4},{4,5},{5,6},{6,7},{7,8},{8,9},{9,10},{10,1... | collective-permute-start | bytes 196616 | tf_op jit(solution)/shard_map/ppermute | solution.py:10
  106.4 4.6 %collective-permute-done.16 = bf16[1,128,256]{2,1,0:T(8,128)(2,1)S(1)} collective-permute-done((bf16[1,128,256]{2,1,0:T(8,128)(2,1)S(1)}, bf16[1,128,256]{2,1,0:T(8,128)(2,1)S(1)}, u32[]{:S(2)}, u32[]{:S(2)}) %collective-permute-start.16) | collective-permute-done | bytes 65568 | tf_op jit(solution)/shard_map/ppermute | solution.py:10
  111.3 10.6 %collective-permute-start.17 = (f32[896,256]{1,0:T(8,128)S(1)}, f32[896,256]{1,0:T(8,128)S(1)}, u32[]{:S(2)}, u32[]{:S(2)}) collective-permute-start(f32[896,256]{1,0:T(8,128)S(1)} %maximum_select_fusion), channel_id=1, source_target_pairs={{0,512},{512,0},{1,513},{513,1},{2,514},{514,2},{3,515},{515,3},{4... | collective-permute-start | bytes 2752520 | tf_op jit(solution)/shard_map/ppermute | solution.py:183
  122.3 1.6 %collective-permute-done.17 = f32[896,256]{1,0:T(8,128)S(1)} collective-permute-done((f32[896,256]{1,0:T(8,128)S(1)}, f32[896,256]{1,0:T(8,128)S(1)}, u32[]{:S(2)}, u32[]{:S(2)}) %collective-permute-start.17) | collective-permute-done | bytes 917536 | tf_op jit(solution)/shard_map/ppermute | solution.py:183
  (219 shorter events, 36.0 us)
Async XLA Ops:
  1.7 11.2 %collective-permute-start.1 = (bf16[1,128,256]{1,2,0:T(8,128)(2,1)S(1)}, bf16[1,128,256]{1,2,0:T(8,128)(2,1)S(1)}, u32[]{:S(2)}, u32[]{:S(2)}) collective-permute-start(bf16[1,128,256]{1,2,0:T(8,128)(2,1)S(1)} %bitcast.325), channel_id=1, source_target_pairs={{1,0},{2,1},{3,2},{4,3},{5,4},{6,5},{7,6},{8,7},{9,8},{10,9},{11,1... | collective-permute-start | bytes 196616 | tf_op jit(solution)/shard_map/ppermute | solution.py:10
  4.4 8.5 %collective-permute-start = (bf16[1,128,256]{1,2,0:T(8,128)(2,1)S(1)}, bf16[1,128,256]{1,2,0:T(8,128)(2,1)S(1)}, u32[]{:S(2)}, u32[]{:S(2)}) collective-permute-start(bf16[1,128,256]{1,2,0:T(8,128)(2,1)S(1)} %bitcast.326), channel_id=1, source_target_pairs={{0,1},{1,2},{2,3},{3,4},{4,5},{5,6},{6,7},{7,8},{8,9},{9,10},{10,1... | collective-permute-start | bytes 196616 | tf_op jit(solution)/shard_map/ppermute | solution.py:10
  8.3 14.8 %collective-permute-start.4 = (bf16[1792,256]{1,0:T(8,128)(2,1)S(1)}, bf16[1792,256]{1,0:T(8,128)(2,1)}, u32[]{:S(2)}, u32[]{:S(2)}) collective-permute-start(bf16[1792,256]{1,0:T(8,128)(2,1)S(1)} %pad_maximum_fusion), channel_id=1, source_target_pairs={{0,512},{512,0},{1,513},{513,1},{2,514},{514,2},{3,515},{515,3},{4... | collective-permute-start | bytes 2752520 | tf_op jit(solution)/shard_map/ppermute | solution.py:151
  11.8 42.6 %copy-start.40 = (s32[320]{0:T(512)}, s32[320]{0:T(512)S(1)}, u32[]{:S(2)}) copy-start(s32[320]{0:T(512)S(1)} %add.178) | copy-start | bytes 3844
  12.0 47.1 %copy-start.5 = (bf16[1,1,1,5,64,256]{5,4,3,2,1,0:T(8,128)(2,1)}, bf16[1,1,1,5,64,256]{5,4,3,2,1,0:T(8,128)(2,1)S(1)}, u32[]{:S(2)}) copy-start(bf16[1,1,1,5,64,256]{5,4,3,2,1,0:T(8,128)(2,1)S(1)} %get-tuple-element.57) | copy-start | bytes 491524
  13.0 5.5 %collective-permute-start.3 = (bf16[1,3,128,256]{2,3,1,0:T(8,128)(2,1)S(1)}, bf16[1,3,128,256]{2,3,1,0:T(8,128)(2,1)S(1)}, u32[]{:S(2)}, u32[]{:S(2)}) collective-permute-start(bf16[1,3,128,256]{2,3,1,0:T(8,128)(2,1)S(1)} %get-tuple-element.44), channel_id=1, source_target_pairs={{64,0},{128,64},{192,128},{256,192},{320,256},{384,320},{448,384},... | collective-permute-start | bytes 589832 | tf_op jit(solution)/shard_map/ppermute | solution.py:10
  15.9 6.4 %collective-permute-start.2 = (bf16[1,3,128,256]{2,3,1,0:T(8,128)(2,1)S(1)}, bf16[1,3,128,256]{2,3,1,0:T(8,128)(2,1)S(1)}, u32[]{:S(2)}, u32[]{:S(2)}) collective-permute-start(bf16[1,3,128,256]{2,3,1,0:T(8,128)(2,1)S(1)} %get-tuple-element.44), channel_id=1, source_target_pairs={{0,64},{64,128},{128,192},{192,256},{256,320},{320,384},{384,448},... | collective-permute-start | bytes 589832 | tf_op jit(solution)/shard_map/ppermute | solution.py:10
  26.8 22.5 %copy-start.38 = (f32[320]{0:T(512)}, f32[320]{0:T(512)S(1)}, u32[]{:S(2)}) copy-start(f32[320]{0:T(512)S(1)} %add_rsqrt_fusion.1) | copy-start | bytes 3844
  27.7 21.7 %copy-start.18 = (bf16[1,1,1,5,64,256]{5,4,3,2,1,0:T(8,128)(2,1)S(1)}, bf16[1,1,1,5,64,256]{5,4,3,2,1,0:T(8,128)(2,1)}, u32[]{:S(2)}) copy-start(bf16[1,1,1,5,64,256]{5,4,3,2,1,0:T(8,128)(2,1)} %copy-done.17) | copy-start | bytes 491524
  27.9 27.6 %copy-start.9 = (f32[128,256]{1,0:T(8,128)}, f32[128,256]{1,0:T(8,128)S(1)}, u32[]{:S(2)}) copy-start(f32[128,256]{1,0:T(8,128)S(1)} %get-tuple-element.50) | copy-start | bytes 393220
  28.0 17.1 %copy-start.45 = (f32[128]{0:T(128)}, f32[128]{0:T(128)S(1)}, u32[]{:S(2)}) copy-start(f32[128]{0:T(128)S(1)} %broadcast_multiply_fusion.11) | copy-start | bytes 1540
  29.1 9.9 %collective-permute-start.6 = (bf16[1,128,256]{2,1,0:T(8,128)(2,1)S(1)}, bf16[1,128,256]{2,1,0:T(8,128)(2,1)S(1)}, u32[]{:S(2)}, u32[]{:S(2)}) collective-permute-start(bf16[1,128,256]{2,1,0:T(8,128)(2,1)S(1)} %bitcast.310), channel_id=1, source_target_pairs={{1,0},{2,1},{3,2},{4,3},{5,4},{6,5},{7,6},{8,7},{9,8},{10,9},{11,1... | collective-permute-start | bytes 196616 | tf_op jit(solution)/shard_map/ppermute | solution.py:10
  36.8 8.3 %collective-permute-start.5 = (bf16[1,128,256]{2,1,0:T(8,128)(2,1)S(1)}, bf16[1,128,256]{2,1,0:T(8,128)(2,1)S(1)}, u32[]{:S(2)}, u32[]{:S(2)}) collective-permute-start(bf16[1,128,256]{2,1,0:T(8,128)(2,1)S(1)} %bitcast.311), channel_id=1, source_target_pairs={{0,1},{1,2},{2,3},{3,4},{4,5},{5,6},{6,7},{7,8},{8,9},{9,10},{10,1... | collective-permute-start | bytes 196616 | tf_op jit(solution)/shard_map/ppermute | solution.py:10
  45.1 5.4 %collective-permute-start.8 = (bf16[1,3,128,256]{3,2,1,0:T(8,128)(2,1)S(1)}, bf16[1,3,128,256]{3,2,1,0:T(8,128)(2,1)S(1)}, u32[]{:S(2)}, u32[]{:S(2)}) collective-permute-start(bf16[1,3,128,256]{3,2,1,0:T(8,128)(2,1)S(1)} %get-tuple-element.42), channel_id=1, source_target_pairs={{64,0},{128,64},{192,128},{256,192},{320,256},{384,320},{448,384},... | collective-permute-start | bytes 589832 | tf_op jit(solution)/shard_map/ppermute | solution.py:10
  48.0 6.4 %collective-permute-start.7 = (bf16[1,3,128,256]{3,2,1,0:T(8,128)(2,1)S(1)}, bf16[1,3,128,256]{3,2,1,0:T(8,128)(2,1)S(1)}, u32[]{:S(2)}, u32[]{:S(2)}) collective-permute-start(bf16[1,3,128,256]{3,2,1,0:T(8,128)(2,1)S(1)} %get-tuple-element.42), channel_id=1, source_target_pairs={{0,64},{64,128},{128,192},{192,256},{256,320},{320,384},{384,448},... | collective-permute-start | bytes 589832 | tf_op jit(solution)/shard_map/ppermute | solution.py:10
  63.9 5.9 %collective-permute-start.9 = (bf16[1,3,128,256]{3,2,1,0:T(8,128)(2,1)S(1)}, bf16[1,3,128,256]{3,2,1,0:T(8,128)(2,1)S(1)}, u32[]{:S(2)}, u32[]{:S(2)}) collective-permute-start(bf16[1,3,128,256]{3,2,1,0:T(8,128)(2,1)S(1)} %get-tuple-element.35), channel_id=1, source_target_pairs={{64,0},{128,64},{192,128},{256,192},{320,256},{384,320},{448,384},... | collective-permute-start | bytes 589832 | tf_op jit(solution)/shard_map/ppermute | solution.py:10
  67.2 6.4 %collective-permute-start.10 = (bf16[1,3,128,256]{3,2,1,0:T(8,128)(2,1)S(1)}, bf16[1,3,128,256]{3,2,1,0:T(8,128)(2,1)S(1)}, u32[]{:S(2)}, u32[]{:S(2)}) collective-permute-start(bf16[1,3,128,256]{3,2,1,0:T(8,128)(2,1)S(1)} %get-tuple-element.36), channel_id=1, source_target_pairs={{0,64},{64,128},{128,192},{192,256},{256,320},{320,384},{384,448},... | collective-permute-start | bytes 589832 | tf_op jit(solution)/shard_map/ppermute | solution.py:10
  73.7 5.7 %collective-permute-start.11 = (bf16[1,128,256]{2,1,0:T(8,128)(2,1)S(1)}, bf16[1,128,256]{2,1,0:T(8,128)(2,1)S(1)}, u32[]{:S(2)}, u32[]{:S(2)}) collective-permute-start(bf16[1,128,256]{2,1,0:T(8,128)(2,1)S(1)} %get-tuple-element.39), channel_id=1, source_target_pairs={{1,0},{2,1},{3,2},{4,3},{5,4},{6,5},{7,6},{8,7},{9,8},{10,9},{11,1... | collective-permute-start | bytes 196616 | tf_op jit(solution)/shard_map/ppermute | solution.py:10
  75.6 8.3 %collective-permute-start.12 = (bf16[1,128,256]{2,1,0:T(8,128)(2,1)S(1)}, bf16[1,128,256]{2,1,0:T(8,128)(2,1)S(1)}, u32[]{:S(2)}, u32[]{:S(2)}) collective-permute-start(bf16[1,128,256]{2,1,0:T(8,128)(2,1)S(1)} %get-tuple-element.40), channel_id=1, source_target_pairs={{0,1},{1,2},{2,3},{3,4},{4,5},{5,6},{6,7},{7,8},{8,9},{9,10},{10,1... | collective-permute-start | bytes 196616 | tf_op jit(solution)/shard_map/ppermute | solution.py:10
  90.8 6.0 %collective-permute-start.13 = (bf16[1,3,128,256]{3,2,1,0:T(8,128)(2,1)S(1)}, bf16[1,3,128,256]{3,2,1,0:T(8,128)(2,1)S(1)}, u32[]{:S(2)}, u32[]{:S(2)}) collective-permute-start(bf16[1,3,128,256]{3,2,1,0:T(8,128)(2,1)S(1)} %get-tuple-element.33), channel_id=1, source_target_pairs={{64,0},{128,64},{192,128},{256,192},{320,256},{384,320},{448,384},... | collective-permute-start | bytes 589832 | tf_op jit(solution)/shard_map/ppermute | solution.py:10
  94.2 6.4 %collective-permute-start.14 = (bf16[1,3,128,256]{3,2,1,0:T(8,128)(2,1)S(1)}, bf16[1,3,128,256]{3,2,1,0:T(8,128)(2,1)S(1)}, u32[]{:S(2)}, u32[]{:S(2)}) collective-permute-start(bf16[1,3,128,256]{3,2,1,0:T(8,128)(2,1)S(1)} %get-tuple-element.34), channel_id=1, source_target_pairs={{0,64},{64,128},{128,192},{192,256},{256,320},{320,384},{384,448},... | collective-permute-start | bytes 589832 | tf_op jit(solution)/shard_map/ppermute | solution.py:10
  100.7 5.7 %collective-permute-start.15 = (bf16[1,128,256]{2,1,0:T(8,128)(2,1)S(1)}, bf16[1,128,256]{2,1,0:T(8,128)(2,1)S(1)}, u32[]{:S(2)}, u32[]{:S(2)}) collective-permute-start(bf16[1,128,256]{2,1,0:T(8,128)(2,1)S(1)} %get-tuple-element.37), channel_id=1, source_target_pairs={{1,0},{2,1},{3,2},{4,3},{5,4},{6,5},{7,6},{8,7},{9,8},{10,9},{11,1... | collective-permute-start | bytes 196616 | tf_op jit(solution)/shard_map/ppermute | solution.py:10
  102.7 8.3 %collective-permute-start.16 = (bf16[1,128,256]{2,1,0:T(8,128)(2,1)S(1)}, bf16[1,128,256]{2,1,0:T(8,128)(2,1)S(1)}, u32[]{:S(2)}, u32[]{:S(2)}) collective-permute-start(bf16[1,128,256]{2,1,0:T(8,128)(2,1)S(1)} %get-tuple-element.38), channel_id=1, source_target_pairs={{0,1},{1,2},{2,3},{3,4},{4,5},{5,6},{6,7},{7,8},{8,9},{9,10},{10,1... | collective-permute-start | bytes 196616 | tf_op jit(solution)/shard_map/ppermute | solution.py:10
  111.3 12.7 %collective-permute-start.17 = (f32[896,256]{1,0:T(8,128)S(1)}, f32[896,256]{1,0:T(8,128)S(1)}, u32[]{:S(2)}, u32[]{:S(2)}) collective-permute-start(f32[896,256]{1,0:T(8,128)S(1)} %maximum_select_fusion), channel_id=1, source_target_pairs={{0,512},{512,0},{1,513},{513,1},{2,514},{514,2},{3,515},{515,3},{4... | collective-permute-start | bytes 2752520 | tf_op jit(solution)/shard_map/ppermute | solution.py:183
  (51 other events, 357.2 us)
